TPU v7x, 512 devices: a whole 4x8x8 slice. The times are simulated.
512 devices in a mesh: row: 4 (over y_hi), col: 16 (over y_lo, x, core), depth: 8 (over z).
Axes of the slice: x: 4, y: 8 (y_hi: 4, y_lo: 2; y = y_hi * 2 + y_lo), z: 8, core: 2. Of those that a mesh axis runs over, the one named last changes fastest.
Arguments:
- block_values: bfloat16 [32, 16, 16, 128, 128], P(('row', 'depth'), 'col'), may hold values from 0.0049743652 to 0.5
- block_cols: int32 [32, 16, 16], P(('row', 'depth'), 'col'), may hold values from 0 to 511, as said below
- live_count: int32 [32, 16], P(('row', 'depth'), 'col'), may hold values from 8 to 16, as said below
- out_pattern: int32 [4, 16, 32, 2], P('row', 'col'), may hold values from 0 to 511, as said below
Outputs:
- squared_log: bfloat16 [4, 16, 32, 128, 128], P('row', 'col', 'depth')
Inputs may be any that keep to these rules, and one draw needn't show every extreme that they name: Block row i's blocks are its first live_count slots; in every draw some block row is full. `block_cols`: the slots of one block row name distinct block columns. Call (k // 16) % 8 the depth part of a block index k and k // 32 its column group. Among the live slots of one block row at most 2 name a column in any one depth part and at most 2 in any one column group; both bounds are reached in every draw. The 32 entries of out_pattern[r, c] are distinct pairs (i, j) with i // 128 == r and j // 32 == c.
All inputs are finite; a program needn't handle non-finite values.
Results may differ from a plain program's by a relative error of at most 0.001.
Values may be sent and summed in bfloat16 or wider, within the bound.
No kernel may reach another device: no remote copies, remote signals or barrier semaphores. Data moves between devices by JAX's collectives and lax.ppermute only.
A program may use at most 128 MiB of HBM per device.

v0:
```python
import math

import jax
import jax.numpy as jnp
from jax import lax
from jax.sharding import PartitionSpec as P


def pack_slots(values, col_ids, targets, is_live, part_count, capacity):
    row_count = col_ids.shape[0]
    block_size = values.shape[-1]
    chosen = (
        targets[:, :, None] == jnp.arange(part_count, dtype=jnp.int32)[None, None, :]
    ) & is_live[:, :, None]
    running = jnp.cumsum(chosen.astype(jnp.int32), axis=1) - 1
    order_in = jnp.sum(jnp.where(chosen, running, 0), axis=2)
    row_ids = jnp.arange(row_count, dtype=jnp.int32)[:, None]
    total = part_count * row_count * capacity
    position = (targets * row_count + row_ids) * capacity + order_in
    position = jnp.where(is_live, position, total).reshape(-1)
    packed = jnp.zeros((total, block_size, block_size), values.dtype)
    packed = packed.at[position].set(values.reshape(-1, block_size, block_size), mode="drop")
    packed_cols = (
        jnp.full((total,), -1, jnp.int32).at[position].set(col_ids.reshape(-1), mode="drop")
    )
    return (
        packed.reshape(part_count, row_count, capacity, block_size, block_size),
        packed_cols.reshape(part_count, row_count, capacity),
    )


def body(block_values, block_cols, live_count, out_pattern):
    depths = lax.axis_size("depth")
    columns = lax.axis_size("col")
    row_groups = lax.axis_size("row")
    row_index = lax.axis_index("row")
    rows_dev = block_values.shape[1]
    slot_count = block_values.shape[2]
    block_size = block_values.shape[3]
    group_rows = columns * rows_dev
    group_count = row_groups * depths
    total_rows = group_count * group_rows
    col_block = total_rows // columns
    pair_size = group_count // columns
    cap_left = slot_count // depths
    cap_right = pair_size * (slot_count // group_count) + min(pair_size, slot_count % group_count)
    values = block_values.reshape(rows_dev, slot_count, block_size, block_size)
    col_ids = block_cols.reshape(rows_dev, slot_count)
    counts = live_count.reshape(rows_dev)
    is_live = jnp.arange(slot_count, dtype=jnp.int32)[None, :] < counts[:, None]
    left_vals, left_cols = pack_slots(
        values, col_ids, col_ids // group_rows % depths, is_live, depths, cap_left
    )
    left_vals, left_cols = (
        lax.all_to_all(left_vals, "depth", split_axis=0, concat_axis=0, tiled=True),
        lax.all_to_all(left_cols, "depth", split_axis=0, concat_axis=0, tiled=True),
    )
    left_vals, left_cols = (
        lax.all_gather(left_vals[None], "col", axis=0, tiled=True),
        lax.all_gather(left_cols[None], "col", axis=0, tiled=True),
    )
    left_shape = left_cols.shape
    source_col = lax.broadcasted_iota(jnp.int32, left_shape, 0)
    source_depth = lax.broadcasted_iota(jnp.int32, left_shape, 1)
    source_row = lax.broadcasted_iota(jnp.int32, left_shape, 2)
    left_rows = (
        (row_index * depths + source_depth) * group_rows + source_col * rows_dev + source_row
    ).reshape(-1)
    left_flat = left_vals.reshape(-1, block_size, block_size)
    left_ids = left_cols.reshape(-1)
    right_vals, right_cols = pack_slots(
        values, col_ids, col_ids // col_block, is_live, columns, cap_right
    )
    right_vals, right_cols = (
        lax.all_to_all(right_vals, "col", split_axis=0, concat_axis=0, tiled=True),
        lax.all_to_all(right_cols, "col", split_axis=0, concat_axis=0, tiled=True),
    )
    right_vals, right_cols = (
        lax.all_gather(right_vals[None], "row", axis=0, tiled=True),
        lax.all_gather(right_cols[None], "row", axis=0, tiled=True),
    )
    right_flat = right_vals.reshape(-1, cap_right, block_size, block_size)
    right_ids = right_cols.reshape(-1, cap_right)
    safe_inner = jnp.maximum(left_ids, 0)
    inner_block = safe_inner // group_rows
    inner_within = safe_inner % group_rows
    right_index = (
        inner_block // depths * columns + inner_within // rows_dev
    ) * rows_dev + inner_within % rows_dev
    pattern_rows = out_pattern[0, 0, :, 0]
    pattern_cols = out_pattern[0, 0, :, 1]
    pattern_len = pattern_rows.shape[0]
    pattern_ids = jnp.arange(pattern_len, dtype=jnp.int32)
    slot_total = left_ids.shape[0]
    step_len = math.gcd(slot_total, 32)
    turns = slot_total // step_len

    def one_turn(partial_value, turn):
        begin = turn * step_len
        left_part = lax.dynamic_slice_in_dim(left_flat, begin, step_len, 0)
        left_part_ids = lax.dynamic_slice_in_dim(left_ids, begin, step_len, 0)
        left_part_rows = lax.dynamic_slice_in_dim(left_rows, begin, step_len, 0)
        picked_index = lax.dynamic_slice_in_dim(right_index, begin, step_len, 0)
        right_part = jnp.take(right_flat, picked_index, axis=0)
        right_part_ids = jnp.take(right_ids, picked_index, axis=0)
        usable = (left_part_ids >= 0)[:, None] & (right_part_ids >= 0)
        matched = (
            (left_part_rows[:, None, None] == pattern_rows[None, None, :])
            & (right_part_ids[:, :, None] == pattern_cols[None, None, :])
            & usable[:, :, None]
        )
        target = jnp.where(
            jnp.any(matched, axis=2),
            jnp.sum(jnp.where(matched, pattern_ids[None, None, :], 0), axis=2),
            pattern_len,
        )
        products = jnp.einsum(
            "lab,lsbc->lsac", left_part, right_part, preferred_element_type=jnp.float32
        )
        summed = jax.ops.segment_sum(
            products.reshape(-1, block_size, block_size),
            target.reshape(-1),
            num_segments=pattern_len + 1,
        )
        return (partial_value + summed[:pattern_len], None)

    partial_sum = jnp.zeros((pattern_len, block_size, block_size), jnp.float32)
    partial_sum, _ = lax.scan(one_turn, partial_sum, jnp.arange(turns, dtype=jnp.int32))
    share = lax.psum_scatter(partial_sum[None, None], "depth", scatter_dimension=2, tiled=True)
    return jnp.log1p(share).astype(jnp.bfloat16)


def solution(mesh):
    in_specs = (
        P(("row", "depth"), "col", None, None, None),
        P(("row", "depth"), "col", None),
        P(("row", "depth"), "col"),
        P("row", "col", None, None),
    )
    out_specs = P("row", "col", "depth", None, None)
    return jax.shard_map(body, mesh=mesh, in_specs=in_specs, out_specs=out_specs, check_vma=False)
```

profile of v0, /device:TPU:6, one launch (start us, length us, event | category | flops | bytes accessed | tf_op | source)
XLA Modules:
  0.0 458.7 jit_solution(4325967407088816377)
XLA Ops:
  11.5 23.5 %all_to_all.20 = bf16[16,1,2,128,128]{4,3,2,1,0:T(8,128)(2,1)} all-to-all(bf16[16,1,2,128,128]{4,3,2,1,0:T(8,128)(2,1)S(1)} %bitcast.75), channel_id=1, replica_groups=mesh['row'=4,'col'=16,'depth'=8] {'col'}, dimensions={0} | all-to-all | bytes 2097152 | tf_op jit(solution)/shard_map/all_to_all | solution.py:75
  36.3 24.9 %all_to_all.21 = bf16[8,1,2,128,128]{4,3,2,1,0:T(8,128)(2,1)} all-to-all(bf16[8,1,2,128,128]{4,3,2,1,0:T(8,128)(2,1)S(1)} %bitcast.76), channel_id=1, replica_groups=mesh['row'=4,'col'=16,'depth'=8] {'depth'}, dimensions={0} | all-to-all | bytes 1048576 | tf_op jit(solution)/shard_map/all_to_all | solution.py:55
  67.6 5.9 %all-to-all-done = s32[8,1,2]{2,1,0:T(1,128)S(1)} async-done(((s32[8,1,2]{2,1,0:T(1,128)}), s32[8,1,2]{2,1,0:T(1,128)S(1)}, u32[]{:S(2)}, u32[]{:S(2)}) %all-to-all-start) | async-done | bytes 96 | tf_op jit(solution)/shard_map/all_to_all | solution.py:56
  78.3 16.7 %all-gather = s32[128,1,2]{2,1,0:T(1,128)S(1)} all-gather(s32[8,1,2]{2,1,0:T(1,128)S(1)} %all-to-all-done), channel_id=2, replica_groups=mesh['row'=4,'col'=16,'depth'=8] {'col'}, dimensions={0}, use_global_device_ids=true | all-gather | bytes 1088 | tf_op jit(solution)/shard_map/all_gather | solution.py:60
  96.5 18.2 %all-gather.1 = s32[64,1,2]{2,1,0:T(1,128)S(1)} all-gather(s32[16,1,2]{2,1,0:T(1,128)S(1)} %all-to-all-done.1), channel_id=3, replica_groups=mesh['row'=4,'col'=16,'depth'=8] {'row'}, dimensions={0}, use_global_device_ids=true | all-gather | bytes 640 | tf_op jit(solution)/shard_map/all_gather | solution.py:80
  114.7 10.0 %all-gather.7.cloned.1.call-done = bf16[64,1,2,128,128]{4,3,2,1,0:T(8,128)(2,1)} async-done(((bf16[16,1,2,128,128]{4,3,2,1,0:T(8,128)(2,1)}), bf16[64,1,2,128,128]{4,3,2,1,0:T(8,128)(2,1)}) %all-gather.7.cloned.1.call-update) | async-done | bytes 4194320 | tf_op jit(solution)/shard_map/all_gather | solution.py:79
  124.8 58.3 %all-gather.9.cloned.1.call-done = bf16[128,1,2,128,128]{4,3,2,1,0:T(8,128)(2,1)} async-done(((bf16[8,1,2,128,128]{4,3,2,1,0:T(8,128)(2,1)}), bf16[128,1,2,128,128]{4,3,2,1,0:T(8,128)(2,1)}) %all-gather.9.cloned.1.call-update) | async-done | bytes 8388624 | tf_op jit(solution)/shard_map/all_gather | solution.py:59
  183.0 220.6 %while.11 = (s32[]{:T(128)}, f32[32,128,128]{2,1,0:T(8,128)}, s32[8]{0:T(128)S(1)}, s32[256]{0:T(256)S(1)}, s32[1,1,32,1]{2,3,1,0:T(1,128)S(1)}, /*index=5*/s32[...) while((s32[]{:T(128)}, f32[32,128,128]{2,1,0:T(8,128)}, ...), condition=%wide.region_12.13_spmd.clone, body=%wide.region_8.12_spmd.clone.sunk | while | flops 271602016 | bytes 40973512 | solution.py:128
  191.5 5.6 %copy.50 = f32[64,128,128]{2,1,0:T(8,128)} copy(f32[64,128,128]{1,2,0:T(8,128)} %bitcast.71) | data formatting | bytes 8388608 | tf_op jit(solution)/shard_map/while/body/eval_jaxpr/reshape | solution.py:121
  198.8 8.8 %scatter_fusion = f32[33,128,128]{2,1,0:T(8,128)S(1)} fusion(f32[33,128,128]{2,1,0:T(8,128)S(1)} %broadcast.733, s32[64]{0:T(128)S(1)} %reshape.896, f32[64,128,128]{2,1,0:T(8,128)} %copy.50), kind=kCustom, calls=%fused_computation.2.clone.clone.1 | custom fusion | flops 1048576 | bytes 12583168 | tf_op jit(solution)/shard_map/while/body/eval_jaxpr/scatter-add | solution.py:120
  225.0 8.8 %scatter_fusion = f32[33,128,128]{2,1,0:T(8,128)S(1)} fusion(f32[33,128,128]{2,1,0:T(8,128)S(1)} %broadcast.733, s32[64]{0:T(128)S(1)} %reshape.896, f32[64,128,128]{2,1,0:T(8,128)} %copy.50), kind=kCustom, calls=%fused_computation.2.clone.clone.1 | custom fusion | flops 1048576 | bytes 12583168 | tf_op jit(solution)/shard_map/while/body/eval_jaxpr/scatter-add | solution.py:120
  245.5 5.6 %copy.50 = f32[64,128,128]{2,1,0:T(8,128)} copy(f32[64,128,128]{1,2,0:T(8,128)} %bitcast.71) | data formatting | bytes 8388608 | tf_op jit(solution)/shard_map/while/body/eval_jaxpr/reshape | solution.py:121
  252.8 8.8 %scatter_fusion = f32[33,128,128]{2,1,0:T(8,128)S(1)} fusion(f32[33,128,128]{2,1,0:T(8,128)S(1)} %broadcast.733, s32[64]{0:T(128)S(1)} %reshape.896, f32[64,128,128]{2,1,0:T(8,128)} %copy.50), kind=kCustom, calls=%fused_computation.2.clone.clone.1 | custom fusion | flops 1048576 | bytes 12583168 | tf_op jit(solution)/shard_map/while/body/eval_jaxpr/scatter-add | solution.py:120
  273.3 5.6 %copy.50 = f32[64,128,128]{2,1,0:T(8,128)} copy(f32[64,128,128]{1,2,0:T(8,128)} %bitcast.71) | data formatting | bytes 8388608 | tf_op jit(solution)/shard_map/while/body/eval_jaxpr/reshape | solution.py:121
  280.5 8.8 %scatter_fusion = f32[33,128,128]{2,1,0:T(8,128)S(1)} fusion(f32[33,128,128]{2,1,0:T(8,128)S(1)} %broadcast.733, s32[64]{0:T(128)S(1)} %reshape.896, f32[64,128,128]{2,1,0:T(8,128)} %copy.50), kind=kCustom, calls=%fused_computation.2.clone.clone.1 | custom fusion | flops 1048576 | bytes 12583168 | tf_op jit(solution)/shard_map/while/body/eval_jaxpr/scatter-add | solution.py:120
  301.0 5.6 %copy.50 = f32[64,128,128]{2,1,0:T(8,128)} copy(f32[64,128,128]{1,2,0:T(8,128)} %bitcast.71) | data formatting | bytes 8388608 | tf_op jit(solution)/shard_map/while/body/eval_jaxpr/reshape | solution.py:121
  308.3 8.8 %scatter_fusion = f32[33,128,128]{2,1,0:T(8,128)S(1)} fusion(f32[33,128,128]{2,1,0:T(8,128)S(1)} %broadcast.733, s32[64]{0:T(128)S(1)} %reshape.896, f32[64,128,128]{2,1,0:T(8,128)} %copy.50), kind=kCustom, calls=%fused_computation.2.clone.clone.1 | custom fusion | flops 1048576 | bytes 12583168 | tf_op jit(solution)/shard_map/while/body/eval_jaxpr/scatter-add | solution.py:120
  328.8 5.6 %copy.50 = f32[64,128,128]{2,1,0:T(8,128)} copy(f32[64,128,128]{1,2,0:T(8,128)} %bitcast.71) | data formatting | bytes 8388608 | tf_op jit(solution)/shard_map/while/body/eval_jaxpr/reshape | solution.py:121
  336.1 8.8 %scatter_fusion = f32[33,128,128]{2,1,0:T(8,128)S(1)} fusion(f32[33,128,128]{2,1,0:T(8,128)S(1)} %broadcast.733, s32[64]{0:T(128)S(1)} %reshape.896, f32[64,128,128]{2,1,0:T(8,128)} %copy.50), kind=kCustom, calls=%fused_computation.2.clone.clone.1 | custom fusion | flops 1048576 | bytes 12583168 | tf_op jit(solution)/shard_map/while/body/eval_jaxpr/scatter-add | solution.py:120
  356.6 5.6 %copy.50 = f32[64,128,128]{2,1,0:T(8,128)} copy(f32[64,128,128]{1,2,0:T(8,128)} %bitcast.71) | data formatting | bytes 8388608 | tf_op jit(solution)/shard_map/while/body/eval_jaxpr/reshape | solution.py:121
  363.8 8.8 %scatter_fusion = f32[33,128,128]{2,1,0:T(8,128)S(1)} fusion(f32[33,128,128]{2,1,0:T(8,128)S(1)} %broadcast.733, s32[64]{0:T(128)S(1)} %reshape.896, f32[64,128,128]{2,1,0:T(8,128)} %copy.50), kind=kCustom, calls=%fused_computation.2.clone.clone.1 | custom fusion | flops 1048576 | bytes 12583168 | tf_op jit(solution)/shard_map/while/body/eval_jaxpr/scatter-add | solution.py:120
  384.3 5.6 %copy.50 = f32[64,128,128]{2,1,0:T(8,128)} copy(f32[64,128,128]{1,2,0:T(8,128)} %bitcast.71) | data formatting | bytes 8388608 | tf_op jit(solution)/shard_map/while/body/eval_jaxpr/reshape | solution.py:121
  391.6 8.8 %scatter_fusion = f32[33,128,128]{2,1,0:T(8,128)S(1)} fusion(f32[33,128,128]{2,1,0:T(8,128)S(1)} %broadcast.733, s32[64]{0:T(128)S(1)} %reshape.896, f32[64,128,128]{2,1,0:T(8,128)} %copy.50), kind=kCustom, calls=%fused_computation.2.clone.clone.1 | custom fusion | flops 1048576 | bytes 12583168 | tf_op jit(solution)/shard_map/while/body/eval_jaxpr/scatter-add | solution.py:120
  403.6 46.9 %reduce-scatter.2.cloned.1.call-done = f32[1,1,4,128,128]{4,3,2,1,0:T(8,128)} async-done(((f32[1,1,32,128,128]{4,3,2,1,0:T(8,128)}), f32[1,1,4,128,128]{4,3,2,1,0:T(8,128)}) %reduce-scatter.2.cloned.1.call-update) | async-done | bytes 262160 | tf_op jit(solution)/shard_map/reduce_scatter | solution.py:129
  (178 shorter events, 125.5 us)
Async XLA Ops:
  6.5 118.2 %all-gather.7.cloned.1.call-start = ((), (), s32[]{:S(2)}) async-start(), calls=%async_computation.6 | async-start | bytes 5242880 | tf_op jit(solution)/shard_map/all_gather | solution.py:79
  11.5 23.7 %copy-start = (bf16[1,1,16,128,128]{4,3,2,1,0:T(8,128)(2,1)S(1)}, bf16[1,1,16,128,128]{4,3,2,1,0:T(8,128)(2,1)}, u32[]{:S(2)}) copy-start(bf16[1,1,16,128,128]{4,3,2,1,0:T(8,128)(2,1)} %param.6) | copy-start | bytes 1572868
  35.0 31.7 %copy-start.1 = (s32[1,1,32,2]{2,3,1,0:T(2,128)S(1)}, s32[1,1,32,2]{2,3,1,0:T(2,128)}, u32[]{:S(2)}) copy-start(s32[1,1,32,2]{2,3,1,0:T(2,128)} %param.9) | copy-start | bytes 772
  35.0 148.1 %all-gather.9.cloned.1.call-start = ((), (), s32[]{:S(2)}) async-start(), calls=%async_computation.7 | async-start | bytes 8912896 | tf_op jit(solution)/shard_map/all_gather | solution.py:59
  62.6 10.9 %all-to-all-start = ((s32[8,1,2]{2,1,0:T(1,128)}), s32[8,1,2]{2,1,0:T(1,128)S(1)}, u32[]{:S(2)}, u32[]{:S(2)}) async-start(s32[8,1,2]{2,1,0:T(1,128)} %bitcast.5), calls=%async_computation | async-start | bytes 8192 | tf_op jit(solution)/shard_map/all_to_all | solution.py:56
  73.5 23.0 %all-to-all-start.1 = ((s32[16,1,2]{2,1,0:T(1,128)}), s32[16,1,2]{2,1,0:T(1,128)S(1)}, u32[]{:S(2)}, u32[]{:S(2)}) async-start(s32[16,1,2]{2,1,0:T(1,128)} %bitcast.8), calls=%async_computation.1 | async-start | bytes 16384 | tf_op jit(solution)/shard_map/all_to_all | solution.py:76
  78.3 372.2 %reduce-scatter.2.cloned.1.call-start = ((), (), s32[]{:S(2)}) async-start(), calls=%async_computation.5 | async-start | bytes 2359296 | tf_op jit(solution)/shard_map/reduce_scatter | solution.py:129
Sparse Core Ops, SparseCore 0:
  35.1 89.6 all-gather.6
  126.9 56.0 all-gather.8
  403.8 46.7 reduce-scatter.1
where the time goes:
time: 462 us; the launch traced here: 459 us
  waiting for transfers between devices  121 us (26%)
  other arithmetic  103 us (22%)
  local copies, waits for them, and re-layouts  91.1 us (20%)
  blocking collectives  83.3 us (18%)
  matrix products  32.2 us (7%)
  between operations  13.9 us (3%)
  starting transfers between devices  8.13 us (2%)
  loops' own time  5.61 us (1%)
    scatter-add x8, other arithmetic, one_turn(): jax.ops.segment_sum(products.reshape(-1, block_size, block_size), target....  70.2 us
    all_gather x1, waiting for transfers between devices, body(): lax.all_gather(left_vals[None], 'col', axis=0, tiled=True)  58.3 us
    reduce_scatter x1, waiting for transfers between devices, body(): lax.psum_scatter(partial_sum[None, None], 'depth', scatter_dimension=2, t...  46.9 us
    reshape x8, local copies, waits for them, and re-layouts, one_turn(): products.reshape(-1, block_size, block_size)  44.8 us
    dot_general x8, matrix products, one_turn(): jnp.einsum('lab,lsbc->lsac', left_part, right_part, preferred_element_typ...  32.2 us
    gather x8, local copies, waits for them, and re-layouts, one_turn(): right_part = jnp.take(right_flat, picked_index, axis=0)  25.1 us
    all_to_all x1, blocking collectives, body(): lax.all_to_all(left_vals, 'depth', split_axis=0, concat_axis=0, tiled=True)  24.9 us
    add x8, other arithmetic, one_turn(): return (partial_value + summed[:pattern_len], None)  24.2 us
  transfers between devices with their start and end apart: 5, of which 4 were waited for; matrix products, arithmetic and copies ran while one was open for 1% of the time, Pallas kernels for 0%

commit v1 on v0

--- a/solution.py
+++ b/solution.py
@@ -81,51 +81,35 @@
     )
     right_flat = right_vals.reshape(-1, cap_right, block_size, block_size)
     right_ids = right_cols.reshape(-1, cap_right)
-    safe_inner = jnp.maximum(left_ids, 0)
-    inner_block = safe_inner // group_rows
-    inner_within = safe_inner % group_rows
-    right_index = (
-        inner_block // depths * columns + inner_within // rows_dev
-    ) * rows_dev + inner_within % rows_dev
     pattern_rows = out_pattern[0, 0, :, 0]
     pattern_cols = out_pattern[0, 0, :, 1]
+    local_row = pattern_rows - row_index * (depths * group_rows)
+    left_pos = (local_row % group_rows) * depths + local_row // group_rows
+    left_sel = left_pos[:, None] * cap_left + jnp.arange(cap_left, dtype=jnp.int32)[None, :]
+    left_flat = left_vals.reshape(-1, block_size, block_size)
+    left_ids = left_cols.reshape(-1)
+    left_pick = jnp.take(left_flat, left_sel.reshape(-1), axis=0)
+    inner = jnp.take(left_ids, left_sel, axis=0)
+    safe_inner = jnp.maximum(inner, 0)
+    right_row = safe_inner // (depths * group_rows) * columns + safe_inner % group_rows
+    right_ids = right_cols.reshape(-1, cap_right)
+    right_flat = right_vals.reshape(-1, block_size, block_size)
+    right_here = jnp.take(right_ids, right_row, axis=0)
+    matched = (right_here == pattern_cols[:, None, None]) & (inner >= 0)[:, :, None]
+    slot = jnp.sum(
+        jnp.where(matched, jnp.arange(cap_right, dtype=jnp.int32)[None, None, :], 0), axis=2
+    )
+    found = jnp.any(matched, axis=2)
+    right_pick = jnp.take(right_flat, (right_row * cap_right + slot).reshape(-1), axis=0)
+    right_pick = jnp.where(
+        found.reshape(-1)[:, None, None], right_pick, jnp.zeros_like(right_pick)
+    )
     pattern_len = pattern_rows.shape[0]
-    pattern_ids = jnp.arange(pattern_len, dtype=jnp.int32)
-    slot_total = left_ids.shape[0]
-    step_len = math.gcd(slot_total, 32)
-    turns = slot_total // step_len
-
-    def one_turn(partial_value, turn):
-        begin = turn * step_len
-        left_part = lax.dynamic_slice_in_dim(left_flat, begin, step_len, 0)
-        left_part_ids = lax.dynamic_slice_in_dim(left_ids, begin, step_len, 0)
-        left_part_rows = lax.dynamic_slice_in_dim(left_rows, begin, step_len, 0)
-        picked_index = lax.dynamic_slice_in_dim(right_index, begin, step_len, 0)
-        right_part = jnp.take(right_flat, picked_index, axis=0)
-        right_part_ids = jnp.take(right_ids, picked_index, axis=0)
-        usable = (left_part_ids >= 0)[:, None] & (right_part_ids >= 0)
-        matched = (
-            (left_part_rows[:, None, None] == pattern_rows[None, None, :])
-            & (right_part_ids[:, :, None] == pattern_cols[None, None, :])
-            & usable[:, :, None]
-        )
-        target = jnp.where(
-            jnp.any(matched, axis=2),
-            jnp.sum(jnp.where(matched, pattern_ids[None, None, :], 0), axis=2),
-            pattern_len,
-        )
-        products = jnp.einsum(
-            "lab,lsbc->lsac", left_part, right_part, preferred_element_type=jnp.float32
-        )
-        summed = jax.ops.segment_sum(
-            products.reshape(-1, block_size, block_size),
-            target.reshape(-1),
-            num_segments=pattern_len + 1,
-        )
-        return (partial_value + summed[:pattern_len], None)
-
-    partial_sum = jnp.zeros((pattern_len, block_size, block_size), jnp.float32)
-    partial_sum, _ = lax.scan(one_turn, partial_sum, jnp.arange(turns, dtype=jnp.int32))
+    left_pick = left_pick.reshape(pattern_len, cap_left, block_size, block_size)
+    right_pick = right_pick.reshape(pattern_len, cap_left, block_size, block_size)
+    partial_sum = jnp.einsum(
+        "pqab,pqbc->pac", left_pick, right_pick, preferred_element_type=jnp.float32
+    )
     share = lax.psum_scatter(partial_sum[None, None], "depth", scatter_dimension=2, tiled=True)
     return jnp.log1p(share).astype(jnp.bfloat16)
 

time: 462 us -> 248 us (0.54)
  other arithmetic: 103 us -> 4.79 us
  local copies, waits for them, and re-layouts: 91.1 us -> 19 us
  matrix products: 32.2 us -> 3.74 us
  waiting for transfers between devices: 121 us -> 114 us
  loops' own time: 5.61 us -> 0 us
    scatter-add x8 -> x0, other arithmetic: 70.2 us -> none  [one_turn(): jax.ops.segment_sum(products.reshape(-1, block_size, block_size), target....]
    reshape x8 -> x0, local copies, waits for them, and re-layouts: 44.8 us -> none  [one_turn(): products.reshape(-1, block_size, block_size)]
    dot_general x8 -> x1, matrix products: 32.2 us -> 3.74 us  [body(): jnp.einsum('pqab,pqbc->pac', left_pick, right_pick, preferred_element_typ...]
    add x10 -> x0, other arithmetic: 24.3 us -> none  [the longest x8 24.2 us: one_turn(): return (partial_value + summed[:pattern_len], None)]
    gather x24 -> x8, local copies, waits for them, and re-layouts: 30.3 us -> 10.7 us  [the longest x1 5.59 us: body(): left_pick = jnp.take(left_flat, left_sel.reshape(-1), axis=0)]
    another operation x1 -> x0, loops' own time: 5.61 us -> none  [body(): lax.scan(one_turn, partial_sum, jnp.arange(turns, dtype=jnp.int32))]
    dynamic_slice x16 -> x0, local copies, waits for them, and re-layouts: 5.28 us -> none  [the longest x8 4.66 us: body(): lax.scan(one_turn, partial_sum, jnp.arange(turns, dtype=jnp.int32))]
  transfers between devices with their start and end apart: 5 -> 5, of which waited for: 4 -> 4; matrix products, arithmetic and copies ran while one was open for 1% -> 5% of each run, Pallas kernels for 0% -> 0%
where the time goes in v1:
time: 248 us; the launch traced here: 247 us
  waiting for transfers between devices  114 us (46%)
  blocking collectives  83.8 us (34%)
  local copies, waits for them, and re-layouts  19 us (8%)
  between operations  14 us (6%)
  starting transfers between devices  8.13 us (3%)
  other arithmetic  4.79 us (2%)
  matrix products  3.74 us (2%)
    all_gather x1, waiting for transfers between devices, body(): lax.all_gather(left_vals[None], 'col', axis=0, tiled=True)  54.9 us
    reduce_scatter x1, waiting for transfers between devices, body(): lax.psum_scatter(partial_sum[None, None], 'depth', scatter_dimension=2, t...  47 us
    all_to_all x1, blocking collectives, body(): lax.all_to_all(left_vals, 'depth', split_axis=0, concat_axis=0, tiled=True)  24.9 us
    all_to_all x1, blocking collectives, body(): lax.all_to_all(right_vals, 'col', split_axis=0, concat_axis=0, tiled=True)  23.5 us
    all_gather x1, blocking collectives, body(): lax.all_gather(right_cols[None], 'row', axis=0, tiled=True)  18.8 us
    all_gather x1, blocking collectives, body(): lax.all_gather(left_cols[None], 'col', axis=0, tiled=True)  16.7 us
    all_gather x1, waiting for transfers between devices, body(): lax.all_gather(right_vals[None], 'row', axis=0, tiled=True)  6.4 us
    gather x1, local copies, waits for them, and re-layouts, body(): left_pick = jnp.take(left_flat, left_sel.reshape(-1), axis=0)  5.59 us
  transfers between devices with their start and end apart: 5, of which 4 were waited for; matrix products, arithmetic and copies ran while one was open for 5% of the time, Pallas kernels for 0%

profile of v1, /device:TPU:6, one launch (start us, length us, event | category | flops | bytes accessed | tf_op | source)
XLA Modules:
  0.0 247.4 jit_solution(14366866786504797072)
XLA Ops:
  7.2 0.7 and_select_fusion.7
  8.5 0.7 fusion.30
  9.4 2.1 scatter_fusion.1
  11.5 23.5 %all_to_all.20 = bf16[16,1,2,128,128]{4,3,2,1,0:T(8,128)(2,1)} all-to-all(bf16[16,1,2,128,128]{4,3,2,1,0:T(8,128)(2,1)S(1)} %bitcast.90), channel_id=1, replica_groups=mesh['row'=4,'col'=16,'depth'=8] {'col'}, dimensions={0} | all-to-all | bytes 2097152 | tf_op jit(solution)/shard_map/all_to_all | solution.py:75
  35.2 1.2 scatter_fusion
  36.3 24.9 %all_to_all.21 = bf16[8,1,2,128,128]{4,3,2,1,0:T(8,128)(2,1)} all-to-all(bf16[8,1,2,128,128]{4,3,2,1,0:T(8,128)(2,1)S(1)} %bitcast.91), channel_id=1, replica_groups=mesh['row'=4,'col'=16,'depth'=8] {'depth'}, dimensions={0} | all-to-all | bytes 1048576 | tf_op jit(solution)/shard_map/all_to_all | solution.py:55
  61.2 0.8 scatter_custom_fusion.1
  62.0 0.7 reshape.1067
  62.6 3.3 %all-to-all-start.1 = ((s32[8,1,2]{2,1,0:T(1,128)}), s32[8,1,2]{2,1,0:T(1,128)S(1)}, u32[]{:S(2)}, u32[]{:S(2)}) async-start(s32[8,1,2]{2,1,0:T(1,128)} %bitcast.11), calls=%async_computation.1 | async-start | bytes 8192 | tf_op jit(solution)/shard_map/all_to_all | solution.py:56
  65.9 0.8 scatter_custom_fusion.2
  66.7 0.7 reshape.1069
  68.0 5.5 %all-to-all-done.1 = s32[8,1,2]{2,1,0:T(1,128)S(1)} async-done(((s32[8,1,2]{2,1,0:T(1,128)}), s32[8,1,2]{2,1,0:T(1,128)S(1)}, u32[]{:S(2)}, u32[]{:S(2)}) %all-to-all-start.1) | async-done | bytes 96 | tf_op jit(solution)/shard_map/all_to_all | solution.py:56
  73.5 4.8 %all-to-all-start.2 = ((s32[16,1,2]{2,1,0:T(1,128)}), s32[16,1,2]{2,1,0:T(1,128)S(1)}, u32[]{:S(2)}, u32[]{:S(2)}) async-start(s32[16,1,2]{2,1,0:T(1,128)} %bitcast.14), calls=%async_computation.2 | async-start | bytes 16384 | tf_op jit(solution)/shard_map/all_to_all | solution.py:76
  78.3 16.7 %all-gather.1 = s32[128,1,2]{2,1,0:T(1,128)S(1)} all-gather(s32[8,1,2]{2,1,0:T(1,128)S(1)} %all-to-all-done.1), channel_id=3, replica_groups=mesh['row'=4,'col'=16,'depth'=8] {'col'}, dimensions={0}, use_global_device_ids=true | all-gather | bytes 1088 | tf_op jit(solution)/shard_map/all_gather | solution.py:60
  95.6 0.8 reduce.5
  96.5 0.8 gather_fusion.1
  98.1 18.8 %all-gather.2 = s32[64,1,2]{2,1,0:T(1,128)S(1)} all-gather(s32[16,1,2]{2,1,0:T(1,128)S(1)} %all-to-all-done.2), channel_id=4, replica_groups=mesh['row'=4,'col'=16,'depth'=8] {'row'}, dimensions={0}, use_global_device_ids=true | all-gather | bytes 640 | tf_op jit(solution)/shard_map/all_gather | solution.py:80
  118.4 6.4 %all-gather.9.cloned.1.call-done = bf16[64,1,2,128,128]{4,3,2,1,0:T(8,128)(2,1)} async-done(((bf16[16,1,2,128,128]{4,3,2,1,0:T(8,128)(2,1)}), bf16[64,1,2,128,128]{4,3,2,1,0:T(8,128)(2,1)}) %all-gather.9.cloned.1.call-update) | async-done | bytes 4194320 | tf_op jit(solution)/shard_map/all_gather | solution.py:79
  124.8 3.1 %gather_fusion.3 = bf16[64,128,128]{2,1,0:T(8,128)(2,1)S(1)} fusion(bf16[128,128,128]{2,1,0:T(8,128)(2,1)} %bitcast.97, s32[1024]{0:T(1024)S(1)} %pad_clamp_fusion), kind=kCustom, calls=%fused_computation.3 | custom fusion | bytes 4194560 | tf_op jit(solution)/shard_map/jit(_take)/gather | solution.py:103
  127.9 54.9 %all-gather.7.cloned.1.call-done = bf16[128,1,2,128,128]{4,3,2,1,0:T(8,128)(2,1)} async-done(((bf16[8,1,2,128,128]{4,3,2,1,0:T(8,128)(2,1)}), bf16[128,1,2,128,128]{4,3,2,1,0:T(8,128)(2,1)}) %all-gather.7.cloned.1.call-update) | async-done | bytes 8388624 | tf_op jit(solution)/shard_map/all_gather | solution.py:59
  182.8 5.6 %gather_fusion = bf16[64,128,128]{2,1,0:T(8,128)(2,1)} fusion(bf16[256,128,128]{2,1,0:T(8,128)(2,1)} %bitcast.98, s32[1024]{0:T(1024)S(1)} %pad_clamp_fusion.3), kind=kCustom, calls=%fused_computation | custom fusion | bytes 4194560 | tf_op jit(solution)/shard_map/jit(_take)/gather | solution.py:91
  188.4 3.7 %fusion.7 = f32[1,1,32,128,128]{4,3,2,1,0:T(8,128)} fusion(bf16[32,2,128,128]{3,2,1,0:T(8,128)(2,1)S(1)} %bitcast.93, pred[32,2]{1,0:T(8,128)(4,1)S(1)} %copy.44, pred[32,2]{1,0:T(8,128)(4,1)S(1)} %get-tuple-element.5, bf16[32,2,128,128]{3,2,1,0:T(8,128)(2,1)} %bitcast.94, pred[32,2]{1,0:T(8,128)(4,1)S(1)} %copy.33), kind=kOutput, calls=%fused_computation.15 | convolution fusion | flops 271581184 | bytes 6291648 | tf_op jit(solution)/shard_map/pqab,pqbc->pac/dot_general | solution.py:110
  192.2 47.0 %reduce-scatter.2.cloned.1.call-done = f32[1,1,4,128,128]{4,3,2,1,0:T(8,128)} async-done(((f32[1,1,32,128,128]{4,3,2,1,0:T(8,128)}), f32[1,1,4,128,128]{4,3,2,1,0:T(8,128)}) %reduce-scatter.2.cloned.1.call-update) | async-done | bytes 262160 | tf_op jit(solution)/shard_map/reduce_scatter | solution.py:113
  239.2 1.7 log-plus-one_convert_fusion
  (54 shorter events, 4.5 us)
Async XLA Ops:
  6.5 118.2 %all-gather.9.cloned.1.call-start = ((), (), s32[]{:S(2)}) async-start(), calls=%async_computation.7 | async-start | bytes 5242880 | tf_op jit(solution)/shard_map/all_gather | solution.py:79
  11.5 23.7 %copy-start = (bf16[1,1,16,128,128]{4,3,2,1,0:T(8,128)(2,1)S(1)}, bf16[1,1,16,128,128]{4,3,2,1,0:T(8,128)(2,1)}, u32[]{:S(2)}) copy-start(bf16[1,1,16,128,128]{4,3,2,1,0:T(8,128)(2,1)} %param.4) | copy-start | bytes 1572868
  35.0 32.4 %copy-start.1 = (s32[1,1,32,2]{2,3,1,0:T(2,128)S(1)}, s32[1,1,32,2]{2,3,1,0:T(2,128)}, u32[]{:S(2)}) copy-start(s32[1,1,32,2]{2,3,1,0:T(2,128)} %param.7) | copy-start | bytes 772
  35.0 147.8 %all-gather.7.cloned.1.call-start = ((), (), s32[]{:S(2)}) async-start(), calls=%async_computation.6 | async-start | bytes 8912896 | tf_op jit(solution)/shard_map/all_gather | solution.py:59
  62.6 10.9 %all-to-all-start.1 = ((s32[8,1,2]{2,1,0:T(1,128)}), s32[8,1,2]{2,1,0:T(1,128)S(1)}, u32[]{:S(2)}, u32[]{:S(2)}) async-start(s32[8,1,2]{2,1,0:T(1,128)} %bitcast.11), calls=%async_computation.1 | async-start | bytes 8192 | tf_op jit(solution)/shard_map/all_to_all | solution.py:56
  73.5 24.6 %all-to-all-start.2 = ((s32[16,1,2]{2,1,0:T(1,128)}), s32[16,1,2]{2,1,0:T(1,128)S(1)}, u32[]{:S(2)}, u32[]{:S(2)}) async-start(s32[16,1,2]{2,1,0:T(1,128)} %bitcast.14), calls=%async_computation.2 | async-start | bytes 16384 | tf_op jit(solution)/shard_map/all_to_all | solution.py:76
  78.3 160.9 %reduce-scatter.2.cloned.1.call-start = ((), (), s32[]{:S(2)}) async-start(), calls=%async_computation.5 | async-start | bytes 2359296 | tf_op jit(solution)/shard_map/reduce_scatter | solution.py:113
Sparse Core Ops, SparseCore 0:
  35.1 89.6 all-gather.8
  126.9 55.8 all-gather.6
  192.3 46.8 reduce-scatter.1

commit v2 on v1

v2 whole, which is shorter than its diff:
```python
import jax
import jax.numpy as jnp
from jax import lax
from jax.sharding import PartitionSpec as P


def pack_slots(values, col_ids, targets, is_live, part_count, capacity):
    row_count = col_ids.shape[0]
    block_size = values.shape[-1]
    chosen = (
        targets[:, :, None] == jnp.arange(part_count, dtype=jnp.int32)[None, None, :]
    ) & is_live[:, :, None]
    running = jnp.cumsum(chosen.astype(jnp.int32), axis=1) - 1
    order_in = jnp.sum(jnp.where(chosen, running, 0), axis=2)
    row_ids = jnp.arange(row_count, dtype=jnp.int32)[:, None]
    total = part_count * row_count * capacity
    position = (targets * row_count + row_ids) * capacity + order_in
    position = jnp.where(is_live, position, total).reshape(-1)
    packed = jnp.zeros((total, block_size, block_size), values.dtype)
    packed = packed.at[position].set(values.reshape(-1, block_size, block_size), mode="drop")
    return packed.reshape(part_count, row_count, capacity, block_size, block_size)


def body(block_values, block_cols, live_count, out_pattern):
    depths = lax.axis_size("depth")
    columns = lax.axis_size("col")
    row_groups = lax.axis_size("row")
    row_index = lax.axis_index("row")
    depth_index = lax.axis_index("depth")
    col_index = lax.axis_index("col")
    slot_count = block_values.shape[2]
    block_size = block_values.shape[3]
    group_rows = columns
    plane_rows = depths * group_rows
    col_block = row_groups * plane_rows // columns
    cap_left = slot_count // depths
    cap_right = 2
    values = block_values.reshape(1, slot_count, block_size, block_size)
    col_ids = block_cols.reshape(1, slot_count)
    counts = live_count.reshape(1)
    slots = jnp.arange(slot_count, dtype=jnp.int32)
    is_live = slots[None, :] < counts[:, None]

    meta = jnp.concatenate([col_ids, counts[:, None]], axis=1).astype(jnp.float32)
    meta = lax.all_gather(meta, ("row", "depth", "col"), axis=0, tiled=True).astype(jnp.int32)
    all_cols = meta[:, :slot_count]
    all_live = slots[None, :] < meta[:, slot_count:]

    left_vals = pack_slots(
        values, col_ids, col_ids // group_rows % depths, is_live, depths, cap_left
    )
    left_vals = lax.all_to_all(left_vals, "depth", split_axis=0, concat_axis=0, tiled=True)
    left_vals = lax.all_gather(left_vals[None], "col", axis=0, tiled=True)
    right_vals = pack_slots(
        values, col_ids, col_ids // col_block, is_live, columns, cap_right
    )
    right_vals = lax.all_to_all(right_vals, "col", split_axis=0, concat_axis=0, tiled=True)
    right_parts = [right_vals]
    for shift in range(1, row_groups):
        right_parts.append(
            lax.ppermute(
                right_vals,
                "row",
                perm=[(src, (src + shift) % row_groups) for src in range(row_groups)],
            )
        )
    right_flat = jnp.stack(right_parts).reshape(-1, block_size, block_size)

    pattern_rows = out_pattern[0, 0, :, 0]
    pattern_cols = out_pattern[0, 0, :, 1]
    pattern_len = pattern_rows.shape[0]
    local_row = pattern_rows - row_index * plane_rows
    left_pos = (local_row % group_rows) * depths + local_row // group_rows
    left_sel = left_pos[:, None] * cap_left + jnp.arange(cap_left, dtype=jnp.int32)[None, :]

    row_cols = jnp.take(all_cols, pattern_rows, axis=0)
    row_live = jnp.take(all_live, pattern_rows, axis=0)
    chosen = row_live & (row_cols // group_rows % depths == depth_index)
    rank = jnp.cumsum(chosen.astype(jnp.int32), axis=1) - 1
    picks = jnp.arange(cap_left, dtype=jnp.int32)
    hit = chosen[:, None, :] & (rank[:, None, :] == picks[None, :, None])
    has_inner = jnp.any(hit, axis=2)
    inner = jnp.sum(jnp.where(hit, row_cols[:, None, :], 0), axis=2)

    inner_cols = jnp.take(all_cols, inner, axis=0)
    inner_live = jnp.take(all_live, inner, axis=0)
    in_group = inner_live & (inner_cols // col_block == col_index)
    before = jnp.cumsum(in_group.astype(jnp.int32), axis=2) - 1
    match = in_group & (inner_cols == pattern_cols[:, None, None])
    found = jnp.any(match, axis=2) & has_inner
    slot = jnp.sum(jnp.where(match, before, 0), axis=2)
    shift_of = (row_index - inner // plane_rows) % row_groups
    right_row = shift_of * columns + inner % group_rows

    left_flat = left_vals.reshape(-1, block_size, block_size)
    left_pick = jnp.take(left_flat, left_sel.reshape(-1), axis=0)
    right_pick = jnp.take(right_flat, (right_row * cap_right + slot).reshape(-1), axis=0)
    right_pick = jnp.where(
        found.reshape(-1)[:, None, None], right_pick, jnp.zeros_like(right_pick)
    )
    left_pick = left_pick.reshape(pattern_len, cap_left, block_size, block_size)
    right_pick = right_pick.reshape(pattern_len, cap_left, block_size, block_size)
    partial_sum = jnp.einsum(
        "pqab,pqbc->pac", left_pick, right_pick, preferred_element_type=jnp.float32
    )
    share = lax.psum_scatter(partial_sum[None, None], "depth", scatter_dimension=2, tiled=True)
    return jnp.log1p(share).astype(jnp.bfloat16)


def solution(mesh):
    in_specs = (
        P(("row", "depth"), "col", None, None, None),
        P(("row", "depth"), "col", None),
        P(("row", "depth"), "col"),
        P("row", "col", None, None),
    )
    out_specs = P("row", "col", "depth", None, None)
    return jax.shard_map(body, mesh=mesh, in_specs=in_specs, out_specs=out_specs, check_vma=False)
```

time: 248 us -> 871 us (3.51)
  blocking collectives: 83.8 us -> 705 us
  waiting for transfers between devices: 114 us -> 99.4 us
  starting transfers between devices: 8.13 us -> 20.3 us
    all_gather x2 -> x1, blocking collectives: 35.5 us -> 677 us  [body(): lax.all_gather(meta, ('row', 'depth', 'col'), axis=0, tiled=True)]
    all_gather x2 -> x1, waiting for transfers between devices: 61.3 us -> 0.02 us  [body(): left_vals = lax.all_gather(left_vals[None], 'col', axis=0, tiled=True)]
    ppermute x0 -> x3, waiting for transfers between devices: none -> 51.7 us  [body(): lax.ppermute(right_vals, 'row', perm=[(src, (src + shift) % row_groups) f...]
    all_to_all x1 -> x0, blocking collectives: 23.5 us -> none  [body(): lax.all_to_all(right_vals, 'col', split_axis=0, concat_axis=0, tiled=True)]
    ppermute x0 -> x3, starting transfers between devices: none -> 14.5 us  [body(): lax.ppermute(right_vals, 'row', perm=[(src, (src + shift) % row_groups) f...]
  transfers between devices with their start and end apart: 5 -> 6, of which waited for: 4 -> 3; matrix products, arithmetic and copies ran while one was open for 5% -> 2% of each run, Pallas kernels for 0% -> 0%
where the time goes in v2:
time: 871 us; the launch traced here: 870 us
  blocking collectives  705 us (81%)
  waiting for transfers between devices  99.4 us (11%)
  starting transfers between devices  20.3 us (2%)
  local copies, waits for them, and re-layouts  18.6 us (2%)
  between operations  14.3 us (2%)
    all_gather x1, blocking collectives, body(): lax.all_gather(meta, ('row', 'depth', 'col'), axis=0, tiled=True)  677 us
    ppermute x3, waiting for transfers between devices, body(): lax.ppermute(right_vals, 'row', perm=[(src, (src + shift) % row_groups) f...  51.7 us
    reduce_scatter x1, waiting for transfers between devices, body(): lax.psum_scatter(partial_sum[None, None], 'depth', scatter_dimension=2, t...  47.6 us
    all_to_all x1, blocking collectives, body(): lax.all_to_all(left_vals, 'depth', split_axis=0, concat_axis=0, tiled=True)  27.7 us
  transfers between devices with their start and end apart: 6, of which 3 were waited for; matrix products, arithmetic and copies ran while one was open for 2% of the time, Pallas kernels for 0%

profile of v2, /device:TPU:6, one launch (start us, length us, event | category | flops | bytes accessed | tf_op | source)
XLA Modules:
  0.0 870.0 jit_solution(6802126021564995380)
XLA Ops:
  7.2 0.7 and_select_fusion.8
  8.5 0.7 fusion.41
  9.3 2.1 scatter_fusion
  11.4 27.7 %all_to_all.10 = bf16[8,1,2,128,128]{4,3,2,1,0:T(8,128)(2,1)} all-to-all(bf16[8,1,2,128,128]{4,3,2,1,0:T(8,128)(2,1)S(1)} %bitcast.99), channel_id=1, replica_groups=mesh['row'=4,'col'=16,'depth'=8] {'depth'}, dimensions={0} | all-to-all | bytes 1048576 | tf_op jit(solution)/shard_map/all_to_all | solution.py:52
  39.1 1.3 broadcast_in_dim.133
  40.4 2.7 scatter_fusion.1
  43.1 5.8 all-to-all-start.1
  49.0 677.3 %all-gather.1 = f32[512,1,17]{2,1,0:T(1,128)S(1)} all-gather(f32[1,1,17]{2,1,0:T(1,128)S(1)} %fusion.46), channel_id=1, replica_groups=mesh['row'=4,'col'=16,'depth'=8] {'row','depth','col'}, dimensions={0}, use_global_device_ids=true | all-gather | bytes 34884 | tf_op jit(solution)/shard_map/all_gather | solution.py:45
  726.3 0.6 gather_fusion.2
  727.3 0.6 gather_fusion.1
  728.6 0.6 gather_fusion.4
  729.2 0.6 gather_fusion.3
  730.1 6.6 collective-permute-start.1
  736.7 1.9 collective-permute-start
  738.6 6.0 collective-permute-start.2
  745.4 0.4 reduce_window_sum.46
  746.3 32.6 %collective-permute-done.1 = bf16[16,1,2,128,128]{4,3,2,0,1:T(8,128)(2,1)S(1)} collective-permute-done((bf16[16,1,2,128,128]{4,3,2,0,1:T(8,128)(2,1)S(1)}, bf16[16,1,2,128,128]{4,3,2,0,1:T(8,128)(2,1)S(1)}, u32[]{:S(2)}, u32[]{:S(2)}) %collective-permute-start.1) | collective-permute-done | bytes 1048608 | tf_op jit(solution)/shard_map/ppermute | solution.py:61
  778.9 19.1 %collective-permute-done = bf16[16,1,2,128,128]{4,3,2,0,1:T(8,128)(2,1)S(1)} collective-permute-done((bf16[16,1,2,128,128]{4,3,2,0,1:T(8,128)(2,1)S(1)}, bf16[16,1,2,128,128]{4,3,2,0,1:T(8,128)(2,1)S(1)}, u32[]{:S(2)}, u32[]{:S(2)}) %collective-permute-start) | collective-permute-done | bytes 1048608 | tf_op jit(solution)/shard_map/ppermute | solution.py:61
  798.0 3.3 pad_maximum_fusion
  801.3 3.1 gather_fusion.5
  804.5 5.6 gather_fusion
  810.0 3.7 fusion.7
  813.8 47.6 %reduce-scatter.2.cloned.1.call-done = f32[1,1,4,128,128]{4,3,2,1,0:T(8,128)} async-done(((f32[1,1,32,128,128]{4,3,2,1,0:T(8,128)}), f32[1,1,4,128,128]{4,3,2,1,0:T(8,128)}) %reduce-scatter.2.cloned.1.call-update) | async-done | bytes 262160 | tf_op jit(solution)/shard_map/reduce_scatter | solution.py:106
  861.4 1.7 log-plus-one_convert_fusion
  (61 shorter events, 3.5 us)
Async XLA Ops:
  6.5 797.9 %all-gather.4.cloned.1.call-start = ((), (), s32[]{:S(2)}) async-start(), calls=%async_computation.4 | async-start | bytes 8912896 | tf_op jit(solution)/shard_map/all_gather | solution.py:53
  9.3 31.1 %copy-start = (bf16[1,1,16,128,128]{4,3,2,1,0:T(8,128)(2,1)S(1)}, bf16[1,1,16,128,128]{4,3,2,1,0:T(8,128)(2,1)}, u32[]{:S(2)}) copy-start(bf16[1,1,16,128,128]{4,3,2,1,0:T(8,128)(2,1)} %param.4) | copy-start | bytes 1572868
  40.4 8.5 copy-start.1
  40.4 685.9 %copy-start.2 = (s32[1,1,32,2]{2,3,1,0:T(2,128)S(1)}, s32[1,1,32,2]{2,3,1,0:T(2,128)}, u32[]{:S(2)}) copy-start(s32[1,1,32,2]{2,3,1,0:T(2,128)} %param.7) | copy-start | bytes 772
  43.1 687.0 %all-to-all-start.1 = ((bf16[16,1,2,128,128]{4,3,2,1,0:T(8,128)(2,1)}), bf16[16,1,2,128,128]{4,3,2,1,0:T(8,128)(2,1)S(1)}, u32[]{:S(2)}, u32[]{:S(2)}) async-start(bf16[16,1,2,128,128]{4,3,2,1,0:T(8,128)(2,1)} %bitcast.22), calls=%async_computation.1 | async-start | bytes 2097152 | tf_op jit(solution)/shard_map/all_to_all | solution.py:57
  48.8 812.6 %reduce-scatter.2.cloned.1.call-start = ((), (), s32[]{:S(2)}) async-start(), calls=%async_computation.3 | async-start | bytes 2359296 | tf_op jit(solution)/shard_map/reduce_scatter | solution.py:106
  730.1 48.8 %collective-permute-start.1 = (bf16[16,1,2,128,128]{4,3,2,0,1:T(8,128)(2,1)S(1)}, bf16[16,1,2,128,128]{4,3,2,0,1:T(8,128)(2,1)S(1)}, u32[]{:S(2)}, u32[]{:S(2)}) collective-permute-start(bf16[16,1,2,128,128]{4,3,2,0,1:T(8,128)(2,1)S(1)} %bitcast.100), channel_id=1, source_target_pairs={{0,256},{128,384},{256,0},{384,128},{1,257},{129,385},{257,1},{385... | collective-permute-start | bytes 3145736 | tf_op jit(solution)/shard_map/ppermute | solution.py:61
  736.7 61.3 %collective-permute-start = (bf16[16,1,2,128,128]{4,3,2,0,1:T(8,128)(2,1)S(1)}, bf16[16,1,2,128,128]{4,3,2,0,1:T(8,128)(2,1)S(1)}, u32[]{:S(2)}, u32[]{:S(2)}) collective-permute-start(bf16[16,1,2,128,128]{4,3,2,0,1:T(8,128)(2,1)S(1)} %bitcast.101), channel_id=1, source_target_pairs={{0,128},{128,256},{256,384},{384,0},{1,129},{129,257},{257,385},{3... | collective-permute-start | bytes 3145736 | tf_op jit(solution)/shard_map/ppermute | solution.py:61
  738.6 59.4 %collective-permute-start.2 = (bf16[16,1,2,128,128]{4,3,2,1,0:T(8,128)(2,1)S(1)}, bf16[16,1,2,128,128]{4,3,2,1,0:T(8,128)(2,1)}, u32[]{:S(2)}, u32[]{:S(2)}) collective-permute-start(bf16[16,1,2,128,128]{4,3,2,1,0:T(8,128)(2,1)S(1)} %all-to-all-done.1), channel_id=1, source_target_pairs={{0,384},{128,0},{256,128},{384,256},{1,385},{129,1},{257,129},{385... | collective-permute-start | bytes 3145736 | tf_op jit(solution)/shard_map/ppermute | solution.py:61
Sparse Core Ops, SparseCore 0:
  39.2 64.5 all-gather.3
  813.9 47.4 reduce-scatter.1

commit v3 on v1

--- a/solution.py
+++ b/solution.py
@@ -75,12 +75,16 @@
         lax.all_to_all(right_vals, "col", split_axis=0, concat_axis=0, tiled=True),
         lax.all_to_all(right_cols, "col", split_axis=0, concat_axis=0, tiled=True),
     )
-    right_vals, right_cols = (
-        lax.all_gather(right_vals[None], "row", axis=0, tiled=True),
-        lax.all_gather(right_cols[None], "row", axis=0, tiled=True),
+    row_perms = [
+        [(src, (src + shift) % row_groups) for src in range(row_groups)]
+        for shift in range(1, row_groups)
+    ]
+    right_vals = jnp.stack(
+        [right_vals] + [lax.ppermute(right_vals, "row", perm=perm) for perm in row_perms]
     )
-    right_flat = right_vals.reshape(-1, cap_right, block_size, block_size)
-    right_ids = right_cols.reshape(-1, cap_right)
+    right_cols = jnp.stack(
+        [right_cols] + [lax.ppermute(right_cols, "row", perm=perm) for perm in row_perms]
+    )
     pattern_rows = out_pattern[0, 0, :, 0]
     pattern_cols = out_pattern[0, 0, :, 1]
     local_row = pattern_rows - row_index * (depths * group_rows)
@@ -91,7 +95,7 @@
     left_pick = jnp.take(left_flat, left_sel.reshape(-1), axis=0)
     inner = jnp.take(left_ids, left_sel, axis=0)
     safe_inner = jnp.maximum(inner, 0)
-    right_row = safe_inner // (depths * group_rows) * columns + safe_inner % group_rows
+    right_row = (row_index - safe_inner // (depths * group_rows)) % row_groups * columns + safe_inner % group_rows
     right_ids = right_cols.reshape(-1, cap_right)
     right_flat = right_vals.reshape(-1, block_size, block_size)
     right_here = jnp.take(right_ids, right_row, axis=0)

time: 248 us -> 284 us (1.15)
  starting transfers between devices: 8.13 us -> 41.4 us
  blocking collectives: 83.8 us -> 63.1 us
  waiting for transfers between devices: 114 us -> 130 us
  other arithmetic: 4.79 us -> 8.12 us
  local copies, waits for them, and re-layouts: 19 us -> 21.9 us
    ppermute x0 -> x6, waiting for transfers between devices: none -> 83.8 us  [the longest x3 79.9 us: body(): lax.ppermute(right_vals, 'row', perm=perm)]
    all_gather x1, waiting for transfers between devices: 54.9 us -> 0.02 us  [body(): lax.all_gather(left_vals[None], 'col', axis=0, tiled=True)]
    ppermute x0 -> x6, starting transfers between devices: none -> 26.6 us  [the longest x3 13.5 us: body(): lax.ppermute(right_cols, 'row', perm=perm)]
    all_to_all x1 -> x0, blocking collectives: 23.5 us -> none  [body(): lax.all_to_all(right_vals, 'col', split_axis=0, concat_axis=0, tiled=True)]
    all_gather x1 -> x0, blocking collectives: 18.8 us -> none  [body(): lax.all_gather(right_cols[None], 'row', axis=0, tiled=True)]
    all_gather x1, blocking collectives: 16.7 us -> 35.4 us  [body(): lax.all_gather(left_cols[None], 'col', axis=0, tiled=True)]
    reduce_scatter x1, waiting for transfers between devices: 47 us -> 40.3 us  [body(): lax.psum_scatter(partial_sum[None, None], 'depth', scatter_dimension=2, t...]
    all_gather x1 -> x0, waiting for transfers between devices: 6.4 us -> none  [body(): lax.all_gather(right_vals[None], 'row', axis=0, tiled=True)]
  transfers between devices with their start and end apart: 5 -> 11, of which waited for: 4 -> 8; matrix products, arithmetic and copies ran while one was open for 5% -> 7% of each run, Pallas kernels for 0% -> 0%
where the time goes in v3:
time: 284 us; the launch traced here: 283 us
  waiting for transfers between devices  130 us (46%)
  blocking collectives  63.1 us (22%)
  starting transfers between devices  41.4 us (15%)
  local copies, waits for them, and re-layouts  21.9 us (8%)
  between operations  14.3 us (5%)
  other arithmetic  8.12 us (3%)
  matrix products  3.74 us (1%)
    ppermute x3, waiting for transfers between devices, body(): lax.ppermute(right_vals, 'row', perm=perm)  79.9 us
    reduce_scatter x1, waiting for transfers between devices, body(): lax.psum_scatter(partial_sum[None, None], 'depth', scatter_dimension=2, t...  40.3 us
    all_gather x1, blocking collectives, body(): lax.all_gather(left_cols[None], 'col', axis=0, tiled=True)  35.4 us
    all_to_all x1, blocking collectives, body(): lax.all_to_all(left_vals, 'depth', split_axis=0, concat_axis=0, tiled=True)  27.7 us
    ppermute x3, starting transfers between devices, body(): lax.ppermute(right_cols, 'row', perm=perm)  13.5 us
    ppermute x3, starting transfers between devices, body(): lax.ppermute(right_vals, 'row', perm=perm)  13.1 us
    all_to_all x1, waiting for transfers between devices, body(): lax.all_to_all(left_cols, 'depth', split_axis=0, concat_axis=0, tiled=True)  6.14 us
    all_to_all x1, starting transfers between devices, body(): lax.all_to_all(right_cols, 'col', split_axis=0, concat_axis=0, tiled=True)  5.81 us
  transfers between devices with their start and end apart: 11, of which 8 were waited for; matrix products, arithmetic and copies ran while one was open for 7% of the time, Pallas kernels for 0%

profile of v3, /device:TPU:6, one launch (start us, length us, event | category | flops | bytes accessed | tf_op | source)
XLA Modules:
  0.0 283.0 jit_solution(14216771074762856966)
XLA Ops:
  9.3 2.1 scatter_fusion
  11.3 27.7 %all_to_all.20 = bf16[8,1,2,128,128]{4,3,2,1,0:T(8,128)(2,1)} all-to-all(bf16[8,1,2,128,128]{4,3,2,1,0:T(8,128)(2,1)S(1)} %bitcast.101), channel_id=1, replica_groups=mesh['row'=4,'col'=16,'depth'=8] {'depth'}, dimensions={0} | all-to-all | bytes 1048576 | tf_op jit(solution)/shard_map/all_to_all | solution.py:55
  40.5 3.2 %all-to-all-start.1 = ((s32[8,1,2]{2,1,0:T(1,128)}), s32[8,1,2]{2,1,0:T(1,128)S(1)}, u32[]{:S(2)}, u32[]{:S(2)}) async-start(s32[8,1,2]{2,1,0:T(1,128)} %bitcast.11), calls=%async_computation.1 | async-start | bytes 8192 | tf_op jit(solution)/shard_map/all_to_all | solution.py:56
  45.2 6.1 %all-to-all-done.1 = s32[8,1,2]{2,1,0:T(1,128)S(1)} async-done(((s32[8,1,2]{2,1,0:T(1,128)}), s32[8,1,2]{2,1,0:T(1,128)S(1)}, u32[]{:S(2)}, u32[]{:S(2)}) %all-to-all-start.1) | async-done | bytes 96 | tf_op jit(solution)/shard_map/all_to_all | solution.py:56
  51.3 5.8 %all-to-all-start.2 = ((s32[16,1,2]{2,1,0:T(1,128)}), s32[16,1,2]{2,1,0:T(1,128)S(1)}, u32[]{:S(2)}, u32[]{:S(2)}) async-start(s32[16,1,2]{2,1,0:T(1,128)} %bitcast.14), calls=%async_computation.2 | async-start | bytes 16384 | tf_op jit(solution)/shard_map/all_to_all | solution.py:76
  58.5 2.6 scatter_fusion.1
  61.2 5.7 %all-to-all-start.3 = ((bf16[16,1,2,128,128]{4,3,2,1,0:T(8,128)(2,1)}), bf16[16,1,2,128,128]{4,3,2,1,0:T(8,128)(2,1)S(1)}, u32[]{:S(2)}, u32[]{:S(2)}) async-start(bf16[16,1,2,128,128]{4,3,2,1,0:T(8,128)(2,1)} %bitcast.22), calls=%async_computation.3 | async-start | bytes 2097152 | tf_op jit(solution)/shard_map/all_to_all | solution.py:75
  67.6 35.4 %all-gather.1 = s32[128,1,2]{2,1,0:T(1,128)S(1)} all-gather(s32[8,1,2]{2,1,0:T(1,128)S(1)} %all-to-all-done.1), channel_id=3, replica_groups=mesh['row'=4,'col'=16,'depth'=8] {'col'}, dimensions={0}, use_global_device_ids=true | all-gather | bytes 1088 | tf_op jit(solution)/shard_map/all_gather | solution.py:60
  106.1 5.3 %collective-permute-start.2 = (s32[16,1,2]{2,1,0:T(1,128)S(1)}, s32[16,1,2]{2,1,0:T(1,128)S(1)}, u32[]{:S(2)}, u32[]{:S(2)}) collective-permute-start(s32[16,1,2]{2,1,0:T(1,128)S(1)} %all-to-all-done.2), channel_id=1, source_target_pairs={{0,384},{128,0},{256,128},{384,256},{1,385},{129,1},{257,129},{385... | collective-permute-start | bytes 392 | tf_op jit(solution)/shard_map/ppermute | solution.py:86
  111.4 4.6 %collective-permute-start.1 = (s32[16,1,2]{2,1,0:T(1,128)S(1)}, s32[16,1,2]{2,1,0:T(1,128)S(1)}, u32[]{:S(2)}, u32[]{:S(2)}) collective-permute-start(s32[16,1,2]{2,1,0:T(1,128)S(1)} %all-to-all-done.2), channel_id=1, source_target_pairs={{0,256},{128,384},{256,0},{384,128},{1,257},{129,385},{257,1},{385... | collective-permute-start | bytes 392 | tf_op jit(solution)/shard_map/ppermute | solution.py:86
  116.0 3.6 %collective-permute-start = (s32[16,1,2]{2,1,0:T(1,128)S(1)}, s32[16,1,2]{2,1,0:T(1,128)S(1)}, u32[]{:S(2)}, u32[]{:S(2)}) collective-permute-start(s32[16,1,2]{2,1,0:T(1,128)S(1)} %all-to-all-done.2), channel_id=1, source_target_pairs={{0,128},{128,256},{256,384},{384,0},{1,129},{129,257},{257,385},{3... | collective-permute-start | bytes 392 | tf_op jit(solution)/shard_map/ppermute | solution.py:86
  121.0 2.7 collective-permute-done
  123.8 5.2 %collective-permute-start.4 = (bf16[16,1,2,128,128]{4,3,2,0,1:T(8,128)(2,1)S(1)}, bf16[16,1,2,128,128]{4,3,2,0,1:T(8,128)(2,1)S(1)}, u32[]{:S(2)}, u32[]{:S(2)}) collective-permute-start(bf16[16,1,2,128,128]{4,3,2,0,1:T(8,128)(2,1)S(1)} %bitcast.102), channel_id=1, source_target_pairs={{0,256},{128,384},{256,0},{384,128},{1,257},{129,385},{257,1},{385... | collective-permute-start | bytes 3145736 | tf_op jit(solution)/shard_map/ppermute | solution.py:83
  128.9 1.9 collective-permute-start.3
  130.9 6.0 %collective-permute-start.5 = (bf16[16,1,2,128,128]{4,3,2,1,0:T(8,128)(2,1)S(1)}, bf16[16,1,2,128,128]{4,3,2,1,0:T(8,128)(2,1)}, u32[]{:S(2)}, u32[]{:S(2)}) collective-permute-start(bf16[16,1,2,128,128]{4,3,2,1,0:T(8,128)(2,1)S(1)} %all-to-all-done.3), channel_id=1, source_target_pairs={{0,384},{128,0},{256,128},{384,256},{1,385},{129,1},{257,129},{385... | collective-permute-start | bytes 3145736 | tf_op jit(solution)/shard_map/ppermute | solution.py:83
  138.4 37.3 %collective-permute-done.4 = bf16[16,1,2,128,128]{4,3,2,0,1:T(8,128)(2,1)S(1)} collective-permute-done((bf16[16,1,2,128,128]{4,3,2,0,1:T(8,128)(2,1)S(1)}, bf16[16,1,2,128,128]{4,3,2,0,1:T(8,128)(2,1)S(1)}, u32[]{:S(2)}, u32[]{:S(2)}) %collective-permute-start.4) | collective-permute-done | bytes 1048608 | tf_op jit(solution)/shard_map/ppermute | solution.py:83
  175.7 20.9 %collective-permute-done.3 = bf16[16,1,2,128,128]{4,3,2,0,1:T(8,128)(2,1)S(1)} collective-permute-done((bf16[16,1,2,128,128]{4,3,2,0,1:T(8,128)(2,1)S(1)}, bf16[16,1,2,128,128]{4,3,2,0,1:T(8,128)(2,1)S(1)}, u32[]{:S(2)}, u32[]{:S(2)}) %collective-permute-start.3) | collective-permute-done | bytes 1048608 | tf_op jit(solution)/shard_map/ppermute | solution.py:83
  196.6 21.8 %collective-permute-done.5 = bf16[16,1,2,128,128]{4,3,2,1,0:T(8,128)(2,1)} collective-permute-done((bf16[16,1,2,128,128]{4,3,2,1,0:T(8,128)(2,1)S(1)}, bf16[16,1,2,128,128]{4,3,2,1,0:T(8,128)(2,1)}, u32[]{:S(2)}, u32[]{:S(2)}) %collective-permute-start.5) | collective-permute-done | bytes 1048608 | tf_op jit(solution)/shard_map/ppermute | solution.py:83
  218.4 3.3 %pad_maximum_fusion = bf16[4,16,1,2,128,128]{5,4,3,1,2,0:T(8,128)(2,1)} fusion(bf16[1,16,1,2,128,128]{5,4,3,1,2,0:T(8,128)(2,1)} %bitcast.28, bf16[1,16,1,2,128,128]{5,4,3,1,2,0:T(8,128)(2,1)S(1)} %bitcast.110, bf16[1,16,1,2,128,128]{5,4,3,1,2,0:T(8,128)(2,1)S(1)} %bitcast.111, bf16[1,16,1,2,128,128]{5,4,3,1,2,0:T(8,128)(2,1)S(1)} %bitcast.104), kind=kLoop, calls=%fused_computation.8 | loop fusion | flops 6291456 | bytes 8388608 | tf_op jit(solution)/shard_map/stack | solution.py:82
  221.6 3.1 %gather_fusion.3 = bf16[64,128,128]{2,1,0:T(8,128)(2,1)S(1)} fusion(bf16[128,128,128]{2,1,0:T(8,128)(2,1)} %bitcast.100, s32[1024]{0:T(1024)S(1)} %pad_clamp_fusion), kind=kCustom, calls=%fused_computation.3 | custom fusion | bytes 4194560 | tf_op jit(solution)/shard_map/jit(_take)/gather | solution.py:107
  224.8 5.6 %gather_fusion = bf16[64,128,128]{2,1,0:T(8,128)(2,1)} fusion(bf16[256,128,128]{2,1,0:T(8,128)(2,1)} %bitcast.112, s32[1024]{0:T(1024)S(1)} %pad_clamp_fusion.3), kind=kCustom, calls=%fused_computation | custom fusion | bytes 4194560 | tf_op jit(solution)/shard_map/jit(_take)/gather | solution.py:95
  230.4 3.7 %fusion.7 = f32[1,1,32,128,128]{4,3,2,1,0:T(8,128)} fusion(bf16[32,2,128,128]{3,2,1,0:T(8,128)(2,1)S(1)} %bitcast.106, pred[32,2]{1,0:T(8,128)(4,1)S(1)} %copy.74, pred[32,2]{1,0:T(8,128)(4,1)S(1)} %get-tuple-element.5, bf16[32,2,128,128]{3,2,1,0:T(8,128)(2,1)} %bitcast.107, pred[32,2]{1,0:T(8,128)(4,1)S(1)} %copy.59), kind=kOutput, calls=%fused_computation.16 | convolution fusion | flops 271581184 | bytes 6291648 | tf_op jit(solution)/shard_map/pqab,pqbc->pac/dot_general | solution.py:114
  234.2 40.3 %reduce-scatter.2.cloned.1.call-done = f32[1,1,4,128,128]{4,3,2,1,0:T(8,128)} async-done(((f32[1,1,32,128,128]{4,3,2,1,0:T(8,128)}), f32[1,1,4,128,128]{4,3,2,1,0:T(8,128)}) %reduce-scatter.2.cloned.1.call-update) | async-done | bytes 262160 | tf_op jit(solution)/shard_map/reduce_scatter | solution.py:117
  274.4 1.7 log-plus-one_convert_fusion
  (70 shorter events, 13.0 us)
Async XLA Ops:
  6.5 218.3 %all-gather.4.cloned.1.call-start = ((), (), s32[]{:S(2)}) async-start(), calls=%async_computation.6 | async-start | bytes 8912896 | tf_op jit(solution)/shard_map/all_gather | solution.py:59
  9.3 49.2 %copy-start = (bf16[1,1,16,128,128]{4,3,2,1,0:T(8,128)(2,1)S(1)}, bf16[1,1,16,128,128]{4,3,2,1,0:T(8,128)(2,1)}, u32[]{:S(2)}) copy-start(bf16[1,1,16,128,128]{4,3,2,1,0:T(8,128)(2,1)} %param.4) | copy-start | bytes 1572868
  40.5 10.8 %all-to-all-start.1 = ((s32[8,1,2]{2,1,0:T(1,128)}), s32[8,1,2]{2,1,0:T(1,128)S(1)}, u32[]{:S(2)}, u32[]{:S(2)}) async-start(s32[8,1,2]{2,1,0:T(1,128)} %bitcast.11), calls=%async_computation.1 | async-start | bytes 8192 | tf_op jit(solution)/shard_map/all_to_all | solution.py:56
  51.3 9.8 %all-to-all-start.2 = ((s32[16,1,2]{2,1,0:T(1,128)}), s32[16,1,2]{2,1,0:T(1,128)S(1)}, u32[]{:S(2)}, u32[]{:S(2)}) async-start(s32[16,1,2]{2,1,0:T(1,128)} %bitcast.14), calls=%async_computation.2 | async-start | bytes 16384 | tf_op jit(solution)/shard_map/all_to_all | solution.py:76
  58.5 8.5 %copy-start.1 = (s32[1,1,32,2]{2,3,1,0:T(2,128)S(1)}, s32[1,1,32,2]{2,3,1,0:T(2,128)}, u32[]{:S(2)}) copy-start(s32[1,1,32,2]{2,3,1,0:T(2,128)} %param.7) | copy-start | bytes 772
  61.2 62.6 %all-to-all-start.3 = ((bf16[16,1,2,128,128]{4,3,2,1,0:T(8,128)(2,1)}), bf16[16,1,2,128,128]{4,3,2,1,0:T(8,128)(2,1)S(1)}, u32[]{:S(2)}, u32[]{:S(2)}) async-start(bf16[16,1,2,128,128]{4,3,2,1,0:T(8,128)(2,1)} %bitcast.22), calls=%async_computation.3 | async-start | bytes 2097152 | tf_op jit(solution)/shard_map/all_to_all | solution.py:75
  66.9 207.5 %reduce-scatter.2.cloned.1.call-start = ((), (), s32[]{:S(2)}) async-start(), calls=%async_computation.5 | async-start | bytes 2359296 | tf_op jit(solution)/shard_map/reduce_scatter | solution.py:117
  106.1 13.5 %collective-permute-start.2 = (s32[16,1,2]{2,1,0:T(1,128)S(1)}, s32[16,1,2]{2,1,0:T(1,128)S(1)}, u32[]{:S(2)}, u32[]{:S(2)}) collective-permute-start(s32[16,1,2]{2,1,0:T(1,128)S(1)} %all-to-all-done.2), channel_id=1, source_target_pairs={{0,384},{128,0},{256,128},{384,256},{1,385},{129,1},{257,129},{385... | collective-permute-start | bytes 392 | tf_op jit(solution)/shard_map/ppermute | solution.py:86
  111.4 9.5 %collective-permute-start.1 = (s32[16,1,2]{2,1,0:T(1,128)S(1)}, s32[16,1,2]{2,1,0:T(1,128)S(1)}, u32[]{:S(2)}, u32[]{:S(2)}) collective-permute-start(s32[16,1,2]{2,1,0:T(1,128)S(1)} %all-to-all-done.2), channel_id=1, source_target_pairs={{0,256},{128,384},{256,0},{384,128},{1,257},{129,385},{257,1},{385... | collective-permute-start | bytes 392 | tf_op jit(solution)/shard_map/ppermute | solution.py:86
  116.0 7.7 %collective-permute-start = (s32[16,1,2]{2,1,0:T(1,128)S(1)}, s32[16,1,2]{2,1,0:T(1,128)S(1)}, u32[]{:S(2)}, u32[]{:S(2)}) collective-permute-start(s32[16,1,2]{2,1,0:T(1,128)S(1)} %all-to-all-done.2), channel_id=1, source_target_pairs={{0,128},{128,256},{256,384},{384,0},{1,129},{129,257},{257,385},{3... | collective-permute-start | bytes 392 | tf_op jit(solution)/shard_map/ppermute | solution.py:86
  123.8 51.9 %collective-permute-start.4 = (bf16[16,1,2,128,128]{4,3,2,0,1:T(8,128)(2,1)S(1)}, bf16[16,1,2,128,128]{4,3,2,0,1:T(8,128)(2,1)S(1)}, u32[]{:S(2)}, u32[]{:S(2)}) collective-permute-start(bf16[16,1,2,128,128]{4,3,2,0,1:T(8,128)(2,1)S(1)} %bitcast.102), channel_id=1, source_target_pairs={{0,256},{128,384},{256,0},{384,128},{1,257},{129,385},{257,1},{385... | collective-permute-start | bytes 3145736 | tf_op jit(solution)/shard_map/ppermute | solution.py:83
  128.9 67.6 %collective-permute-start.3 = (bf16[16,1,2,128,128]{4,3,2,0,1:T(8,128)(2,1)S(1)}, bf16[16,1,2,128,128]{4,3,2,0,1:T(8,128)(2,1)S(1)}, u32[]{:S(2)}, u32[]{:S(2)}) collective-permute-start(bf16[16,1,2,128,128]{4,3,2,0,1:T(8,128)(2,1)S(1)} %bitcast.103), channel_id=1, source_target_pairs={{0,128},{128,256},{256,384},{384,0},{1,129},{129,257},{257,385},{3... | collective-permute-start | bytes 3145736 | tf_op jit(solution)/shard_map/ppermute | solution.py:83
  130.9 87.5 %collective-permute-start.5 = (bf16[16,1,2,128,128]{4,3,2,1,0:T(8,128)(2,1)S(1)}, bf16[16,1,2,128,128]{4,3,2,1,0:T(8,128)(2,1)}, u32[]{:S(2)}, u32[]{:S(2)}) collective-permute-start(bf16[16,1,2,128,128]{4,3,2,1,0:T(8,128)(2,1)S(1)} %all-to-all-done.3), channel_id=1, source_target_pairs={{0,384},{128,0},{256,128},{384,256},{1,385},{129,1},{257,129},{385... | collective-permute-start | bytes 3145736 | tf_op jit(solution)/shard_map/ppermute | solution.py:83
Sparse Core Ops, SparseCore 0:
  39.2 65.1 all-gather.3
  234.3 40.1 reduce-scatter.1

commit v4 on v1

--- a/solution.py
+++ b/solution.py
@@ -3,7 +3,9 @@
 import jax
 import jax.numpy as jnp
 from jax import lax
-from jax.sharding import PartitionSpec as P
+from jax.sharding import Mesh, PartitionSpec as P
+
+COL = ("ylo", "x", "core")
 
 
 def pack_slots(values, col_ids, targets, is_live, part_count, capacity):
@@ -31,7 +33,7 @@
 
 def body(block_values, block_cols, live_count, out_pattern):
     depths = lax.axis_size("depth")
-    columns = lax.axis_size("col")
+    columns = lax.axis_size(COL)
     row_groups = lax.axis_size("row")
     row_index = lax.axis_index("row")
     rows_dev = block_values.shape[1]
@@ -55,25 +57,17 @@
         lax.all_to_all(left_vals, "depth", split_axis=0, concat_axis=0, tiled=True),
         lax.all_to_all(left_cols, "depth", split_axis=0, concat_axis=0, tiled=True),
     )
-    left_vals, left_cols = (
-        lax.all_gather(left_vals[None], "col", axis=0, tiled=True),
-        lax.all_gather(left_cols[None], "col", axis=0, tiled=True),
-    )
-    left_shape = left_cols.shape
-    source_col = lax.broadcasted_iota(jnp.int32, left_shape, 0)
-    source_depth = lax.broadcasted_iota(jnp.int32, left_shape, 1)
-    source_row = lax.broadcasted_iota(jnp.int32, left_shape, 2)
-    left_rows = (
-        (row_index * depths + source_depth) * group_rows + source_col * rows_dev + source_row
-    ).reshape(-1)
-    left_flat = left_vals.reshape(-1, block_size, block_size)
-    left_ids = left_cols.reshape(-1)
+    chip_vals = lax.all_gather(left_vals[None], ("ylo", "x"), axis=0, tiled=True)
+    other_vals = lax.ppermute(chip_vals, "core", perm=[(0, 1), (1, 0)])
+    core_index = lax.axis_index("core")
+    core_count = lax.axis_size("core")
+    left_cols = lax.all_gather(left_cols[None], COL, axis=0, tiled=True)
     right_vals, right_cols = pack_slots(
         values, col_ids, col_ids // col_block, is_live, columns, cap_right
     )
     right_vals, right_cols = (
-        lax.all_to_all(right_vals, "col", split_axis=0, concat_axis=0, tiled=True),
-        lax.all_to_all(right_cols, "col", split_axis=0, concat_axis=0, tiled=True),
+        lax.all_to_all(right_vals, COL, split_axis=0, concat_axis=0, tiled=True),
+        lax.all_to_all(right_cols, COL, split_axis=0, concat_axis=0, tiled=True),
     )
     right_vals, right_cols = (
         lax.all_gather(right_vals[None], "row", axis=0, tiled=True),
@@ -86,9 +80,18 @@
     local_row = pattern_rows - row_index * (depths * group_rows)
     left_pos = (local_row % group_rows) * depths + local_row // group_rows
     left_sel = left_pos[:, None] * cap_left + jnp.arange(cap_left, dtype=jnp.int32)[None, :]
-    left_flat = left_vals.reshape(-1, block_size, block_size)
     left_ids = left_cols.reshape(-1)
-    left_pick = jnp.take(left_flat, left_sel.reshape(-1), axis=0)
+    source_col = local_row % group_rows
+    chip_sel = (
+        (source_col // core_count * depths + local_row // group_rows)[:, None] * cap_left
+        + jnp.arange(cap_left, dtype=jnp.int32)[None, :]
+    ).reshape(-1)
+    own_core = jnp.repeat(source_col % core_count == core_index, cap_left)
+    left_pick = jnp.where(
+        own_core[:, None, None],
+        jnp.take(chip_vals.reshape(-1, block_size, block_size), chip_sel, axis=0),
+        jnp.take(other_vals.reshape(-1, block_size, block_size), chip_sel, axis=0),
+    )
     inner = jnp.take(left_ids, left_sel, axis=0)
     safe_inner = jnp.maximum(inner, 0)
     right_row = safe_inner // (depths * group_rows) * columns + safe_inner % group_rows
@@ -115,11 +118,16 @@
 
 
 def solution(mesh):
+    rows, cols, depths = mesh.devices.shape
+    chips_x = cols // 4
+    fine = Mesh(
+        mesh.devices.reshape(rows, 2, chips_x, 2, depths), ("row", "ylo", "x", "core", "depth")
+    )
     in_specs = (
-        P(("row", "depth"), "col", None, None, None),
-        P(("row", "depth"), "col", None),
-        P(("row", "depth"), "col"),
-        P("row", "col", None, None),
+        P(("row", "depth"), COL, None, None, None),
+        P(("row", "depth"), COL, None),
+        P(("row", "depth"), COL),
+        P("row", COL, None, None),
     )
-    out_specs = P("row", "col", "depth", None, None)
-    return jax.shard_map(body, mesh=mesh, in_specs=in_specs, out_specs=out_specs, check_vma=False)
+    out_specs = P("row", COL, "depth", None, None)
+    return jax.shard_map(body, mesh=fine, in_specs=in_specs, out_specs=out_specs, check_vma=False)

time: 248 us -> 256 us (1.032)
  waiting for transfers between devices: 114 us -> 103 us
  blocking collectives: 83.8 us -> 91.5 us
  other arithmetic: 4.79 us -> 9.41 us
  local copies, waits for them, and re-layouts: 19 us -> 23.4 us
  starting transfers between devices: 8.13 us -> 11.3 us
    all_gather x1, waiting for transfers between devices: 54.9 us -> 32 us  [body(): lax.all_gather(left_vals[None], ('ylo', 'x'), axis=0, tiled=True)]
    all_gather x1, waiting for transfers between devices: 6.4 us -> 21.1 us  [body(): lax.all_gather(right_vals[None], 'row', axis=0, tiled=True)]
    select_n x3 -> x5, other arithmetic: 1.38 us -> 5.9 us  [the longest x1 2.62 us: body(): jnp.where(own_core[:, None, None], jnp.take(chip_vals.reshape(-1, block_s...]
    all_to_all x1, blocking collectives: 23.5 us -> 27.4 us  [body(): lax.all_to_all(right_vals, COL, split_axis=0, concat_axis=0, tiled=True)]
    gather x1 -> x2, local copies, waits for them, and re-layouts: 5.59 us -> 8.78 us  [the longest x1 4.42 us: body(): jnp.take(chip_vals.reshape(-1, block_size, block_size), chip_sel, axis=0)]
    all_to_all x1, blocking collectives: 24.9 us -> 27.7 us  [body(): lax.all_to_all(left_vals, 'depth', split_axis=0, concat_axis=0, tiled=True)]
  transfers between devices with their start and end apart: 5 -> 6, of which waited for: 4 -> 4; matrix products, arithmetic and copies ran while one was open for 5% -> 8% of each run, Pallas kernels for 0% -> 0%
where the time goes in v4:
time: 256 us; the launch traced here: 255 us
  waiting for transfers between devices  103 us (40%)
  blocking collectives  91.5 us (36%)
  local copies, waits for them, and re-layouts  23.4 us (9%)
  between operations  14.1 us (6%)
  starting transfers between devices  11.3 us (4%)
  other arithmetic  9.41 us (4%)
    reduce_scatter x1, waiting for transfers between devices, body(): lax.psum_scatter(partial_sum[None, None], 'depth', scatter_dimension=2, t...  44.7 us
    all_gather x1, waiting for transfers between devices, body(): lax.all_gather(left_vals[None], ('ylo', 'x'), axis=0, tiled=True)  32 us
    all_to_all x1, blocking collectives, body(): lax.all_to_all(left_vals, 'depth', split_axis=0, concat_axis=0, tiled=True)  27.7 us
    all_to_all x1, blocking collectives, body(): lax.all_to_all(right_vals, COL, split_axis=0, concat_axis=0, tiled=True)  27.4 us
    all_gather x1, waiting for transfers between devices, body(): lax.all_gather(right_vals[None], 'row', axis=0, tiled=True)  21.1 us
    all_gather x1, blocking collectives, body(): lax.all_gather(right_cols[None], 'row', axis=0, tiled=True)  20.2 us
    all_gather x1, blocking collectives, body(): left_cols = lax.all_gather(left_cols[None], COL, axis=0, tiled=True)  16.1 us
    all_to_all x1, starting transfers between devices, body(): lax.all_to_all(right_cols, COL, split_axis=0, concat_axis=0, tiled=True)  6.04 us
  transfers between devices with their start and end apart: 6, of which 4 were waited for; matrix products, arithmetic and copies ran while one was open for 8% of the time, Pallas kernels for 0%

profile of v4, /device:TPU:6, one launch (start us, length us, event | category | flops | bytes accessed | tf_op | source)
XLA Modules:
  0.0 254.7 jit_solution(2445932648093475256)
XLA Ops:
  9.3 2.1 scatter_fusion
  11.3 27.7 %all_to_all.20 = bf16[8,1,2,128,128]{4,3,2,1,0:T(8,128)(2,1)} all-to-all(bf16[8,1,2,128,128]{4,3,2,1,0:T(8,128)(2,1)S(1)} %bitcast.83), channel_id=1, replica_groups=mesh['row'=4,'ylo'=2,'x'=4,'core'=2,'depth'=8] {'depth'}, dimensions={0} | all-to-all | bytes 1048576 | tf_op jit(solution)/shard_map/all_to_all | solution.py:57
  39.4 1.1 scatter_fusion.1
  40.5 27.4 %all_to_all.21 = bf16[16,1,2,128,128]{4,3,2,1,0:T(8,128)(2,1)} all-to-all(bf16[16,1,2,128,128]{4,3,2,1,0:T(8,128)(2,1)S(1)} %bitcast.82), channel_id=1, replica_groups=mesh['row'=4,'ylo'=2,'x'=4,'core'=2,'depth'=8] {'ylo','x','core'}, dimensions={0} | all-to-all | bytes 2097152 | tf_op jit(solution)/shard_map/all_to_all | solution.py:69
  68.0 32.0 %all-gather.7.cloned.1.call-done = bf16[64,1,2,128,128]{4,3,2,1,0:T(8,128)(2,1)} async-done(((bf16[8,1,2,128,128]{4,3,2,1,0:T(8,128)(2,1)}), bf16[64,1,2,128,128]{4,3,2,1,0:T(8,128)(2,1)}) %all-gather.7.cloned.1.call-update) | async-done | bytes 4194320 | tf_op jit(solution)/shard_map/all_gather | solution.py:60
  100.0 1.9 collective-permute-start
  101.9 0.8 scatter_custom_fusion.1
  103.3 3.3 %all-to-all-start.1 = ((s32[8,1,2]{2,1,0:T(1,128)}), s32[8,1,2]{2,1,0:T(1,128)S(1)}, u32[]{:S(2)}, u32[]{:S(2)}) async-start(s32[8,1,2]{2,1,0:T(1,128)} %bitcast.12), calls=%async_computation.1 | async-start | bytes 8192 | tf_op jit(solution)/shard_map/all_to_all | solution.py:58
  106.6 0.8 scatter_custom_fusion.2
  109.1 5.2 %all-to-all-done.1 = s32[8,1,2]{2,1,0:T(1,128)S(1)} async-done(((s32[8,1,2]{2,1,0:T(1,128)}), s32[8,1,2]{2,1,0:T(1,128)S(1)}, u32[]{:S(2)}, u32[]{:S(2)}) %all-to-all-start.1) | async-done | bytes 96 | tf_op jit(solution)/shard_map/all_to_all | solution.py:58
  114.2 6.0 %all-to-all-start.2 = ((s32[16,1,2]{2,1,0:T(1,128)}), s32[16,1,2]{2,1,0:T(1,128)S(1)}, u32[]{:S(2)}, u32[]{:S(2)}) async-start(s32[16,1,2]{2,1,0:T(1,128)} %bitcast.15), calls=%async_computation.2 | async-start | bytes 16384 | tf_op jit(solution)/shard_map/all_to_all | solution.py:70
  120.3 16.1 %all-gather.1 = s32[128,1,2]{2,1,0:T(1,128)S(1)} all-gather(s32[8,1,2]{2,1,0:T(1,128)S(1)} %all-to-all-done.1), channel_id=3, replica_groups=mesh['row'=4,'ylo'=2,'x'=4,'core'=2,'depth'=8] {'ylo','x','core'}, dimensions={0}, use_global_device_ids=true | all-gather | bytes 1088 | tf_op jit(solution)/shard_map/all_gather | solution.py:64
  137.0 0.8 reduce.5
  137.9 0.8 gather_fusion
  139.4 20.2 %all-gather.2 = s32[64,1,2]{2,1,0:T(1,128)S(1)} all-gather(s32[16,1,2]{2,1,0:T(1,128)S(1)} %all-to-all-done.2), channel_id=4, replica_groups=mesh['row'=4,'ylo'=2,'x'=4,'core'=2,'depth'=8] {'row'}, dimensions={0}, use_global_device_ids=true | all-gather | bytes 640 | tf_op jit(solution)/shard_map/all_gather | solution.py:74
  160.9 4.4 %gather_fusion.2 = bf16[64,128,128]{2,1,0:T(8,128)(2,1)} fusion(bf16[128,128,128]{2,1,0:T(8,128)(2,1)} %bitcast.88, s32[1024]{0:T(1024)S(1)} %pad_clamp_fusion.3), kind=kCustom, calls=%fused_computation.clone | custom fusion | bytes 4194560 | tf_op jit(solution)/shard_map/jit(_take)/gather | solution.py:92
  165.3 21.1 %all-gather.9.cloned.1.call-done = bf16[64,1,2,128,128]{4,3,2,1,0:T(8,128)(2,1)} async-done(((bf16[16,1,2,128,128]{4,3,2,1,0:T(8,128)(2,1)}), bf16[64,1,2,128,128]{4,3,2,1,0:T(8,128)(2,1)}) %all-gather.9.cloned.1.call-update) | async-done | bytes 4194320 | tf_op jit(solution)/shard_map/all_gather | solution.py:73
  186.5 4.3 %gather_fusion.4 = bf16[64,128,128]{2,1,0:T(8,128)(2,1)} fusion(bf16[128,128,128]{2,1,0:T(8,128)(2,1)} %bitcast.89, s32[1024]{0:T(1024)S(1)} %pad_clamp_fusion), kind=kCustom, calls=%fused_computation.2.clone | custom fusion | bytes 4194560 | tf_op jit(solution)/shard_map/jit(_take)/gather | solution.py:106
  190.8 1.9 select_select_fusion
  192.7 4.4 %gather_fusion.3 = bf16[64,128,128]{2,1,0:T(8,128)(2,1)} fusion(bf16[128,128,128]{2,1,0:T(8,128)(2,1)} %bitcast.10, s32[1024]{0:T(1024)S(1)} %pad_clamp_fusion.3), kind=kCustom, calls=%fused_computation.1.clone | custom fusion | bytes 4194560 | tf_op jit(solution)/shard_map/jit(_take)/gather | solution.py:93
  197.1 2.6 %select_select_fusion.1 = bf16[64,128,128]{2,1,0:T(8,128)(2,1)S(1)} fusion(bf16[64,128,128]{2,1,0:T(8,128)(2,1)} %gather_fusion.3, bf16[64,128,128]{2,1,0:T(8,128)(2,1)} %gather_fusion.2, pred[64]{0:T(512)(128)(4,1)S(1)} %compare_and_fusion.1, pred[64]{0:T(512)(128)(4,1)S(1)} %broadcast_in_dim.115), kind=kLoop, calls=%fused_computation.10 | loop fusion | flops 3145728 | bytes 6291584 | tf_op jit(solution)/shard_map/jit(_where)/select_n | solution.py:90
  199.7 2.0 convolution_bitcast_fusion
  201.8 44.7 %reduce-scatter.2.cloned.1.call-done = f32[1,1,4,128,128]{4,3,2,1,0:T(8,128)} async-done(((f32[1,1,32,128,128]{4,3,2,1,0:T(8,128)}), f32[1,1,4,128,128]{4,3,2,1,0:T(8,128)}) %reduce-scatter.2.cloned.1.call-update) | async-done | bytes 262160 | tf_op jit(solution)/shard_map/reduce_scatter | solution.py:116
  246.5 1.7 log-plus-one_convert_fusion
  (63 shorter events, 7.3 us)
Async XLA Ops:
  6.5 93.4 %all-gather.7.cloned.1.call-start = ((), (), s32[]{:S(2)}) async-start(), calls=%async_computation.6 | async-start | bytes 4718592 | tf_op jit(solution)/shard_map/all_gather | solution.py:60
  9.3 30.1 %copy-start = (bf16[1,1,16,128,128]{4,3,2,1,0:T(8,128)(2,1)S(1)}, bf16[1,1,16,128,128]{4,3,2,1,0:T(8,128)(2,1)}, u32[]{:S(2)}) copy-start(bf16[1,1,16,128,128]{4,3,2,1,0:T(8,128)(2,1)} %param.6) | copy-start | bytes 1572868
  39.1 147.4 %all-gather.9.cloned.1.call-start = ((), (), s32[]{:S(2)}) async-start(), calls=%async_computation.7 | async-start | bytes 5242880 | tf_op jit(solution)/shard_map/all_gather | solution.py:73
  39.4 68.0 %copy-start.1 = (s32[1,1,32,2]{2,3,1,0:T(2,128)S(1)}, s32[1,1,32,2]{2,3,1,0:T(2,128)}, u32[]{:S(2)}) copy-start(s32[1,1,32,2]{2,3,1,0:T(2,128)} %param.9) | copy-start | bytes 772
  100.0 92.8 %collective-permute-start = (bf16[8,8,1,2,128,128]{5,4,3,1,0,2:T(8,128)(2,1)}, bf16[8,8,1,2,128,128]{5,4,3,1,0,2:T(8,128)(2,1)}, u32[]{:S(2)}, u32[]{:S(2)}) collective-permute-start(bf16[8,8,1,2,128,128]{5,4,3,1,0,2:T(8,128)(2,1)} %bitcast.87), channel_id=1, source_target_pairs={{0,8},{8,0},{1,9},{9,1},{2,10},{10,2},{3,11},{11,3},{4,12},{12,4},... | collective-permute-start | bytes 12582920 | tf_op jit(solution)/shard_map/ppermute | solution.py:61
  103.3 10.9 %all-to-all-start.1 = ((s32[8,1,2]{2,1,0:T(1,128)}), s32[8,1,2]{2,1,0:T(1,128)S(1)}, u32[]{:S(2)}, u32[]{:S(2)}) async-start(s32[8,1,2]{2,1,0:T(1,128)} %bitcast.12), calls=%async_computation.1 | async-start | bytes 8192 | tf_op jit(solution)/shard_map/all_to_all | solution.py:58
  114.2 25.2 %all-to-all-start.2 = ((s32[16,1,2]{2,1,0:T(1,128)}), s32[16,1,2]{2,1,0:T(1,128)S(1)}, u32[]{:S(2)}, u32[]{:S(2)}) async-start(s32[16,1,2]{2,1,0:T(1,128)} %bitcast.15), calls=%async_computation.2 | async-start | bytes 16384 | tf_op jit(solution)/shard_map/all_to_all | solution.py:70
  120.2 126.2 %reduce-scatter.2.cloned.1.call-start = ((), (), s32[]{:S(2)}) async-start(), calls=%async_computation.5 | async-start | bytes 2359296 | tf_op jit(solution)/shard_map/reduce_scatter | solution.py:116
Sparse Core Ops, SparseCore 0:
  39.2 60.7 all-gather.6
  102.1 84.3 all-gather.8
  201.9 44.4 reduce-scatter.1

commit v5 on v1

--- a/solution.py
+++ b/solution.py
@@ -29,6 +29,11 @@
     )
 
 
+def gather_by_exchange(x, axis, size):
+    copies = jnp.broadcast_to(x[None], (size,) + x.shape)
+    return lax.all_to_all(copies, axis, split_axis=0, concat_axis=0, tiled=True)
+
+
 def body(block_values, block_cols, live_count, out_pattern):
     depths = lax.axis_size("depth")
     columns = lax.axis_size("col")
@@ -55,10 +60,8 @@
         lax.all_to_all(left_vals, "depth", split_axis=0, concat_axis=0, tiled=True),
         lax.all_to_all(left_cols, "depth", split_axis=0, concat_axis=0, tiled=True),
     )
-    left_vals, left_cols = (
-        lax.all_gather(left_vals[None], "col", axis=0, tiled=True),
-        lax.all_gather(left_cols[None], "col", axis=0, tiled=True),
-    )
+    left_vals = lax.all_gather(left_vals[None], "col", axis=0, tiled=True)
+    left_cols = gather_by_exchange(left_cols, "col", columns)
     left_shape = left_cols.shape
     source_col = lax.broadcasted_iota(jnp.int32, left_shape, 0)
     source_depth = lax.broadcasted_iota(jnp.int32, left_shape, 1)
@@ -75,10 +78,8 @@
         lax.all_to_all(right_vals, "col", split_axis=0, concat_axis=0, tiled=True),
         lax.all_to_all(right_cols, "col", split_axis=0, concat_axis=0, tiled=True),
     )
-    right_vals, right_cols = (
-        lax.all_gather(right_vals[None], "row", axis=0, tiled=True),
-        lax.all_gather(right_cols[None], "row", axis=0, tiled=True),
-    )
+    right_vals = gather_by_exchange(right_vals, "row", row_groups)
+    right_cols = gather_by_exchange(right_cols, "row", row_groups)
     right_flat = right_vals.reshape(-1, cap_right, block_size, block_size)
     right_ids = right_cols.reshape(-1, cap_right)
     pattern_rows = out_pattern[0, 0, :, 0]

time: 248 us -> 272 us (1.097)
  waiting for transfers between devices: 114 us -> 154 us
  blocking collectives: 83.8 us -> 46.6 us
  starting transfers between devices: 8.13 us -> 25.7 us
  local copies, waits for them, and re-layouts: 19 us -> 23.3 us
    all_to_all x0 -> x3, waiting for transfers between devices: none -> 103 us  [gather_by_exchange(): return lax.all_to_all(copies, axis, split_axis=0, concat_axis=0, tiled=True)]
    all_gather x2 -> x1, waiting for transfers between devices: 61.3 us -> 0.02 us  [body(): left_vals = lax.all_gather(left_vals[None], 'col', axis=0, tiled=True)]
    all_gather x2 -> x0, blocking collectives: 35.5 us -> none  [the longest x1 18.8 us: body(): lax.all_gather(right_cols[None], 'row', axis=0, tiled=True)]
    all_to_all x0 -> x3, starting transfers between devices: none -> 16.6 us  [gather_by_exchange(): return lax.all_to_all(copies, axis, split_axis=0, concat_axis=0, tiled=True)]
    reduce_scatter x1, waiting for transfers between devices: 47 us -> 41.2 us  [body(): lax.psum_scatter(partial_sum[None, None], 'depth', scatter_dimension=2, t...]
    all_to_all x1, blocking collectives: 23.5 us -> 18.9 us  [body(): lax.all_to_all(right_vals, 'col', split_axis=0, concat_axis=0, tiled=True)]
    broadcast_in_dim x0 -> x3, local copies, waits for them, and re-layouts: none -> 4.41 us  [gather_by_exchange(): copies = jnp.broadcast_to(x[None], (size,) + x.shape)]
    all_to_all x1, blocking collectives: 24.9 us -> 27.7 us  [body(): lax.all_to_all(left_vals, 'depth', split_axis=0, concat_axis=0, tiled=True)]
  transfers between devices with their start and end apart: 5 -> 7, of which waited for: 4 -> 6; matrix products, arithmetic and copies ran while one was open for 5% -> 6% of each run, Pallas kernels for 0% -> 0%
where the time goes in v5:
time: 272 us
  waiting for transfers between devices  154 us (57%)
  blocking collectives  46.6 us (17%)
  starting transfers between devices  25.7 us (9%)
  local copies, waits for them, and re-layouts  23.3 us (9%)
  between operations  14.3 us (5%)
  other arithmetic  3.99 us (1%)
  matrix products  3.74 us (1%)
    all_to_all x3, waiting for transfers between devices, gather_by_exchange(): return lax.all_to_all(copies, axis, split_axis=0, concat_axis=0, tiled=True)  103 us
    reduce_scatter x1, waiting for transfers between devices, body(): lax.psum_scatter(partial_sum[None, None], 'depth', scatter_dimension=2, t...  41.2 us
    all_to_all x1, blocking collectives, body(): lax.all_to_all(left_vals, 'depth', split_axis=0, concat_axis=0, tiled=True)  27.7 us
    all_to_all x1, blocking collectives, body(): lax.all_to_all(right_vals, 'col', split_axis=0, concat_axis=0, tiled=True)  18.9 us
    all_to_all x3, starting transfers between devices, gather_by_exchange(): return lax.all_to_all(copies, axis, split_axis=0, concat_axis=0, tiled=True)  16.6 us
    all_to_all x1, waiting for transfers between devices, body(): lax.all_to_all(left_cols, 'depth', split_axis=0, concat_axis=0, tiled=True)  7.5 us
    all_to_all x1, starting transfers between devices, body(): lax.all_to_all(right_cols, 'col', split_axis=0, concat_axis=0, tiled=True)  5.81 us
    gather x1, local copies, waits for them, and re-layouts, body(): left_pick = jnp.take(left_flat, left_sel.reshape(-1), axis=0)  5.59 us
  transfers between devices with their start and end apart: 7, of which 6 were waited for; matrix products, arithmetic and copies ran while one was open for 6% of the time, Pallas kernels for 0%

profile of v5, /device:TPU:6, one launch (start us, length us, event | category | flops | bytes accessed | tf_op | source)
XLA Modules:
  0.0 271.6 jit_solution(4329214912613453806)
XLA Ops:
  9.3 2.1 scatter_fusion
  11.4 27.7 %all_to_all.35 = bf16[8,1,2,128,128]{4,3,2,1,0:T(8,128)(2,1)} all-to-all(bf16[8,1,2,128,128]{4,3,2,1,0:T(8,128)(2,1)S(1)} %bitcast.98), channel_id=1, replica_groups=mesh['row'=4,'col'=16,'depth'=8] {'depth'}, dimensions={0} | all-to-all | bytes 1048576 | tf_op jit(solution)/shard_map/all_to_all | solution.py:60
  39.1 0.8 scatter_custom_fusion.2
  39.8 0.7 reshape.1078
  40.5 5.8 %all-to-all-start.3 = ((s32[16,1,2]{2,1,0:T(1,128)}), s32[16,1,2]{2,1,0:T(1,128)S(1)}, u32[]{:S(2)}, u32[]{:S(2)}) async-start(s32[16,1,2]{2,1,0:T(1,128)} %bitcast.15), calls=%async_computation.3 | async-start | bytes 16384 | tf_op jit(solution)/shard_map/all_to_all | solution.py:79
  46.4 0.8 scatter_custom_fusion.1
  47.8 2.6 all-to-all-done.3
  50.4 3.2 %all-to-all-start.1 = ((s32[8,1,2]{2,1,0:T(1,128)}), s32[8,1,2]{2,1,0:T(1,128)S(1)}, u32[]{:S(2)}, u32[]{:S(2)}) async-start(s32[8,1,2]{2,1,0:T(1,128)} %bitcast.11), calls=%async_computation.1 | async-start | bytes 8192 | tf_op jit(solution)/shard_map/all_to_all | solution.py:61
  53.7 7.5 %all-to-all-done.1 = s32[8,1,2]{2,1,0:T(1,128)S(1)} async-done(((s32[8,1,2]{2,1,0:T(1,128)}), s32[8,1,2]{2,1,0:T(1,128)S(1)}, u32[]{:S(2)}, u32[]{:S(2)}) %all-to-all-start.1) | async-done | bytes 96 | tf_op jit(solution)/shard_map/all_to_all | solution.py:61
  61.8 6.2 %all-to-all-start.4 = ((s32[4,16,1,2]{1,3,2,0:T(2,128)}), s32[4,16,1,2]{1,3,2,0:T(2,128)S(1)}, u32[]{:S(2)}, u32[]{:S(2)}) async-start(s32[4,16,1,2]{1,3,2,0:T(2,128)} %broadcast_in_dim.135), calls=%async_computation.4 | async-start | bytes 8192 | tf_op jit(solution)/shard_map/all_to_all | solution.py:34
  68.1 7.6 %all-to-all-done.4 = s32[4,16,1,2]{1,3,2,0:T(2,128)S(1)} async-done(((s32[4,16,1,2]{1,3,2,0:T(2,128)}), s32[4,16,1,2]{1,3,2,0:T(2,128)S(1)}, u32[]{:S(2)}, u32[]{:S(2)}) %all-to-all-start.4) | async-done | bytes 544 | tf_op jit(solution)/shard_map/all_to_all | solution.py:34
  76.3 5.4 %all-to-all-start.2 = ((s32[16,8,1,2]{1,3,2,0:T(2,128)}), s32[16,8,1,2]{1,3,2,0:T(2,128)S(1)}, u32[]{:S(2)}, u32[]{:S(2)}) async-start(s32[16,8,1,2]{1,3,2,0:T(2,128)} %broadcast_in_dim.130), calls=%async_computation.2 | async-start | bytes 32768 | tf_op jit(solution)/shard_map/all_to_all | solution.py:34
  81.9 1.2 scatter_fusion.1
  83.1 2.8 %all-to-all-done.2 = s32[16,8,1,2]{1,3,2,0:T(2,128)S(1)} async-done(((s32[16,8,1,2]{1,3,2,0:T(2,128)}), s32[16,8,1,2]{1,3,2,0:T(2,128)S(1)}, u32[]{:S(2)}, u32[]{:S(2)}) %all-to-all-start.2) | async-done | bytes 1056 | tf_op jit(solution)/shard_map/all_to_all | solution.py:34
  85.9 18.9 %all_to_all.36 = bf16[16,1,2,128,128]{4,3,2,1,0:T(8,128)(2,1)S(1)} all-to-all(bf16[16,1,2,128,128]{4,3,2,1,0:T(8,128)(2,1)S(1)} %bitcast.97), channel_id=1, replica_groups=mesh['row'=4,'col'=16,'depth'=8] {'col'}, dimensions={0} | all-to-all | bytes 2097152 | tf_op jit(solution)/shard_map/all_to_all | solution.py:78
  104.7 3.2 %broadcast_in_dim.144 = bf16[4,16,1,2,128,128]{5,4,3,2,1,0:T(8,128)(2,1)} broadcast(bf16[16,2,128,128]{3,2,1,0:T(8,128)(2,1)S(1)} %bitcast.99), dimensions={1,3,4,5} | broadcast | bytes 5242880 | tf_op jit(solution)/shard_map/broadcast_in_dim | solution.py:33
  107.9 5.1 %all-to-all-start.6 = ((bf16[4,16,1,2,128,128]{5,4,3,2,1,0:T(8,128)(2,1)}), bf16[4,16,1,2,128,128]{5,4,3,2,1,0:T(8,128)(2,1)}, u32[]{:S(2)}, u32[]{:S(2)}) async-start(bf16[4,16,1,2,128,128]{5,4,3,2,1,0:T(8,128)(2,1)} %broadcast_in_dim.144), calls=%async_computation.6 | async-start | bytes 8388608 | tf_op jit(solution)/shard_map/all_to_all | solution.py:34
  114.1 0.8 gather_fusion.1
  117.1 92.2 %all-to-all-done.6 = bf16[4,16,1,2,128,128]{5,4,3,2,1,0:T(8,128)(2,1)} async-done(((bf16[4,16,1,2,128,128]{5,4,3,2,1,0:T(8,128)(2,1)}), bf16[4,16,1,2,128,128]{5,4,3,2,1,0:T(8,128)(2,1)}, u32[]{:S(2)}, u32[]{:S(2)}) %all-to-all-start.6) | async-done | bytes 4194336 | tf_op jit(solution)/shard_map/all_to_all | solution.py:34
  209.3 3.1 %gather_fusion.3 = bf16[64,128,128]{2,1,0:T(8,128)(2,1)S(1)} fusion(bf16[128,128,128]{2,1,0:T(8,128)(2,1)} %bitcast.22, s32[1024]{0:T(1024)S(1)} %pad_clamp_fusion), kind=kCustom, calls=%fused_computation.3 | custom fusion | bytes 4194560 | tf_op jit(solution)/shard_map/jit(_take)/gather | solution.py:104
  212.5 5.6 %gather_fusion = bf16[64,128,128]{2,1,0:T(8,128)(2,1)} fusion(bf16[256,128,128]{2,1,0:T(8,128)(2,1)} %bitcast.105, s32[1024]{0:T(1024)S(1)} %pad_clamp_fusion.3), kind=kCustom, calls=%fused_computation | custom fusion | bytes 4194560 | tf_op jit(solution)/shard_map/jit(_take)/gather | solution.py:92
  218.1 3.7 %fusion.7 = f32[1,1,32,128,128]{4,3,2,1,0:T(8,128)} fusion(bf16[32,2,128,128]{3,2,1,0:T(8,128)(2,1)S(1)} %bitcast.101, pred[32,2]{1,0:T(8,128)(4,1)S(1)} %copy.52, pred[32,2]{1,0:T(8,128)(4,1)S(1)} %get-tuple-element.5, bf16[32,2,128,128]{3,2,1,0:T(8,128)(2,1)} %bitcast.102, pred[32,2]{1,0:T(8,128)(4,1)S(1)} %copy.38), kind=kOutput, calls=%fused_computation.15 | convolution fusion | flops 271581184 | bytes 6291648 | tf_op jit(solution)/shard_map/pqab,pqbc->pac/dot_general | solution.py:111
  221.9 41.2 %reduce-scatter.2.cloned.1.call-done = f32[1,1,4,128,128]{4,3,2,1,0:T(8,128)} async-done(((f32[1,1,32,128,128]{4,3,2,1,0:T(8,128)}), f32[1,1,4,128,128]{4,3,2,1,0:T(8,128)}) %reduce-scatter.2.cloned.1.call-update) | async-done | bytes 262160 | tf_op jit(solution)/shard_map/reduce_scatter | solution.py:114
  263.1 1.7 log-plus-one_convert_fusion
  (60 shorter events, 7.6 us)
Async XLA Ops:
  6.5 206.0 %all-gather.3.cloned.1.call-start = ((), (), s32[]{:S(2)}) async-start(), calls=%async_computation.9 | async-start | bytes 8912896 | tf_op jit(solution)/shard_map/all_gather | solution.py:63
  9.3 72.7 %copy-start = (bf16[1,1,16,128,128]{4,3,2,1,0:T(8,128)(2,1)S(1)}, bf16[1,1,16,128,128]{4,3,2,1,0:T(8,128)(2,1)}, u32[]{:S(2)}) copy-start(bf16[1,1,16,128,128]{4,3,2,1,0:T(8,128)(2,1)} %param.4) | copy-start | bytes 1572868
  40.5 9.8 %all-to-all-start.3 = ((s32[16,1,2]{2,1,0:T(1,128)}), s32[16,1,2]{2,1,0:T(1,128)S(1)}, u32[]{:S(2)}, u32[]{:S(2)}) async-start(s32[16,1,2]{2,1,0:T(1,128)} %bitcast.15), calls=%async_computation.3 | async-start | bytes 16384 | tf_op jit(solution)/shard_map/all_to_all | solution.py:79
  50.4 10.8 %all-to-all-start.1 = ((s32[8,1,2]{2,1,0:T(1,128)}), s32[8,1,2]{2,1,0:T(1,128)S(1)}, u32[]{:S(2)}, u32[]{:S(2)}) async-start(s32[8,1,2]{2,1,0:T(1,128)} %bitcast.11), calls=%async_computation.1 | async-start | bytes 8192 | tf_op jit(solution)/shard_map/all_to_all | solution.py:61
  61.8 13.9 %all-to-all-start.4 = ((s32[4,16,1,2]{1,3,2,0:T(2,128)}), s32[4,16,1,2]{1,3,2,0:T(2,128)S(1)}, u32[]{:S(2)}, u32[]{:S(2)}) async-start(s32[4,16,1,2]{1,3,2,0:T(2,128)} %broadcast_in_dim.135), calls=%async_computation.4 | async-start | bytes 8192 | tf_op jit(solution)/shard_map/all_to_all | solution.py:34
  76.3 9.5 %all-to-all-start.2 = ((s32[16,8,1,2]{1,3,2,0:T(2,128)}), s32[16,8,1,2]{1,3,2,0:T(2,128)S(1)}, u32[]{:S(2)}, u32[]{:S(2)}) async-start(s32[16,8,1,2]{1,3,2,0:T(2,128)} %broadcast_in_dim.130), calls=%async_computation.2 | async-start | bytes 32768 | tf_op jit(solution)/shard_map/all_to_all | solution.py:34
  107.9 5.1 %copy-start.1 = (s32[1,1,32,2]{2,3,1,0:T(2,128)S(1)}, s32[1,1,32,2]{2,3,1,0:T(2,128)}, u32[]{:S(2)}) copy-start(s32[1,1,32,2]{2,3,1,0:T(2,128)} %param.7) | copy-start | bytes 772
  107.9 101.4 %all-to-all-start.6 = ((bf16[4,16,1,2,128,128]{5,4,3,2,1,0:T(8,128)(2,1)}), bf16[4,16,1,2,128,128]{5,4,3,2,1,0:T(8,128)(2,1)}, u32[]{:S(2)}, u32[]{:S(2)}) async-start(bf16[4,16,1,2,128,128]{5,4,3,2,1,0:T(8,128)(2,1)} %broadcast_in_dim.144), calls=%async_computation.6 | async-start | bytes 8388608 | tf_op jit(solution)/shard_map/all_to_all | solution.py:34
  113.0 150.1 %reduce-scatter.2.cloned.1.call-start = ((), (), s32[]{:S(2)}) async-start(), calls=%async_computation.8 | async-start | bytes 2359296 | tf_op jit(solution)/shard_map/reduce_scatter | solution.py:114
Sparse Core Ops, SparseCore 0:
  39.2 53.7 all-gather.2
  222.0 41.0 reduce-scatter.1

commit v6 on v5

v6 whole, which is shorter than its diff:
```python
import jax
import jax.numpy as jnp
from jax import lax
from jax.sharding import PartitionSpec as P

ID_ROWS = 16
ID_BASE = 32


def pack_slots(values, col_ids, targets, is_live, part_count, capacity):
    slot_count = col_ids.shape[0]
    block_size = values.shape[-1]
    chosen = (targets[:, None] == jnp.arange(part_count, dtype=jnp.int32)[None, :]) & is_live[:, None]
    running = jnp.cumsum(chosen.astype(jnp.int32), axis=0) - 1
    order_in = jnp.sum(jnp.where(chosen, running, 0), axis=1)
    total = part_count * capacity
    position = jnp.where(is_live, targets * capacity + order_in, total)
    packed = jnp.zeros((total, block_size, block_size), values.dtype)
    packed = packed.at[position].set(values, mode="drop")
    packed_cols = jnp.full((total,), -1, jnp.int32).at[position].set(col_ids, mode="drop")
    high = packed_cols // ID_BASE
    low = packed_cols - high * ID_BASE
    codes = jnp.stack([high, low]).reshape(2, part_count, capacity).transpose(1, 0, 2)
    id_rows = jnp.zeros((part_count, ID_ROWS, block_size), values.dtype)
    id_rows = id_rows.at[:, :2, :capacity].set(codes.astype(values.dtype))
    return jnp.concatenate(
        [packed.reshape(part_count, capacity * block_size, block_size), id_rows], axis=1
    )


def unpack_ids(payload, capacity, block_size):
    codes = payload[..., capacity * block_size : capacity * block_size + 2, :capacity]
    codes = codes.astype(jnp.int32)
    return codes[..., 0, :] * ID_BASE + codes[..., 1, :]


def unpack_blocks(payload, capacity, block_size):
    blocks = payload[..., : capacity * block_size, :]
    return blocks.reshape(-1, block_size, block_size)


def gather_by_exchange(x, axis, size):
    copies = jnp.broadcast_to(x[None], (size,) + x.shape)
    return lax.all_to_all(copies, axis, split_axis=0, concat_axis=0, tiled=True)


def body(block_values, block_cols, live_count, out_pattern):
    depths = lax.axis_size("depth")
    columns = lax.axis_size("col")
    row_groups = lax.axis_size("row")
    row_index = lax.axis_index("row")
    slot_count = block_values.shape[2]
    block_size = block_values.shape[3]
    group_rows = columns
    plane_rows = depths * group_rows
    col_block = row_groups * plane_rows // columns
    cap_left = slot_count // depths
    cap_right = 2
    values = block_values.reshape(slot_count, block_size, block_size)
    col_ids = block_cols.reshape(slot_count)
    is_live = jnp.arange(slot_count, dtype=jnp.int32) < live_count.reshape(())

    left = pack_slots(values, col_ids, col_ids // group_rows % depths, is_live, depths, cap_left)
    left = lax.all_to_all(left, "depth", split_axis=0, concat_axis=0, tiled=True)
    left = lax.all_gather(left[None], "col", axis=0, tiled=True)
    right = pack_slots(values, col_ids, col_ids // col_block, is_live, columns, cap_right)
    right = lax.all_to_all(right, "col", split_axis=0, concat_axis=0, tiled=True)
    right = gather_by_exchange(right, "row", row_groups)

    left_ids = unpack_ids(left, cap_left, block_size).reshape(-1)
    right_ids = unpack_ids(right, cap_right, block_size).reshape(-1, cap_right)
    left_flat = unpack_blocks(left, cap_left, block_size)
    right_flat = unpack_blocks(right, cap_right, block_size)

    pattern_rows = out_pattern[0, 0, :, 0]
    pattern_cols = out_pattern[0, 0, :, 1]
    pattern_len = pattern_rows.shape[0]
    local_row = pattern_rows - row_index * plane_rows
    left_pos = (local_row % group_rows) * depths + local_row // group_rows
    left_sel = left_pos[:, None] * cap_left + jnp.arange(cap_left, dtype=jnp.int32)[None, :]
    left_pick = jnp.take(left_flat, left_sel.reshape(-1), axis=0)
    inner = jnp.take(left_ids, left_sel, axis=0)
    safe_inner = jnp.maximum(inner, 0)
    right_row = safe_inner // plane_rows * columns + safe_inner % group_rows
    right_here = jnp.take(right_ids, right_row, axis=0)
    matched = (right_here == pattern_cols[:, None, None]) & (inner >= 0)[:, :, None]
    slot = jnp.sum(
        jnp.where(matched, jnp.arange(cap_right, dtype=jnp.int32)[None, None, :], 0), axis=2
    )
    found = jnp.any(matched, axis=2)
    right_pick = jnp.take(right_flat, (right_row * cap_right + slot).reshape(-1), axis=0)
    right_pick = jnp.where(
        found.reshape(-1)[:, None, None], right_pick, jnp.zeros_like(right_pick)
    )
    left_pick = left_pick.reshape(pattern_len, cap_left, block_size, block_size)
    right_pick = right_pick.reshape(pattern_len, cap_left, block_size, block_size)
    partial_sum = jnp.einsum(
        "pqab,pqbc->pac", left_pick, right_pick, preferred_element_type=jnp.float32
    )
    share = lax.psum_scatter(partial_sum[None, None], "depth", scatter_dimension=2, tiled=True)
    return jnp.log1p(share).astype(jnp.bfloat16)


def solution(mesh):
    in_specs = (
        P(("row", "depth"), "col", None, None, None),
        P(("row", "depth"), "col", None),
        P(("row", "depth"), "col"),
        P("row", "col", None, None),
    )
    out_specs = P("row", "col", "depth", None, None)
    return jax.shard_map(body, mesh=mesh, in_specs=in_specs, out_specs=out_specs, check_vma=False)
```

time: 272 us -> 281 us (1.033)
  starting transfers between devices: 25.7 us -> 6.79 us
  blocking collectives: 46.6 us -> 58.7 us
  local copies, waits for them, and re-layouts: 23.3 us -> 33.6 us
  waiting for transfers between devices: 154 us -> 158 us
    slice x0 -> x3, local copies, waits for them, and re-layouts: none -> 13.3 us  [the longest x2 12.4 us: unpack_blocks(): blocks = payload[..., :capacity * block_size, :]]
    all_to_all x2, blocking collectives: 46.6 us -> 58.7 us  [the longest x1 30.1 us: body(): lax.all_to_all(right, 'col', split_axis=0, concat_axis=0, tiled=True)]
    all_to_all x2 -> x0, waiting for transfers between devices: 10.1 us -> none  [the longest x1 7.5 us: body(): lax.all_to_all(left_cols, 'depth', split_axis=0, concat_axis=0, tiled=True)]
    all_to_all x3 -> x1, starting transfers between devices: 16.6 us -> 6.79 us  [gather_by_exchange(): return lax.all_to_all(copies, axis, split_axis=0, concat_axis=0, tiled=True)]
    reduce_scatter x1, waiting for transfers between devices: 41.2 us -> 50.8 us  [body(): lax.psum_scatter(partial_sum[None, None], 'depth', scatter_dimension=2, t...]
    all_to_all x2 -> x0, starting transfers between devices: 9.04 us -> none  [the longest x1 5.81 us: body(): lax.all_to_all(right_cols, 'col', split_axis=0, concat_axis=0, tiled=True)]
    all_to_all x3 -> x1, waiting for transfers between devices: 103 us -> 108 us  [gather_by_exchange(): return lax.all_to_all(copies, axis, split_axis=0, concat_axis=0, tiled=True)]
  transfers between devices with their start and end apart: 7 -> 3, of which waited for: 6 -> 2; matrix products, arithmetic and copies ran while one was open for 6% -> 4% of each run, Pallas kernels for 0% -> 0%
where the time goes in v6:
time: 281 us
  waiting for transfers between devices  158 us (56%)
  blocking collectives  58.7 us (21%)
  local copies, waits for them, and re-layouts  33.6 us (12%)
  between operations  14.3 us (5%)
  starting transfers between devices  6.79 us (2%)
  other arithmetic  5.46 us (2%)
  matrix products  3.68 us (1%)
    all_to_all x1, waiting for transfers between devices, gather_by_exchange(): return lax.all_to_all(copies, axis, split_axis=0, concat_axis=0, tiled=True)  108 us
    reduce_scatter x1, waiting for transfers between devices, body(): lax.psum_scatter(partial_sum[None, None], 'depth', scatter_dimension=2, t...  50.8 us
    all_to_all x1, blocking collectives, body(): lax.all_to_all(right, 'col', split_axis=0, concat_axis=0, tiled=True)  30.1 us
    all_to_all x1, blocking collectives, body(): lax.all_to_all(left, 'depth', split_axis=0, concat_axis=0, tiled=True)  28.5 us
    slice x2, local copies, waits for them, and re-layouts, unpack_blocks(): blocks = payload[..., :capacity * block_size, :]  12.4 us
    all_to_all x1, starting transfers between devices, gather_by_exchange(): return lax.all_to_all(copies, axis, split_axis=0, concat_axis=0, tiled=True)  6.79 us
  transfers between devices with their start and end apart: 3, of which 2 were waited for; matrix products, arithmetic and copies ran while one was open for 4% of the time, Pallas kernels for 0%

profile of v6, /device:TPU:6, one launch (start us, length us, event | category | flops | bytes accessed | tf_op | source)
XLA Modules:
  0.0 280.8 jit_solution(5348765960851438617)
XLA Ops:
  7.2 0.7 and_select_fusion.9
  8.5 0.7 fusion.35
  9.2 0.8 scatter_custom_fusion.1
  10.3 2.1 scatter_fusion
  12.4 28.5 %all_to_all.15 = bf16[8,272,128]{2,1,0:T(8,128)(2,1)} all-to-all(bf16[8,272,128]{2,1,0:T(8,128)(2,1)S(1)} %fusion.17), channel_id=1, replica_groups=mesh['row'=4,'col'=16,'depth'=8] {'depth'}, dimensions={0} | all-to-all | bytes 1114112 | tf_op jit(solution)/shard_map/all_to_all | solution.py:64
  41.0 0.8 scatter_custom_fusion.3
  42.0 0.2 broadcast_in_dim.114
  42.2 1.2 scatter_fusion.1
  43.5 30.1 %all_to_all.16 = bf16[16,272,128]{2,1,0:T(8,128)(2,1)S(1)} all-to-all(bf16[16,272,128]{2,1,0:T(8,128)(2,1)S(1)} %fusion.13), channel_id=1, replica_groups=mesh['row'=4,'col'=16,'depth'=8] {'col'}, dimensions={0} | all-to-all | bytes 2228224 | tf_op jit(solution)/shard_map/all_to_all | solution.py:67
  73.6 2.6 broadcast_in_dim.116
  76.2 6.8 %all-to-all-start.2 = ((bf16[4,16,272,128]{3,2,1,0:T(8,128)(2,1)}), bf16[4,16,272,128]{3,2,1,0:T(8,128)(2,1)}, u32[]{:S(2)}, u32[]{:S(2)}) async-start(bf16[4,16,272,128]{3,2,1,0:T(8,128)(2,1)} %broadcast_in_dim.116), calls=%async_computation.2 | async-start | bytes 8912896 | tf_op jit(solution)/shard_map/all_to_all | solution.py:44
  83.7 107.5 %all-to-all-done.2 = bf16[4,16,272,128]{3,2,1,0:T(8,128)(2,1)} async-done(((bf16[4,16,272,128]{3,2,1,0:T(8,128)(2,1)}), bf16[4,16,272,128]{3,2,1,0:T(8,128)(2,1)}, u32[]{:S(2)}, u32[]{:S(2)}) %all-to-all-start.2) | async-done | bytes 4456480 | tf_op jit(solution)/shard_map/all_to_all | solution.py:44
  191.2 0.9 slice.102
  192.4 4.7 %slice.105 = bf16[4,16,256,128]{3,2,1,0:T(8,128)(2,1)} slice(bf16[4,16,272,128]{3,2,1,0:T(8,128)(2,1)} %all-to-all-done.2), slice={[0:4], [0:16], [0:256], [0:128]} | slice | bytes 8388608 | tf_op jit(solution)/shard_map/slice | solution.py:38
  197.0 1.0 slice_convert_fusion
  198.0 7.7 %slice.98 = bf16[16,8,256,128]{3,2,1,0:T(8,128)(2,1)} slice(bf16[16,8,272,128]{3,2,1,0:T(8,128)(2,1)} %bitcast.96), slice={[0:16], [0:8], [0:256], [0:128]} | slice | bytes 16777216 | tf_op jit(solution)/shard_map/slice | solution.py:38
  206.1 0.8 gather_fusion.1
  207.7 0.6 gather_fusion.2
  208.3 0.3 copy.68
  209.1 4.3 %gather_fusion = bf16[64,128,128]{2,1,0:T(8,128)(2,1)S(1)} fusion(bf16[256,128,128]{2,1,0:T(8,128)(2,1)} %bitcast.93, s32[1024]{0:T(1024)S(1)} %get-tuple-element.46), kind=kCustom, calls=%fused_computation | custom fusion | bytes 4194560 | tf_op jit(solution)/shard_map/jit(_take)/gather | solution.py:81
  213.5 4.4 %gather_fusion.3 = bf16[64,128,128]{2,1,0:T(8,128)(2,1)} fusion(bf16[128,128,128]{2,1,0:T(8,128)(2,1)} %bitcast.94, s32[1024]{0:T(1024)S(1)} %get-tuple-element.45), kind=kCustom, calls=%fused_computation.3 | custom fusion | bytes 4194560 | tf_op jit(solution)/shard_map/jit(_take)/gather | solution.py:91
  217.8 3.7 %fusion.8 = f32[1,1,32,128,128]{4,3,2,1,0:T(8,128)} fusion(bf16[32,2,128,128]{3,2,1,0:T(8,128)(2,1)} %bitcast.101, pred[32,2]{1,0:T(8,128)(4,1)S(1)} %copy.65, pred[32,2]{1,0:T(8,128)(4,1)S(1)} %get-tuple-element.29, bf16[32,2,128,128]{3,2,1,0:T(8,128)(2,1)S(1)} %bitcast.100, pred[32,2]{1,0:T(8,128)(4,1)S(1)} %copy.52), kind=kOutput, calls=%fused_computation.17 | convolution fusion | flops 271581184 | bytes 6291648 | tf_op jit(solution)/shard_map/pqab,pqbc->pac/dot_general | solution.py:97
  221.5 50.8 %reduce-scatter.2.cloned.1.call-done = f32[1,1,4,128,128]{4,3,2,1,0:T(8,128)} async-done(((f32[1,1,32,128,128]{4,3,2,1,0:T(8,128)}), f32[1,1,4,128,128]{4,3,2,1,0:T(8,128)}) %reduce-scatter.2.cloned.1.call-update) | async-done | bytes 262160 | tf_op jit(solution)/shard_map/reduce_scatter | solution.py:100
  272.3 1.7 log-plus-one_convert_fusion
  (64 shorter events, 3.7 us)
Async XLA Ops:
  6.5 190.5 %all-gather.3.cloned.1.call-start = ((), (), s32[]{:S(2)}) async-start(), calls=%async_computation.5 | async-start | bytes 9469952 | tf_op jit(solution)/shard_map/all_gather | solution.py:65
  12.3 29.9 %copy-start = (bf16[1,1,16,128,128]{4,3,2,1,0:T(8,128)(2,1)S(1)}, bf16[1,1,16,128,128]{4,3,2,1,0:T(8,128)(2,1)}, u32[]{:S(2)}) copy-start(bf16[1,1,16,128,128]{4,3,2,1,0:T(8,128)(2,1)} %param.8) | copy-start | bytes 1572868
  76.2 6.8 %copy-start.1 = (s32[1,1,32,2]{2,3,1,0:T(2,128)S(1)}, s32[1,1,32,2]{2,3,1,0:T(2,128)}, u32[]{:S(2)}) copy-start(s32[1,1,32,2]{2,3,1,0:T(2,128)} %param.11) | copy-start | bytes 772
  76.2 115.0 %all-to-all-start.2 = ((bf16[4,16,272,128]{3,2,1,0:T(8,128)(2,1)}), bf16[4,16,272,128]{3,2,1,0:T(8,128)(2,1)}, u32[]{:S(2)}, u32[]{:S(2)}) async-start(bf16[4,16,272,128]{3,2,1,0:T(8,128)(2,1)} %broadcast_in_dim.116), calls=%async_computation.2 | async-start | bytes 8912896 | tf_op jit(solution)/shard_map/all_to_all | solution.py:44
  83.0 189.3 %reduce-scatter.2.cloned.1.call-start = ((), (), s32[]{:S(2)}) async-start(), calls=%async_computation.4 | async-start | bytes 2359296 | tf_op jit(solution)/shard_map/reduce_scatter | solution.py:100
Sparse Core Ops, SparseCore 0:
  41.1 111.1 all-gather.2
  221.6 50.6 reduce-scatter.1

commit v7 on v1

--- a/solution.py
+++ b/solution.py
@@ -48,6 +48,19 @@
     col_ids = block_cols.reshape(rows_dev, slot_count)
     counts = live_count.reshape(rows_dev)
     is_live = jnp.arange(slot_count, dtype=jnp.int32)[None, :] < counts[:, None]
+    right_vals, right_cols = pack_slots(
+        values, col_ids, col_ids // col_block, is_live, columns, cap_right
+    )
+    right_vals, right_cols = (
+        lax.all_to_all(right_vals, "col", split_axis=0, concat_axis=0, tiled=True),
+        lax.all_to_all(right_cols, "col", split_axis=0, concat_axis=0, tiled=True),
+    )
+    right_rows_vals, right_rows_cols = (
+        lax.all_gather(right_vals[None], "row", axis=0, tiled=True),
+        lax.all_gather(right_cols[None], "row", axis=0, tiled=True),
+    )
+    right_vals, right_cols, values = lax.optimization_barrier((right_vals, right_cols, values))
+    right_vals, right_cols = right_rows_vals, right_rows_cols
     left_vals, left_cols = pack_slots(
         values, col_ids, col_ids // group_rows % depths, is_live, depths, cap_left
     )
@@ -68,17 +81,6 @@
     ).reshape(-1)
     left_flat = left_vals.reshape(-1, block_size, block_size)
     left_ids = left_cols.reshape(-1)
-    right_vals, right_cols = pack_slots(
-        values, col_ids, col_ids // col_block, is_live, columns, cap_right
-    )
-    right_vals, right_cols = (
-        lax.all_to_all(right_vals, "col", split_axis=0, concat_axis=0, tiled=True),
-        lax.all_to_all(right_cols, "col", split_axis=0, concat_axis=0, tiled=True),
-    )
-    right_vals, right_cols = (
-        lax.all_gather(right_vals[None], "row", axis=0, tiled=True),
-        lax.all_gather(right_cols[None], "row", axis=0, tiled=True),
-    )
     right_flat = right_vals.reshape(-1, cap_right, block_size, block_size)
     right_ids = right_cols.reshape(-1, cap_right)
     pattern_rows = out_pattern[0, 0, :, 0]

time: 248 us -> 248 us (level)
  blocking collectives: 83.8 us -> 90.7 us
  starting transfers between devices: 8.13 us -> 3.4 us
    all_to_all x0 -> x1, blocking collectives: none -> 8.83 us  [body(): lax.all_to_all(right_cols, 'col', split_axis=0, concat_axis=0, tiled=True)]
    all_to_all x1 -> x0, starting transfers between devices: 4.77 us -> none  [body(): lax.all_to_all(right_cols, 'col', split_axis=0, concat_axis=0, tiled=True)]
    all_gather x1, waiting for transfers between devices: 6.4 us -> 3.67 us  [body(): lax.all_gather(right_vals[None], 'row', axis=0, tiled=True)]
  transfers between devices with their start and end apart: 5 -> 4, of which waited for: 4 -> 4; matrix products, arithmetic and copies ran while one was open for 5% -> 5% of each run, Pallas kernels for 0% -> 0%
where the time goes in v7:
time: 248 us
  waiting for transfers between devices  113 us (46%)
  blocking collectives  90.7 us (37%)
  local copies, waits for them, and re-layouts  18.4 us (7%)
  between operations  14 us (6%)
  other arithmetic  4.81 us (2%)
  matrix products  3.75 us (2%)
  starting transfers between devices  3.4 us (1%)
    all_gather x1, waiting for transfers between devices, body(): lax.all_gather(left_vals[None], 'col', axis=0, tiled=True)  55.2 us
    reduce_scatter x1, waiting for transfers between devices, body(): lax.psum_scatter(partial_sum[None, None], 'depth', scatter_dimension=2, t...  46.9 us
    all_to_all x1, blocking collectives, body(): lax.all_to_all(left_vals, 'depth', split_axis=0, concat_axis=0, tiled=True)  24.4 us
    all_to_all x1, blocking collectives, body(): lax.all_to_all(right_vals, 'col', split_axis=0, concat_axis=0, tiled=True)  23.5 us
    all_gather x1, blocking collectives, body(): lax.all_gather(left_cols[None], 'col', axis=0, tiled=True)  17.6 us
    all_gather x1, blocking collectives, body(): lax.all_gather(right_cols[None], 'row', axis=0, tiled=True)  16.4 us
    all_to_all x1, blocking collectives, body(): lax.all_to_all(right_cols, 'col', split_axis=0, concat_axis=0, tiled=True)  8.83 us
    all_to_all x1, waiting for transfers between devices, body(): lax.all_to_all(left_cols, 'depth', split_axis=0, concat_axis=0, tiled=True)  6.82 us
  transfers between devices with their start and end apart: 4, of which 4 were waited for; matrix products, arithmetic and copies ran while one was open for 5% of the time, Pallas kernels for 0%

profile of v7, /device:TPU:6, one launch (start us, length us, event | category | flops | bytes accessed | tf_op | source)
XLA Modules:
  0.0 247.6 jit_solution(485157097881314056)
XLA Ops:
  7.2 0.7 and_select_fusion.7
  8.5 0.7 fusion.30
  9.4 2.1 scatter_fusion
  11.5 23.5 %all_to_all.20 = bf16[16,1,2,128,128]{4,3,2,1,0:T(8,128)(2,1)} all-to-all(bf16[16,1,2,128,128]{4,3,2,1,0:T(8,128)(2,1)S(1)} %bitcast.88), channel_id=1, replica_groups=mesh['row'=4,'col'=16,'depth'=8] {'col'}, dimensions={0} | all-to-all | bytes 2097152 | tf_op jit(solution)/shard_map/all_to_all | solution.py:55
  35.0 0.8 scatter_custom_fusion.1
  35.9 8.8 %all_to_all.21 = s32[16,1,2]{2,1,0:T(1,128)S(1)} all-to-all(s32[16,1,2]{2,1,0:T(1,128)S(1)} %bitcast.98), channel_id=1, replica_groups=mesh['row'=4,'col'=16,'depth'=8] {'col'}, dimensions={0} | all-to-all | bytes 256 | tf_op jit(solution)/shard_map/all_to_all | solution.py:56
  44.8 1.1 scatter_fusion.1
  46.0 24.4 %all_to_all.22 = bf16[8,1,2,128,128]{4,3,2,1,0:T(8,128)(2,1)} all-to-all(bf16[8,1,2,128,128]{4,3,2,1,0:T(8,128)(2,1)S(1)} %bitcast.89), channel_id=1, replica_groups=mesh['row'=4,'col'=16,'depth'=8] {'depth'}, dimensions={0} | all-to-all | bytes 1048576 | tf_op jit(solution)/shard_map/all_to_all | solution.py:68
  70.4 0.8 scatter_custom_fusion.3
  71.2 0.7 reshape.1077
  71.9 3.3 %all-to-all-start.3 = ((s32[8,1,2]{2,1,0:T(1,128)}), s32[8,1,2]{2,1,0:T(1,128)S(1)}, u32[]{:S(2)}, u32[]{:S(2)}) async-start(s32[8,1,2]{2,1,0:T(1,128)} %bitcast.17), calls=%async_computation.3 | async-start | bytes 8192 | tf_op jit(solution)/shard_map/all_to_all | solution.py:69
  75.9 6.8 %all-to-all-done.3 = s32[8,1,2]{2,1,0:T(1,128)S(1)} async-done(((s32[8,1,2]{2,1,0:T(1,128)}), s32[8,1,2]{2,1,0:T(1,128)S(1)}, u32[]{:S(2)}, u32[]{:S(2)}) %all-to-all-start.3) | async-done | bytes 96 | tf_op jit(solution)/shard_map/all_to_all | solution.py:69
  82.7 17.6 %all-gather.1 = s32[128,1,2]{2,1,0:T(1,128)S(1)} all-gather(s32[8,1,2]{2,1,0:T(1,128)S(1)} %all-to-all-done.3), channel_id=3, replica_groups=mesh['row'=4,'col'=16,'depth'=8] {'col'}, dimensions={0}, use_global_device_ids=true | all-gather | bytes 1088 | tf_op jit(solution)/shard_map/all_gather | solution.py:73
  100.8 0.8 reduce.5
  101.8 0.8 gather_fusion.1
  103.4 16.4 %all-gather.2 = s32[64,1,2]{2,1,0:T(1,128)S(1)} all-gather(s32[16,1,2]{2,1,0:T(1,128)S(1)} %all_to_all.21), channel_id=4, replica_groups=mesh['row'=4,'col'=16,'depth'=8] {'row'}, dimensions={0}, use_global_device_ids=true | all-gather | bytes 640 | tf_op jit(solution)/shard_map/all_gather | solution.py:60
  119.8 0.6 gather_fusion.2
  121.2 3.7 %all-gather.9.cloned.1.call-done = bf16[64,1,2,128,128]{4,3,2,1,0:T(8,128)(2,1)} async-done(((bf16[16,1,2,128,128]{4,3,2,1,0:T(8,128)(2,1)}), bf16[64,1,2,128,128]{4,3,2,1,0:T(8,128)(2,1)}) %all-gather.9.cloned.1.call-update) | async-done | bytes 4194320 | tf_op jit(solution)/shard_map/all_gather | solution.py:59
  124.9 3.1 %gather_fusion.3 = bf16[64,128,128]{2,1,0:T(8,128)(2,1)S(1)} fusion(bf16[128,128,128]{2,1,0:T(8,128)(2,1)} %bitcast.95, s32[1024]{0:T(1024)S(1)} %pad_clamp_fusion), kind=kCustom, calls=%fused_computation.3 | custom fusion | bytes 4194560 | tf_op jit(solution)/shard_map/jit(_take)/gather | solution.py:105
  128.0 55.2 %all-gather.7.cloned.1.call-done = bf16[128,1,2,128,128]{4,3,2,1,0:T(8,128)(2,1)} async-done(((bf16[8,1,2,128,128]{4,3,2,1,0:T(8,128)(2,1)}), bf16[128,1,2,128,128]{4,3,2,1,0:T(8,128)(2,1)}) %all-gather.7.cloned.1.call-update) | async-done | bytes 8388624 | tf_op jit(solution)/shard_map/all_gather | solution.py:72
  183.2 5.6 %gather_fusion = bf16[64,128,128]{2,1,0:T(8,128)(2,1)} fusion(bf16[256,128,128]{2,1,0:T(8,128)(2,1)} %bitcast.96, s32[1024]{0:T(1024)S(1)} %pad_clamp_fusion.3), kind=kCustom, calls=%fused_computation | custom fusion | bytes 4194560 | tf_op jit(solution)/shard_map/jit(_take)/gather | solution.py:93
  188.8 3.7 %fusion.7 = f32[1,1,32,128,128]{4,3,2,1,0:T(8,128)} fusion(bf16[32,2,128,128]{3,2,1,0:T(8,128)(2,1)S(1)} %bitcast.91, pred[32,2]{1,0:T(8,128)(4,1)S(1)} %copy.44, pred[32,2]{1,0:T(8,128)(4,1)S(1)} %get-tuple-element.7, bf16[32,2,128,128]{3,2,1,0:T(8,128)(2,1)} %bitcast.92, pred[32,2]{1,0:T(8,128)(4,1)S(1)} %copy.33), kind=kOutput, calls=%fused_computation.15 | convolution fusion | flops 271581184 | bytes 6291648 | tf_op jit(solution)/shard_map/pqab,pqbc->pac/dot_general | solution.py:112
  192.5 46.9 %reduce-scatter.2.cloned.1.call-done = f32[1,1,4,128,128]{4,3,2,1,0:T(8,128)} async-done(((f32[1,1,32,128,128]{4,3,2,1,0:T(8,128)}), f32[1,1,4,128,128]{4,3,2,1,0:T(8,128)}) %reduce-scatter.2.cloned.1.call-update) | async-done | bytes 262160 | tf_op jit(solution)/shard_map/reduce_scatter | solution.py:115
  239.4 1.7 log-plus-one_convert_fusion
  (53 shorter events, 3.9 us)
Async XLA Ops:
  6.5 118.3 %all-gather.9.cloned.1.call-start = ((), (), s32[]{:S(2)}) async-start(), calls=%async_computation.7 | async-start | bytes 5242880 | tf_op jit(solution)/shard_map/all_gather | solution.py:59
  11.5 33.3 %copy-start = (bf16[1,1,16,128,128]{4,3,2,1,0:T(8,128)(2,1)S(1)}, bf16[1,1,16,128,128]{4,3,2,1,0:T(8,128)(2,1)}, u32[]{:S(2)}) copy-start(bf16[1,1,16,128,128]{4,3,2,1,0:T(8,128)(2,1)} %param.4) | copy-start | bytes 1572868
  35.0 40.3 %copy-start.1 = (s32[1,1,32,2]{2,3,1,0:T(2,128)S(1)}, s32[1,1,32,2]{2,3,1,0:T(2,128)}, u32[]{:S(2)}) copy-start(s32[1,1,32,2]{2,3,1,0:T(2,128)} %param.7) | copy-start | bytes 772
  35.0 148.2 %all-gather.7.cloned.1.call-start = ((), (), s32[]{:S(2)}) async-start(), calls=%async_computation.6 | async-start | bytes 8912896 | tf_op jit(solution)/shard_map/all_gather | solution.py:72
  71.9 10.8 %all-to-all-start.3 = ((s32[8,1,2]{2,1,0:T(1,128)}), s32[8,1,2]{2,1,0:T(1,128)S(1)}, u32[]{:S(2)}, u32[]{:S(2)}) async-start(s32[8,1,2]{2,1,0:T(1,128)} %bitcast.17), calls=%async_computation.3 | async-start | bytes 8192 | tf_op jit(solution)/shard_map/all_to_all | solution.py:69
  75.2 164.2 %reduce-scatter.2.cloned.1.call-start = ((), (), s32[]{:S(2)}) async-start(), calls=%async_computation.5 | async-start | bytes 2359296 | tf_op jit(solution)/shard_map/reduce_scatter | solution.py:115
Sparse Core Ops, SparseCore 0:
  35.1 89.7 all-gather.8
  127.0 56.1 all-gather.6
  192.7 46.7 reduce-scatter.1

commit v8 on v1

--- a/solution.py
+++ b/solution.py
@@ -29,6 +29,11 @@
     )
 
 
+def gather_by_exchange(x, axis, size):
+    copies = jnp.broadcast_to(x[None], (size,) + x.shape)
+    return lax.all_to_all(copies, axis, split_axis=0, concat_axis=0, tiled=True)
+
+
 def body(block_values, block_cols, live_count, out_pattern):
     depths = lax.axis_size("depth")
     columns = lax.axis_size("col")
@@ -57,7 +62,7 @@
     )
     left_vals, left_cols = (
         lax.all_gather(left_vals[None], "col", axis=0, tiled=True),
-        lax.all_gather(left_cols[None], "col", axis=0, tiled=True),
+        gather_by_exchange(left_cols, "col", columns),
     )
     left_shape = left_cols.shape
     source_col = lax.broadcasted_iota(jnp.int32, left_shape, 0)
@@ -77,7 +82,7 @@
     )
     right_vals, right_cols = (
         lax.all_gather(right_vals[None], "row", axis=0, tiled=True),
-        lax.all_gather(right_cols[None], "row", axis=0, tiled=True),
+        gather_by_exchange(right_cols, "row", row_groups),
     )
     right_flat = right_vals.reshape(-1, cap_right, block_size, block_size)
     right_ids = right_cols.reshape(-1, cap_right)

time: 248 us -> 248 us (level)
  blocking collectives: 83.8 us -> 48.3 us
  waiting for transfers between devices: 114 us -> 136 us
  starting transfers between devices: 8.13 us -> 20.9 us
    all_gather x2 -> x0, blocking collectives: 35.5 us -> none  [the longest x1 18.8 us: body(): lax.all_gather(right_cols[None], 'row', axis=0, tiled=True)]
    all_to_all x0 -> x2, starting transfers between devices: none -> 12.7 us  [gather_by_exchange(): return lax.all_to_all(copies, axis, split_axis=0, concat_axis=0, tiled=True)]
    all_to_all x0 -> x2, waiting for transfers between devices: none -> 11.6 us  [gather_by_exchange(): return lax.all_to_all(copies, axis, split_axis=0, concat_axis=0, tiled=True)]
    all_gather x1, waiting for transfers between devices: 6.4 us -> 11.8 us  [body(): lax.all_gather(right_vals[None], 'row', axis=0, tiled=True)]
    all_to_all x1, waiting for transfers between devices: 0.01 us -> 2.57 us  [body(): lax.all_to_all(right_cols, 'col', split_axis=0, concat_axis=0, tiled=True)]
  transfers between devices with their start and end apart: 5 -> 7, of which waited for: 4 -> 7; matrix products, arithmetic and copies ran while one was open for 5% -> 5% of each run, Pallas kernels for 0% -> 0%
where the time goes in v8:
time: 248 us; the launch traced here: 247 us
  waiting for transfers between devices  136 us (55%)
  blocking collectives  48.3 us (19%)
  starting transfers between devices  20.9 us (8%)
  local copies, waits for them, and re-layouts  20.1 us (8%)
  between operations  14 us (6%)
  other arithmetic  4 us (2%)
  matrix products  3.74 us (2%)
    all_gather x1, waiting for transfers between devices, body(): lax.all_gather(left_vals[None], 'col', axis=0, tiled=True)  55.7 us
    reduce_scatter x1, waiting for transfers between devices, body(): lax.psum_scatter(partial_sum[None, None], 'depth', scatter_dimension=2, t...  46.9 us
    all_to_all x1, blocking collectives, body(): lax.all_to_all(left_vals, 'depth', split_axis=0, concat_axis=0, tiled=True)  24.9 us
    all_to_all x1, blocking collectives, body(): lax.all_to_all(right_vals, 'col', split_axis=0, concat_axis=0, tiled=True)  23.5 us
    all_to_all x2, starting transfers between devices, gather_by_exchange(): return lax.all_to_all(copies, axis, split_axis=0, concat_axis=0, tiled=True)  12.7 us
    all_gather x1, waiting for transfers between devices, body(): lax.all_gather(right_vals[None], 'row', axis=0, tiled=True)  11.8 us
    all_to_all x2, waiting for transfers between devices, gather_by_exchange(): return lax.all_to_all(copies, axis, split_axis=0, concat_axis=0, tiled=True)  11.6 us
    all_to_all x1, waiting for transfers between devices, body(): lax.all_to_all(left_cols, 'depth', split_axis=0, concat_axis=0, tiled=True)  7.44 us
  transfers between devices with their start and end apart: 7, of which 7 were waited for; matrix products, arithmetic and copies ran while one was open for 5% of the time, Pallas kernels for 0%

profile of v8, /device:TPU:6, one launch (start us, length us, event | category | flops | bytes accessed | tf_op | source)
XLA Modules:
  0.0 247.1 jit_solution(16107756363442089522)
XLA Ops:
  8.5 0.7 fusion.30
  9.4 2.1 scatter_fusion.1
  11.5 23.5 %all_to_all.30 = bf16[16,1,2,128,128]{4,3,2,1,0:T(8,128)(2,1)} all-to-all(bf16[16,1,2,128,128]{4,3,2,1,0:T(8,128)(2,1)S(1)} %bitcast.96), channel_id=1, replica_groups=mesh['row'=4,'col'=16,'depth'=8] {'col'}, dimensions={0} | all-to-all | bytes 2097152 | tf_op jit(solution)/shard_map/all_to_all | solution.py:80
  35.2 1.2 scatter_fusion
  36.3 24.9 %all_to_all.31 = bf16[8,1,2,128,128]{4,3,2,1,0:T(8,128)(2,1)} all-to-all(bf16[8,1,2,128,128]{4,3,2,1,0:T(8,128)(2,1)S(1)} %bitcast.97), channel_id=1, replica_groups=mesh['row'=4,'col'=16,'depth'=8] {'depth'}, dimensions={0} | all-to-all | bytes 1048576 | tf_op jit(solution)/shard_map/all_to_all | solution.py:60
  61.2 0.8 scatter_custom_fusion.2
  62.0 0.7 reshape.1075
  62.7 4.8 %all-to-all-start.3 = ((s32[16,1,2]{2,1,0:T(1,128)}), s32[16,1,2]{2,1,0:T(1,128)S(1)}, u32[]{:S(2)}, u32[]{:S(2)}) async-start(s32[16,1,2]{2,1,0:T(1,128)} %bitcast.15), calls=%async_computation.3 | async-start | bytes 16384 | tf_op jit(solution)/shard_map/all_to_all | solution.py:81
  67.4 0.8 scatter_custom_fusion.1
  68.9 2.6 %all-to-all-done.3 = s32[16,1,2]{2,1,0:T(1,128)S(1)} async-done(((s32[16,1,2]{2,1,0:T(1,128)}), s32[16,1,2]{2,1,0:T(1,128)S(1)}, u32[]{:S(2)}, u32[]{:S(2)}) %all-to-all-start.3) | async-done | bytes 160 | tf_op jit(solution)/shard_map/all_to_all | solution.py:81
  71.5 3.3 %all-to-all-start.1 = ((s32[8,1,2]{2,1,0:T(1,128)}), s32[8,1,2]{2,1,0:T(1,128)S(1)}, u32[]{:S(2)}, u32[]{:S(2)}) async-start(s32[8,1,2]{2,1,0:T(1,128)} %bitcast.11), calls=%async_computation.1 | async-start | bytes 8192 | tf_op jit(solution)/shard_map/all_to_all | solution.py:61
  74.9 7.4 %all-to-all-done.1 = s32[8,1,2]{2,1,0:T(1,128)S(1)} async-done(((s32[8,1,2]{2,1,0:T(1,128)}), s32[8,1,2]{2,1,0:T(1,128)S(1)}, u32[]{:S(2)}, u32[]{:S(2)}) %all-to-all-start.1) | async-done | bytes 96 | tf_op jit(solution)/shard_map/all_to_all | solution.py:61
  82.9 6.2 %all-to-all-start.4 = ((s32[4,16,1,2]{1,3,2,0:T(2,128)}), s32[4,16,1,2]{1,3,2,0:T(2,128)S(1)}, u32[]{:S(2)}, u32[]{:S(2)}) async-start(s32[4,16,1,2]{1,3,2,0:T(2,128)} %broadcast_in_dim.130), calls=%async_computation.4 | async-start | bytes 8192 | tf_op jit(solution)/shard_map/all_to_all | solution.py:34
  89.3 7.6 %all-to-all-done.4 = s32[4,16,1,2]{1,3,2,0:T(2,128)S(1)} async-done(((s32[4,16,1,2]{1,3,2,0:T(2,128)}), s32[4,16,1,2]{1,3,2,0:T(2,128)S(1)}, u32[]{:S(2)}, u32[]{:S(2)}) %all-to-all-start.4) | async-done | bytes 544 | tf_op jit(solution)/shard_map/all_to_all | solution.py:34
  97.6 6.5 %all-to-all-start.2 = ((s32[16,8,1,2]{1,3,2,0:T(2,128)}), s32[16,8,1,2]{1,3,2,0:T(2,128)S(1)}, u32[]{:S(2)}, u32[]{:S(2)}) async-start(s32[16,8,1,2]{1,3,2,0:T(2,128)} %broadcast_in_dim.125), calls=%async_computation.2 | async-start | bytes 32768 | tf_op jit(solution)/shard_map/all_to_all | solution.py:34
  104.7 4.0 %all-to-all-done.2 = s32[16,8,1,2]{1,3,2,0:T(2,128)S(1)} async-done(((s32[16,8,1,2]{1,3,2,0:T(2,128)}), s32[16,8,1,2]{1,3,2,0:T(2,128)S(1)}, u32[]{:S(2)}, u32[]{:S(2)}) %all-to-all-start.2) | async-done | bytes 1056 | tf_op jit(solution)/shard_map/all_to_all | solution.py:34
  108.9 0.8 gather_fusion.1
  111.9 11.8 %all-gather.7.cloned.1.call-done = bf16[64,1,2,128,128]{4,3,2,1,0:T(8,128)(2,1)} async-done(((bf16[16,1,2,128,128]{4,3,2,1,0:T(8,128)(2,1)}), bf16[64,1,2,128,128]{4,3,2,1,0:T(8,128)(2,1)}) %all-gather.7.cloned.1.call-update) | async-done | bytes 4194320 | tf_op jit(solution)/shard_map/all_gather | solution.py:84
  123.7 3.1 %gather_fusion.3 = bf16[64,128,128]{2,1,0:T(8,128)(2,1)S(1)} fusion(bf16[128,128,128]{2,1,0:T(8,128)(2,1)} %bitcast.103, s32[1024]{0:T(1024)S(1)} %pad_clamp_fusion), kind=kCustom, calls=%fused_computation.3 | custom fusion | bytes 4194560 | tf_op jit(solution)/shard_map/jit(_take)/gather | solution.py:108
  126.9 55.7 %all-gather.5.cloned.1.call-done = bf16[128,1,2,128,128]{4,3,2,1,0:T(8,128)(2,1)} async-done(((bf16[8,1,2,128,128]{4,3,2,1,0:T(8,128)(2,1)}), bf16[128,1,2,128,128]{4,3,2,1,0:T(8,128)(2,1)}) %all-gather.5.cloned.1.call-update) | async-done | bytes 8388624 | tf_op jit(solution)/shard_map/all_gather | solution.py:64
  182.6 5.6 %gather_fusion = bf16[64,128,128]{2,1,0:T(8,128)(2,1)} fusion(bf16[256,128,128]{2,1,0:T(8,128)(2,1)} %bitcast.104, s32[1024]{0:T(1024)S(1)} %pad_clamp_fusion.3), kind=kCustom, calls=%fused_computation | custom fusion | bytes 4194560 | tf_op jit(solution)/shard_map/jit(_take)/gather | solution.py:96
  188.2 3.7 %fusion.7 = f32[1,1,32,128,128]{4,3,2,1,0:T(8,128)} fusion(bf16[32,2,128,128]{3,2,1,0:T(8,128)(2,1)S(1)} %bitcast.99, pred[32,2]{1,0:T(8,128)(4,1)S(1)} %copy.52, pred[32,2]{1,0:T(8,128)(4,1)S(1)} %get-tuple-element.5, bf16[32,2,128,128]{3,2,1,0:T(8,128)(2,1)} %bitcast.100, pred[32,2]{1,0:T(8,128)(4,1)S(1)} %copy.38), kind=kOutput, calls=%fused_computation.15 | convolution fusion | flops 271581184 | bytes 6291648 | tf_op jit(solution)/shard_map/pqab,pqbc->pac/dot_general | solution.py:115
  191.9 46.9 %reduce-scatter.2.cloned.1.call-done = f32[1,1,4,128,128]{4,3,2,1,0:T(8,128)} async-done(((f32[1,1,32,128,128]{4,3,2,1,0:T(8,128)}), f32[1,1,4,128,128]{4,3,2,1,0:T(8,128)}) %reduce-scatter.2.cloned.1.call-update) | async-done | bytes 262160 | tf_op jit(solution)/shard_map/reduce_scatter | solution.py:118
  238.9 1.7 log-plus-one_convert_fusion
  (60 shorter events, 6.9 us)
Async XLA Ops:
  6.5 117.2 %all-gather.7.cloned.1.call-start = ((), (), s32[]{:S(2)}) async-start(), calls=%async_computation.9 | async-start | bytes 5242880 | tf_op jit(solution)/shard_map/all_gather | solution.py:84
  11.5 23.7 %copy-start = (bf16[1,1,16,128,128]{4,3,2,1,0:T(8,128)(2,1)S(1)}, bf16[1,1,16,128,128]{4,3,2,1,0:T(8,128)(2,1)}, u32[]{:S(2)}) copy-start(bf16[1,1,16,128,128]{4,3,2,1,0:T(8,128)(2,1)} %param.4) | copy-start | bytes 1572868
  35.0 32.4 %copy-start.1 = (s32[1,1,32,2]{2,3,1,0:T(2,128)S(1)}, s32[1,1,32,2]{2,3,1,0:T(2,128)}, u32[]{:S(2)}) copy-start(s32[1,1,32,2]{2,3,1,0:T(2,128)} %param.7) | copy-start | bytes 772
  35.0 147.6 %all-gather.5.cloned.1.call-start = ((), (), s32[]{:S(2)}) async-start(), calls=%async_computation.8 | async-start | bytes 8912896 | tf_op jit(solution)/shard_map/all_gather | solution.py:64
  62.7 8.8 %all-to-all-start.3 = ((s32[16,1,2]{2,1,0:T(1,128)}), s32[16,1,2]{2,1,0:T(1,128)S(1)}, u32[]{:S(2)}, u32[]{:S(2)}) async-start(s32[16,1,2]{2,1,0:T(1,128)} %bitcast.15), calls=%async_computation.3 | async-start | bytes 16384 | tf_op jit(solution)/shard_map/all_to_all | solution.py:81
  71.5 10.9 %all-to-all-start.1 = ((s32[8,1,2]{2,1,0:T(1,128)}), s32[8,1,2]{2,1,0:T(1,128)S(1)}, u32[]{:S(2)}, u32[]{:S(2)}) async-start(s32[8,1,2]{2,1,0:T(1,128)} %bitcast.11), calls=%async_computation.1 | async-start | bytes 8192 | tf_op jit(solution)/shard_map/all_to_all | solution.py:61
  82.9 14.0 %all-to-all-start.4 = ((s32[4,16,1,2]{1,3,2,0:T(2,128)}), s32[4,16,1,2]{1,3,2,0:T(2,128)S(1)}, u32[]{:S(2)}, u32[]{:S(2)}) async-start(s32[4,16,1,2]{1,3,2,0:T(2,128)} %broadcast_in_dim.130), calls=%async_computation.4 | async-start | bytes 8192 | tf_op jit(solution)/shard_map/all_to_all | solution.py:34
  97.6 11.1 %all-to-all-start.2 = ((s32[16,8,1,2]{1,3,2,0:T(2,128)}), s32[16,8,1,2]{1,3,2,0:T(2,128)S(1)}, u32[]{:S(2)}, u32[]{:S(2)}) async-start(s32[16,8,1,2]{1,3,2,0:T(2,128)} %broadcast_in_dim.125), calls=%async_computation.2 | async-start | bytes 32768 | tf_op jit(solution)/shard_map/all_to_all | solution.py:34
  104.1 134.8 %reduce-scatter.2.cloned.1.call-start = ((), (), s32[]{:S(2)}) async-start(), calls=%async_computation.7 | async-start | bytes 2359296 | tf_op jit(solution)/shard_map/reduce_scatter | solution.py:118
Sparse Core Ops, SparseCore 0:
  35.1 88.5 all-gather.6
  125.9 56.6 all-gather.4
  192.1 46.7 reduce-scatter.1

commit v9 on v8

--- a/solution.py
+++ b/solution.py
@@ -115,7 +115,14 @@
     partial_sum = jnp.einsum(
         "pqab,pqbc->pac", left_pick, right_pick, preferred_element_type=jnp.float32
     )
-    share = lax.psum_scatter(partial_sum[None, None], "depth", scatter_dimension=2, tiled=True)
+    pieces = lax.all_to_all(
+        partial_sum.reshape(depths, pattern_len // depths, block_size, block_size),
+        "depth",
+        split_axis=0,
+        concat_axis=0,
+        tiled=True,
+    )
+    share = jnp.sum(pieces, axis=0)[None, None]
     return jnp.log1p(share).astype(jnp.bfloat16)
 
 

time: 248 us -> 258 us (1.040)
  blocking collectives: 48.3 us -> 107 us
  waiting for transfers between devices: 136 us -> 89.1 us
    all_to_all x0 -> x1, blocking collectives: none -> 58.8 us  [body(): lax.all_to_all(partial_sum.reshape(depths, pattern_len // depths, block_s...]
    reduce_scatter x1 -> x0, waiting for transfers between devices: 46.9 us -> none  [body(): lax.psum_scatter(partial_sum[None, None], 'depth', scatter_dimension=2, t...]
  transfers between devices with their start and end apart: 7 -> 6, of which waited for: 7 -> 6; matrix products, arithmetic and copies ran while one was open for 5% -> 5% of each run, Pallas kernels for 0% -> 0%
where the time goes in v9:
time: 258 us; the launch traced here: 257 us
  blocking collectives  107 us (41%)
  waiting for transfers between devices  89.1 us (35%)
  starting transfers between devices  20.8 us (8%)
  local copies, waits for them, and re-layouts  20.1 us (8%)
  between operations  14.3 us (6%)
  other arithmetic  3.16 us (1%)
    all_to_all x1, blocking collectives, body(): lax.all_to_all(partial_sum.reshape(depths, pattern_len // depths, block_s...  58.8 us
    all_gather x1, waiting for transfers between devices, body(): lax.all_gather(left_vals[None], 'col', axis=0, tiled=True)  55.7 us
    all_to_all x1, blocking collectives, body(): lax.all_to_all(left_vals, 'depth', split_axis=0, concat_axis=0, tiled=True)  24.9 us
    all_to_all x1, blocking collectives, body(): lax.all_to_all(right_vals, 'col', split_axis=0, concat_axis=0, tiled=True)  23.5 us
    all_to_all x2, starting transfers between devices, gather_by_exchange(): return lax.all_to_all(copies, axis, split_axis=0, concat_axis=0, tiled=True)  12.7 us
    all_gather x1, waiting for transfers between devices, body(): lax.all_gather(right_vals[None], 'row', axis=0, tiled=True)  12.1 us
    all_to_all x2, waiting for transfers between devices, gather_by_exchange(): return lax.all_to_all(copies, axis, split_axis=0, concat_axis=0, tiled=True)  11.3 us
    all_to_all x1, waiting for transfers between devices, body(): lax.all_to_all(left_cols, 'depth', split_axis=0, concat_axis=0, tiled=True)  7.44 us
  transfers between devices with their start and end apart: 6, of which 6 were waited for; matrix products, arithmetic and copies ran while one was open for 5% of the time, Pallas kernels for 0%

profile of v9, /device:TPU:6, one launch (start us, length us, event | category | flops | bytes accessed | tf_op | source)
XLA Modules:
  0.0 256.9 jit_solution(11781544726622953731)
XLA Ops:
  8.5 0.7 fusion.26
  9.4 2.1 scatter_fusion.1
  11.5 23.5 %all_to_all.35 = bf16[16,1,2,128,128]{4,3,2,1,0:T(8,128)(2,1)} all-to-all(bf16[16,1,2,128,128]{4,3,2,1,0:T(8,128)(2,1)S(1)} %bitcast.97), channel_id=1, replica_groups=mesh['row'=4,'col'=16,'depth'=8] {'col'}, dimensions={0} | all-to-all | bytes 2097152 | tf_op jit(solution)/shard_map/all_to_all | solution.py:80
  35.2 1.1 scatter_fusion
  36.3 24.9 %all_to_all.36 = bf16[8,1,2,128,128]{4,3,2,1,0:T(8,128)(2,1)} all-to-all(bf16[8,1,2,128,128]{4,3,2,1,0:T(8,128)(2,1)S(1)} %bitcast.98), channel_id=1, replica_groups=mesh['row'=4,'col'=16,'depth'=8] {'depth'}, dimensions={0} | all-to-all | bytes 1048576 | tf_op jit(solution)/shard_map/all_to_all | solution.py:60
  61.2 0.8 scatter_custom_fusion.2
  62.0 0.7 reshape.1092
  62.6 4.8 %all-to-all-start.3 = ((s32[16,1,2]{2,1,0:T(1,128)}), s32[16,1,2]{2,1,0:T(1,128)S(1)}, u32[]{:S(2)}, u32[]{:S(2)}) async-start(s32[16,1,2]{2,1,0:T(1,128)} %bitcast.15), calls=%async_computation.3 | async-start | bytes 16384 | tf_op jit(solution)/shard_map/all_to_all | solution.py:81
  67.4 0.8 scatter_custom_fusion.1
  68.9 2.6 %all-to-all-done.3 = s32[16,1,2]{2,1,0:T(1,128)S(1)} async-done(((s32[16,1,2]{2,1,0:T(1,128)}), s32[16,1,2]{2,1,0:T(1,128)S(1)}, u32[]{:S(2)}, u32[]{:S(2)}) %all-to-all-start.3) | async-done | bytes 160 | tf_op jit(solution)/shard_map/all_to_all | solution.py:81
  71.5 3.3 %all-to-all-start.1 = ((s32[8,1,2]{2,1,0:T(1,128)}), s32[8,1,2]{2,1,0:T(1,128)S(1)}, u32[]{:S(2)}, u32[]{:S(2)}) async-start(s32[8,1,2]{2,1,0:T(1,128)} %bitcast.11), calls=%async_computation.1 | async-start | bytes 8192 | tf_op jit(solution)/shard_map/all_to_all | solution.py:61
  74.9 7.4 %all-to-all-done.1 = s32[8,1,2]{2,1,0:T(1,128)S(1)} async-done(((s32[8,1,2]{2,1,0:T(1,128)}), s32[8,1,2]{2,1,0:T(1,128)S(1)}, u32[]{:S(2)}, u32[]{:S(2)}) %all-to-all-start.1) | async-done | bytes 96 | tf_op jit(solution)/shard_map/all_to_all | solution.py:61
  82.9 6.2 %all-to-all-start.4 = ((s32[4,16,1,2]{1,3,2,0:T(2,128)}), s32[4,16,1,2]{1,3,2,0:T(2,128)S(1)}, u32[]{:S(2)}, u32[]{:S(2)}) async-start(s32[4,16,1,2]{1,3,2,0:T(2,128)} %broadcast_in_dim.128), calls=%async_computation.4 | async-start | bytes 8192 | tf_op jit(solution)/shard_map/all_to_all | solution.py:34
  89.3 7.6 %all-to-all-done.4 = s32[4,16,1,2]{1,3,2,0:T(2,128)S(1)} async-done(((s32[4,16,1,2]{1,3,2,0:T(2,128)}), s32[4,16,1,2]{1,3,2,0:T(2,128)S(1)}, u32[]{:S(2)}, u32[]{:S(2)}) %all-to-all-start.4) | async-done | bytes 544 | tf_op jit(solution)/shard_map/all_to_all | solution.py:34
  97.6 6.5 %all-to-all-start.2 = ((s32[16,8,1,2]{1,3,2,0:T(2,128)}), s32[16,8,1,2]{1,3,2,0:T(2,128)S(1)}, u32[]{:S(2)}, u32[]{:S(2)}) async-start(s32[16,8,1,2]{1,3,2,0:T(2,128)} %broadcast_in_dim.123), calls=%async_computation.2 | async-start | bytes 32768 | tf_op jit(solution)/shard_map/all_to_all | solution.py:34
  104.6 3.7 %all-to-all-done.2 = s32[16,8,1,2]{1,3,2,0:T(2,128)S(1)} async-done(((s32[16,8,1,2]{1,3,2,0:T(2,128)}), s32[16,8,1,2]{1,3,2,0:T(2,128)S(1)}, u32[]{:S(2)}, u32[]{:S(2)}) %all-to-all-start.2) | async-done | bytes 1056 | tf_op jit(solution)/shard_map/all_to_all | solution.py:34
  108.6 0.8 gather_fusion.1
  111.6 12.1 %all-gather.7.cloned.1.call-done = bf16[64,1,2,128,128]{4,3,2,1,0:T(8,128)(2,1)} async-done(((bf16[16,1,2,128,128]{4,3,2,1,0:T(8,128)(2,1)}), bf16[64,1,2,128,128]{4,3,2,1,0:T(8,128)(2,1)}) %all-gather.7.cloned.1.call-update) | async-done | bytes 4194320 | tf_op jit(solution)/shard_map/all_gather | solution.py:84
  123.7 3.1 %gather_fusion.3 = bf16[64,128,128]{2,1,0:T(8,128)(2,1)S(1)} fusion(bf16[128,128,128]{2,1,0:T(8,128)(2,1)} %bitcast.105, s32[1024]{0:T(1024)S(1)} %pad_clamp_fusion), kind=kCustom, calls=%fused_computation.3 | custom fusion | bytes 4194560 | tf_op jit(solution)/shard_map/jit(_take)/gather | solution.py:108
  126.8 55.7 %all-gather.5.cloned.1.call-done = bf16[128,1,2,128,128]{4,3,2,1,0:T(8,128)(2,1)} async-done(((bf16[8,1,2,128,128]{4,3,2,1,0:T(8,128)(2,1)}), bf16[128,1,2,128,128]{4,3,2,1,0:T(8,128)(2,1)}) %all-gather.5.cloned.1.call-update) | async-done | bytes 8388624 | tf_op jit(solution)/shard_map/all_gather | solution.py:64
  182.5 5.6 %gather_fusion = bf16[64,128,128]{2,1,0:T(8,128)(2,1)} fusion(bf16[256,128,128]{2,1,0:T(8,128)(2,1)} %bitcast.106, s32[1024]{0:T(1024)S(1)} %pad_clamp_fusion.3), kind=kCustom, calls=%fused_computation | custom fusion | bytes 4194560 | tf_op jit(solution)/shard_map/jit(_take)/gather | solution.py:96
  188.1 2.3 fusion
  190.4 58.8 %all_to_all.37 = f32[8,4,128,128]{3,2,1,0:T(8,128)S(1)} all-to-all(f32[8,4,128,128]{3,2,1,0:T(8,128)S(1)} %bitcast.102), channel_id=1, replica_groups=mesh['row'=4,'col'=16,'depth'=8] {'depth'}, dimensions={0} | all-to-all | bytes 4194304 | tf_op jit(solution)/shard_map/all_to_all | solution.py:118
  249.3 0.7 fusion.9
  (59 shorter events, 7.0 us)
Async XLA Ops:
  6.5 117.2 %all-gather.7.cloned.1.call-start = ((), (), s32[]{:S(2)}) async-start(), calls=%async_computation.8 | async-start | bytes 5242880 | tf_op jit(solution)/shard_map/all_gather | solution.py:84
  11.5 23.7 %copy-start = (bf16[1,1,16,128,128]{4,3,2,1,0:T(8,128)(2,1)S(1)}, bf16[1,1,16,128,128]{4,3,2,1,0:T(8,128)(2,1)}, u32[]{:S(2)}) copy-start(bf16[1,1,16,128,128]{4,3,2,1,0:T(8,128)(2,1)} %param.4) | copy-start | bytes 1572868
  35.0 32.4 %copy-start.1 = (s32[1,1,32,2]{2,3,1,0:T(2,128)S(1)}, s32[1,1,32,2]{2,3,1,0:T(2,128)}, u32[]{:S(2)}) copy-start(s32[1,1,32,2]{2,3,1,0:T(2,128)} %param.7) | copy-start | bytes 772
  35.0 147.5 %all-gather.5.cloned.1.call-start = ((), (), s32[]{:S(2)}) async-start(), calls=%async_computation.7 | async-start | bytes 8912896 | tf_op jit(solution)/shard_map/all_gather | solution.py:64
  62.6 8.8 %all-to-all-start.3 = ((s32[16,1,2]{2,1,0:T(1,128)}), s32[16,1,2]{2,1,0:T(1,128)S(1)}, u32[]{:S(2)}, u32[]{:S(2)}) async-start(s32[16,1,2]{2,1,0:T(1,128)} %bitcast.15), calls=%async_computation.3 | async-start | bytes 16384 | tf_op jit(solution)/shard_map/all_to_all | solution.py:81
  71.5 10.9 %all-to-all-start.1 = ((s32[8,1,2]{2,1,0:T(1,128)}), s32[8,1,2]{2,1,0:T(1,128)S(1)}, u32[]{:S(2)}, u32[]{:S(2)}) async-start(s32[8,1,2]{2,1,0:T(1,128)} %bitcast.11), calls=%async_computation.1 | async-start | bytes 8192 | tf_op jit(solution)/shard_map/all_to_all | solution.py:61
  82.9 14.0 %all-to-all-start.4 = ((s32[4,16,1,2]{1,3,2,0:T(2,128)}), s32[4,16,1,2]{1,3,2,0:T(2,128)S(1)}, u32[]{:S(2)}, u32[]{:S(2)}) async-start(s32[4,16,1,2]{1,3,2,0:T(2,128)} %broadcast_in_dim.128), calls=%async_computation.4 | async-start | bytes 8192 | tf_op jit(solution)/shard_map/all_to_all | solution.py:34
  97.6 10.8 %all-to-all-start.2 = ((s32[16,8,1,2]{1,3,2,0:T(2,128)}), s32[16,8,1,2]{1,3,2,0:T(2,128)S(1)}, u32[]{:S(2)}, u32[]{:S(2)}) async-start(s32[16,8,1,2]{1,3,2,0:T(2,128)} %broadcast_in_dim.123), calls=%async_computation.2 | async-start | bytes 32768 | tf_op jit(solution)/shard_map/all_to_all | solution.py:34
Sparse Core Ops, SparseCore 0:
  35.1 88.5 all-gather.6
  125.8 56.6 all-gather.4

commit v10 on v8

--- a/solution.py
+++ b/solution.py
@@ -60,6 +60,14 @@
         lax.all_to_all(left_vals, "depth", split_axis=0, concat_axis=0, tiled=True),
         lax.all_to_all(left_cols, "depth", split_axis=0, concat_axis=0, tiled=True),
     )
+    right_vals, right_cols = pack_slots(
+        values, col_ids, col_ids // col_block, is_live, columns, cap_right
+    )
+    right_vals, right_cols = (
+        lax.all_to_all(right_vals, "col", split_axis=0, concat_axis=0, tiled=True),
+        lax.all_to_all(right_cols, "col", split_axis=0, concat_axis=0, tiled=True),
+    )
+    left_vals, right_vals = lax.optimization_barrier((left_vals, right_vals))
     left_vals, left_cols = (
         lax.all_gather(left_vals[None], "col", axis=0, tiled=True),
         gather_by_exchange(left_cols, "col", columns),
@@ -73,13 +81,6 @@
     ).reshape(-1)
     left_flat = left_vals.reshape(-1, block_size, block_size)
     left_ids = left_cols.reshape(-1)
-    right_vals, right_cols = pack_slots(
-        values, col_ids, col_ids // col_block, is_live, columns, cap_right
-    )
-    right_vals, right_cols = (
-        lax.all_to_all(right_vals, "col", split_axis=0, concat_axis=0, tiled=True),
-        lax.all_to_all(right_cols, "col", split_axis=0, concat_axis=0, tiled=True),
-    )
     right_vals, right_cols = (
         lax.all_gather(right_vals[None], "row", axis=0, tiled=True),
         gather_by_exchange(right_cols, "row", row_groups),

time: 248 us -> 268 us (1.081)
  waiting for transfers between devices: 136 us -> 173 us
  blocking collectives: 48.3 us -> 20 us
  starting transfers between devices: 20.9 us -> 30.8 us
    all_to_all x1 -> x0, blocking collectives: 24.9 us -> none  [body(): lax.all_to_all(left_vals, 'depth', split_axis=0, concat_axis=0, tiled=True)]
    all_gather x1, waiting for transfers between devices: 11.8 us -> 32.2 us  [body(): lax.all_gather(right_vals[None], 'row', axis=0, tiled=True)]
    all_to_all x0 -> x1, waiting for transfers between devices: none -> 16.1 us  [body(): lax.all_to_all(left_vals, 'depth', split_axis=0, concat_axis=0, tiled=True)]
    all_to_all x0 -> x1, starting transfers between devices: none -> 10.3 us  [body(): lax.all_to_all(left_vals, 'depth', split_axis=0, concat_axis=0, tiled=True)]
    all_to_all x1, blocking collectives: 23.5 us -> 20 us  [body(): lax.all_to_all(right_vals, 'col', split_axis=0, concat_axis=0, tiled=True)]
  transfers between devices with their start and end apart: 7 -> 8, of which waited for: 7 -> 8; matrix products, arithmetic and copies ran while one was open for 5% -> 5% of each run, Pallas kernels for 0% -> 0%
where the time goes in v10:
time: 268 us; the launch traced here: 267 us
  waiting for transfers between devices  173 us (65%)
  starting transfers between devices  30.8 us (11%)
  local copies, waits for them, and re-layouts  21.6 us (8%)
  blocking collectives  20 us (7%)
  between operations  14 us (5%)
  other arithmetic  3.99 us (1%)
  matrix products  3.74 us (1%)
    all_gather x1, waiting for transfers between devices, body(): lax.all_gather(left_vals[None], 'col', axis=0, tiled=True)  54.9 us
    reduce_scatter x1, waiting for transfers between devices, body(): lax.psum_scatter(partial_sum[None, None], 'depth', scatter_dimension=2, t...  47 us
    all_gather x1, waiting for transfers between devices, body(): lax.all_gather(right_vals[None], 'row', axis=0, tiled=True)  32.2 us
    all_to_all x1, blocking collectives, body(): lax.all_to_all(right_vals, 'col', split_axis=0, concat_axis=0, tiled=True)  20 us
    all_to_all x1, waiting for transfers between devices, body(): lax.all_to_all(left_vals, 'depth', split_axis=0, concat_axis=0, tiled=True)  16.1 us
    all_to_all x2, waiting for transfers between devices, gather_by_exchange(): return lax.all_to_all(copies, axis, split_axis=0, concat_axis=0, tiled=True)  12.2 us
    all_to_all x2, starting transfers between devices, gather_by_exchange(): return lax.all_to_all(copies, axis, split_axis=0, concat_axis=0, tiled=True)  11.6 us
    all_to_all x1, starting transfers between devices, body(): lax.all_to_all(left_vals, 'depth', split_axis=0, concat_axis=0, tiled=True)  10.3 us
  transfers between devices with their start and end apart: 8, of which 8 were waited for; matrix products, arithmetic and copies ran while one was open for 5% of the time, Pallas kernels for 0%

profile of v10, /device:TPU:6, one launch (start us, length us, event | category | flops | bytes accessed | tf_op | source)
XLA Modules:
  0.0 267.5 jit_solution(4154580945726285030)
XLA Ops:
  9.2 0.9 broadcast_in_dim.120
  10.1 2.8 %scatter_fusion = bf16[16,128,128]{2,1,0:T(8,128)(2,1)} fusion(bf16[16,128,128]{2,1,0:T(8,128)(2,1)} %broadcast_in_dim.120, s32[16]{0:T(128)S(1)} %get-tuple-element.18, bf16[16,128,128]{2,1,0:T(8,128)(2,1)} %bitcast.100), kind=kCustom, calls=%fused_computation.4 | custom fusion | bytes 1572928 | tf_op jit(solution)/shard_map/scatter | solution.py:22
  12.8 10.3 %all-to-all-start = ((bf16[8,1,2,128,128]{4,3,2,1,0:T(8,128)(2,1)}), bf16[8,1,2,128,128]{4,3,2,1,0:T(8,128)(2,1)S(1)}, u32[]{:S(2)}, u32[]{:S(2)}) async-start(bf16[8,1,2,128,128]{4,3,2,1,0:T(8,128)(2,1)} %bitcast.7), calls=%async_computation | async-start | bytes 1048576 | tf_op jit(solution)/shard_map/all_to_all | solution.py:60
  23.5 1.2 scatter_fusion.1
  24.6 16.1 %all-to-all-done = bf16[8,1,2,128,128]{4,3,2,1,0:T(8,128)(2,1)S(1)} async-done(((bf16[8,1,2,128,128]{4,3,2,1,0:T(8,128)(2,1)}), bf16[8,1,2,128,128]{4,3,2,1,0:T(8,128)(2,1)S(1)}, u32[]{:S(2)}, u32[]{:S(2)}) %all-to-all-start) | async-done | bytes 524320 | tf_op jit(solution)/shard_map/all_to_all | solution.py:60
  40.7 20.0 %all_to_all.30 = bf16[16,1,2,128,128]{4,3,2,1,0:T(8,128)(2,1)} all-to-all(bf16[16,1,2,128,128]{4,3,2,1,0:T(8,128)(2,1)S(1)} %bitcast.96), channel_id=1, replica_groups=mesh['row'=4,'col'=16,'depth'=8] {'col'}, dimensions={0} | all-to-all | bytes 2097152 | tf_op jit(solution)/shard_map/all_to_all | solution.py:67
  61.6 0.8 scatter_custom_fusion.3
  63.0 5.6 %all-to-all-start.4 = ((s32[16,1,2]{2,1,0:T(1,128)}), s32[16,1,2]{2,1,0:T(1,128)S(1)}, u32[]{:S(2)}, u32[]{:S(2)}) async-start(s32[16,1,2]{2,1,0:T(1,128)} %bitcast.16), calls=%async_computation.4 | async-start | bytes 16384 | tf_op jit(solution)/shard_map/all_to_all | solution.py:68
  68.6 0.8 scatter_custom_fusion.2
  70.0 2.6 all-to-all-done.4
  72.6 3.3 %all-to-all-start.2 = ((s32[8,1,2]{2,1,0:T(1,128)}), s32[8,1,2]{2,1,0:T(1,128)S(1)}, u32[]{:S(2)}, u32[]{:S(2)}) async-start(s32[8,1,2]{2,1,0:T(1,128)} %bitcast.14), calls=%async_computation.2 | async-start | bytes 8192 | tf_op jit(solution)/shard_map/all_to_all | solution.py:61
  76.0 7.4 %all-to-all-done.2 = s32[8,1,2]{2,1,0:T(1,128)S(1)} async-done(((s32[8,1,2]{2,1,0:T(1,128)}), s32[8,1,2]{2,1,0:T(1,128)S(1)}, u32[]{:S(2)}, u32[]{:S(2)}) %all-to-all-start.2) | async-done | bytes 96 | tf_op jit(solution)/shard_map/all_to_all | solution.py:61
  84.1 6.2 %all-to-all-start.5 = ((s32[4,16,1,2]{1,3,2,0:T(2,128)}), s32[4,16,1,2]{1,3,2,0:T(2,128)S(1)}, u32[]{:S(2)}, u32[]{:S(2)}) async-start(s32[4,16,1,2]{1,3,2,0:T(2,128)} %broadcast_in_dim.131), calls=%async_computation.5 | async-start | bytes 8192 | tf_op jit(solution)/shard_map/all_to_all | solution.py:34
  90.5 7.6 %all-to-all-done.5 = s32[4,16,1,2]{1,3,2,0:T(2,128)S(1)} async-done(((s32[4,16,1,2]{1,3,2,0:T(2,128)}), s32[4,16,1,2]{1,3,2,0:T(2,128)S(1)}, u32[]{:S(2)}, u32[]{:S(2)}) %all-to-all-start.5) | async-done | bytes 544 | tf_op jit(solution)/shard_map/all_to_all | solution.py:34
  98.7 5.4 %all-to-all-start.3 = ((s32[16,8,1,2]{1,3,2,0:T(2,128)}), s32[16,8,1,2]{1,3,2,0:T(2,128)S(1)}, u32[]{:S(2)}, u32[]{:S(2)}) async-start(s32[16,8,1,2]{1,3,2,0:T(2,128)} %broadcast_in_dim.127), calls=%async_computation.3 | async-start | bytes 32768 | tf_op jit(solution)/shard_map/all_to_all | solution.py:34
  104.7 4.6 %all-to-all-done.3 = s32[16,8,1,2]{1,3,2,0:T(2,128)S(1)} async-done(((s32[16,8,1,2]{1,3,2,0:T(2,128)}), s32[16,8,1,2]{1,3,2,0:T(2,128)S(1)}, u32[]{:S(2)}, u32[]{:S(2)}) %all-to-all-start.3) | async-done | bytes 1056 | tf_op jit(solution)/shard_map/all_to_all | solution.py:34
  109.6 0.8 gather_fusion.1
  112.6 32.2 %all-gather.7.cloned.1.call-done = bf16[64,1,2,128,128]{4,3,2,1,0:T(8,128)(2,1)} async-done(((bf16[16,1,2,128,128]{4,3,2,1,0:T(8,128)(2,1)}), bf16[64,1,2,128,128]{4,3,2,1,0:T(8,128)(2,1)}) %all-gather.7.cloned.1.call-update) | async-done | bytes 4194320 | tf_op jit(solution)/shard_map/all_gather | solution.py:85
  144.8 3.1 %gather_fusion.3 = bf16[64,128,128]{2,1,0:T(8,128)(2,1)S(1)} fusion(bf16[128,128,128]{2,1,0:T(8,128)(2,1)} %bitcast.102, s32[1024]{0:T(1024)S(1)} %pad_clamp_fusion), kind=kCustom, calls=%fused_computation.3 | custom fusion | bytes 4194560 | tf_op jit(solution)/shard_map/jit(_take)/gather | solution.py:109
  147.9 54.9 %all-gather.5.cloned.1.call-done = bf16[128,1,2,128,128]{4,3,2,1,0:T(8,128)(2,1)} async-done(((bf16[8,1,2,128,128]{4,3,2,1,0:T(8,128)(2,1)}), bf16[128,1,2,128,128]{4,3,2,1,0:T(8,128)(2,1)}) %all-gather.5.cloned.1.call-update) | async-done | bytes 8388624 | tf_op jit(solution)/shard_map/all_gather | solution.py:72
  202.9 5.6 %gather_fusion = bf16[64,128,128]{2,1,0:T(8,128)(2,1)} fusion(bf16[256,128,128]{2,1,0:T(8,128)(2,1)} %bitcast.103, s32[1024]{0:T(1024)S(1)} %pad_clamp_fusion.3), kind=kCustom, calls=%fused_computation | custom fusion | bytes 4194560 | tf_op jit(solution)/shard_map/jit(_take)/gather | solution.py:97
  208.5 3.7 %fusion.7 = f32[1,1,32,128,128]{4,3,2,1,0:T(8,128)} fusion(bf16[32,2,128,128]{3,2,1,0:T(8,128)(2,1)S(1)} %bitcast.98, pred[32,2]{1,0:T(8,128)(4,1)S(1)} %copy.52, pred[32,2]{1,0:T(8,128)(4,1)S(1)} %get-tuple-element.9, bf16[32,2,128,128]{3,2,1,0:T(8,128)(2,1)} %bitcast.99, pred[32,2]{1,0:T(8,128)(4,1)S(1)} %copy.38), kind=kOutput, calls=%fused_computation.15 | convolution fusion | flops 271581184 | bytes 6291648 | tf_op jit(solution)/shard_map/pqab,pqbc->pac/dot_general | solution.py:116
  212.2 47.0 %reduce-scatter.2.cloned.1.call-done = f32[1,1,4,128,128]{4,3,2,1,0:T(8,128)} async-done(((f32[1,1,32,128,128]{4,3,2,1,0:T(8,128)}), f32[1,1,4,128,128]{4,3,2,1,0:T(8,128)}) %reduce-scatter.2.cloned.1.call-update) | async-done | bytes 262160 | tf_op jit(solution)/shard_map/reduce_scatter | solution.py:119
  259.2 1.7 log-plus-one_convert_fusion
  (63 shorter events, 8.9 us)
Async XLA Ops:
  9.2 14.3 %copy-start = (bf16[1,1,16,128,128]{4,3,2,1,0:T(8,128)(2,1)S(1)}, bf16[1,1,16,128,128]{4,3,2,1,0:T(8,128)(2,1)}, u32[]{:S(2)}) copy-start(bf16[1,1,16,128,128]{4,3,2,1,0:T(8,128)(2,1)} %param.4) | copy-start | bytes 1572868
  12.8 27.9 %all-to-all-start = ((bf16[8,1,2,128,128]{4,3,2,1,0:T(8,128)(2,1)}), bf16[8,1,2,128,128]{4,3,2,1,0:T(8,128)(2,1)S(1)}, u32[]{:S(2)}, u32[]{:S(2)}) async-start(bf16[8,1,2,128,128]{4,3,2,1,0:T(8,128)(2,1)} %bitcast.7), calls=%async_computation | async-start | bytes 1048576 | tf_op jit(solution)/shard_map/all_to_all | solution.py:60
  23.2 121.6 %all-gather.7.cloned.1.call-start = ((), (), s32[]{:S(2)}) async-start(), calls=%async_computation.9 | async-start | bytes 5242880 | tf_op jit(solution)/shard_map/all_gather | solution.py:85
  24.6 43.9 %copy-start.2 = (s32[1,1,32,2]{2,3,1,0:T(2,128)S(1)}, s32[1,1,32,2]{2,3,1,0:T(2,128)}, u32[]{:S(2)}) copy-start(s32[1,1,32,2]{2,3,1,0:T(2,128)} %param.7) | copy-start | bytes 772
  40.7 20.1 %copy-start.1 = (bf16[8,1,2,128,128]{4,3,2,1,0:T(8,128)(2,1)}, bf16[8,1,2,128,128]{4,3,2,1,0:T(8,128)(2,1)S(1)}, u32[]{:S(2)}) copy-start(bf16[8,1,2,128,128]{4,3,2,1,0:T(8,128)(2,1)S(1)} %all-to-all-done) | copy-start | bytes 1572868
  60.8 142.1 %all-gather.5.cloned.1.call-start = ((), (), s32[]{:S(2)}) async-start(), calls=%async_computation.8 | async-start | bytes 8912896 | tf_op jit(solution)/shard_map/all_gather | solution.py:72
  63.0 9.6 %all-to-all-start.4 = ((s32[16,1,2]{2,1,0:T(1,128)}), s32[16,1,2]{2,1,0:T(1,128)S(1)}, u32[]{:S(2)}, u32[]{:S(2)}) async-start(s32[16,1,2]{2,1,0:T(1,128)} %bitcast.16), calls=%async_computation.4 | async-start | bytes 16384 | tf_op jit(solution)/shard_map/all_to_all | solution.py:68
  72.6 10.9 %all-to-all-start.2 = ((s32[8,1,2]{2,1,0:T(1,128)}), s32[8,1,2]{2,1,0:T(1,128)S(1)}, u32[]{:S(2)}, u32[]{:S(2)}) async-start(s32[8,1,2]{2,1,0:T(1,128)} %bitcast.14), calls=%async_computation.2 | async-start | bytes 8192 | tf_op jit(solution)/shard_map/all_to_all | solution.py:61
  84.1 14.0 %all-to-all-start.5 = ((s32[4,16,1,2]{1,3,2,0:T(2,128)}), s32[4,16,1,2]{1,3,2,0:T(2,128)S(1)}, u32[]{:S(2)}, u32[]{:S(2)}) async-start(s32[4,16,1,2]{1,3,2,0:T(2,128)} %broadcast_in_dim.131), calls=%async_computation.5 | async-start | bytes 8192 | tf_op jit(solution)/shard_map/all_to_all | solution.py:34
  98.7 10.6 %all-to-all-start.3 = ((s32[16,8,1,2]{1,3,2,0:T(2,128)}), s32[16,8,1,2]{1,3,2,0:T(2,128)S(1)}, u32[]{:S(2)}, u32[]{:S(2)}) async-start(s32[16,8,1,2]{1,3,2,0:T(2,128)} %broadcast_in_dim.127), calls=%async_computation.3 | async-start | bytes 32768 | tf_op jit(solution)/shard_map/all_to_all | solution.py:34
  104.1 155.1 %reduce-scatter.2.cloned.1.call-start = ((), (), s32[]{:S(2)}) async-start(), calls=%async_computation.7 | async-start | bytes 2359296 | tf_op jit(solution)/shard_map/reduce_scatter | solution.py:119
Sparse Core Ops, SparseCore 0:
  60.9 83.8 all-gather.6
  146.9 55.9 all-gather.4
  212.3 46.8 reduce-scatter.1

commit v11 on v10

--- a/solution.py
+++ b/solution.py
@@ -67,7 +67,6 @@
         lax.all_to_all(right_vals, "col", split_axis=0, concat_axis=0, tiled=True),
         lax.all_to_all(right_cols, "col", split_axis=0, concat_axis=0, tiled=True),
     )
-    left_vals, right_vals = lax.optimization_barrier((left_vals, right_vals))
     left_vals, left_cols = (
         lax.all_gather(left_vals[None], "col", axis=0, tiled=True),
         gather_by_exchange(left_cols, "col", columns),
@@ -81,6 +80,7 @@
     ).reshape(-1)
     left_flat = left_vals.reshape(-1, block_size, block_size)
     left_ids = left_cols.reshape(-1)
+    right_vals, left_vals = lax.optimization_barrier((right_vals, left_vals))
     right_vals, right_cols = (
         lax.all_gather(right_vals[None], "row", axis=0, tiled=True),
         gather_by_exchange(right_cols, "row", row_groups),

time: 268 us -> 249 us (0.929)
  waiting for transfers between devices: 173 us -> 130 us
  blocking collectives: 20 us -> 54.5 us
  starting transfers between devices: 30.8 us -> 20.9 us
    all_to_all x0 -> x1, blocking collectives: none -> 27.7 us  [body(): lax.all_to_all(left_vals, 'depth', split_axis=0, concat_axis=0, tiled=True)]
    all_gather x1, waiting for transfers between devices: 54.9 us -> 33.6 us  [body(): lax.all_gather(left_vals[None], 'col', axis=0, tiled=True)]
    all_to_all x1 -> x0, waiting for transfers between devices: 16.1 us -> none  [body(): lax.all_to_all(left_vals, 'depth', split_axis=0, concat_axis=0, tiled=True)]
    all_to_all x1 -> x0, starting transfers between devices: 10.3 us -> none  [body(): lax.all_to_all(left_vals, 'depth', split_axis=0, concat_axis=0, tiled=True)]
    all_to_all x1, blocking collectives: 20 us -> 26.8 us  [body(): lax.all_to_all(right_vals, 'col', split_axis=0, concat_axis=0, tiled=True)]
    reduce_scatter x1, waiting for transfers between devices: 47 us -> 44 us  [body(): lax.psum_scatter(partial_sum[None, None], 'depth', scatter_dimension=2, t...]
  transfers between devices with their start and end apart: 8 -> 7, of which waited for: 8 -> 7; matrix products, arithmetic and copies ran while one was open for 5% -> 6% of each run, Pallas kernels for 0% -> 0%
where the time goes in v11:
time: 249 us; the launch traced here: 248 us
  waiting for transfers between devices  130 us (52%)
  blocking collectives  54.5 us (22%)
  starting transfers between devices  20.9 us (8%)
  local copies, waits for them, and re-layouts  20.1 us (8%)
  between operations  14 us (6%)
  other arithmetic  4 us (2%)
  matrix products  3.68 us (1%)
    reduce_scatter x1, waiting for transfers between devices, body(): lax.psum_scatter(partial_sum[None, None], 'depth', scatter_dimension=2, t...  44 us
    all_gather x1, waiting for transfers between devices, body(): lax.all_gather(left_vals[None], 'col', axis=0, tiled=True)  33.6 us
    all_gather x1, waiting for transfers between devices, body(): lax.all_gather(right_vals[None], 'row', axis=0, tiled=True)  30.5 us
    all_to_all x1, blocking collectives, body(): lax.all_to_all(left_vals, 'depth', split_axis=0, concat_axis=0, tiled=True)  27.7 us
    all_to_all x1, blocking collectives, body(): lax.all_to_all(right_vals, 'col', split_axis=0, concat_axis=0, tiled=True)  26.8 us
    all_to_all x2, waiting for transfers between devices, gather_by_exchange(): return lax.all_to_all(copies, axis, split_axis=0, concat_axis=0, tiled=True)  12.3 us
    all_to_all x2, starting transfers between devices, gather_by_exchange(): return lax.all_to_all(copies, axis, split_axis=0, concat_axis=0, tiled=True)  12.1 us
    all_to_all x1, waiting for transfers between devices, body(): lax.all_to_all(left_cols, 'depth', split_axis=0, concat_axis=0, tiled=True)  7.42 us
  transfers between devices with their start and end apart: 7, of which 7 were waited for; matrix products, arithmetic and copies ran while one was open for 6% of the time, Pallas kernels for 0%

profile of v11, /device:TPU:6, one launch (start us, length us, event | category | flops | bytes accessed | tf_op | source)
XLA Modules:
  0.0 247.6 jit_solution(14319230415482835016)
XLA Ops:
  8.5 0.7 fusion.31
  9.3 2.1 scatter_fusion.1
  11.4 27.7 %all_to_all.30 = bf16[8,1,2,128,128]{4,3,2,1,0:T(8,128)(2,1)} all-to-all(bf16[8,1,2,128,128]{4,3,2,1,0:T(8,128)(2,1)S(1)} %bitcast.98), channel_id=1, replica_groups=mesh['row'=4,'col'=16,'depth'=8] {'depth'}, dimensions={0} | all-to-all | bytes 1048576 | tf_op jit(solution)/shard_map/all_to_all | solution.py:60
  39.4 1.2 scatter_fusion
  40.6 26.8 %all_to_all.31 = bf16[16,1,2,128,128]{4,3,2,1,0:T(8,128)(2,1)} all-to-all(bf16[16,1,2,128,128]{4,3,2,1,0:T(8,128)(2,1)S(1)} %bitcast.97), channel_id=1, replica_groups=mesh['row'=4,'col'=16,'depth'=8] {'col'}, dimensions={0} | all-to-all | bytes 2097152 | tf_op jit(solution)/shard_map/all_to_all | solution.py:67
  67.4 33.6 %all-gather.5.cloned.1.call-done = bf16[128,1,2,128,128]{4,3,2,1,0:T(8,128)(2,1)} async-done(((bf16[8,1,2,128,128]{4,3,2,1,0:T(8,128)(2,1)}), bf16[128,1,2,128,128]{4,3,2,1,0:T(8,128)(2,1)}) %all-gather.5.cloned.1.call-update) | async-done | bytes 8388624 | tf_op jit(solution)/shard_map/all_gather | solution.py:71
  101.1 0.8 scatter_custom_fusion.3
  101.8 0.7 reshape.1076
  102.5 5.5 %all-to-all-start.4 = ((s32[16,1,2]{2,1,0:T(1,128)}), s32[16,1,2]{2,1,0:T(1,128)S(1)}, u32[]{:S(2)}, u32[]{:S(2)}) async-start(s32[16,1,2]{2,1,0:T(1,128)} %bitcast.17), calls=%async_computation.4 | async-start | bytes 16384 | tf_op jit(solution)/shard_map/all_to_all | solution.py:68
  108.0 0.8 scatter_custom_fusion.2
  109.5 2.6 %all-to-all-done.4 = s32[16,1,2]{2,1,0:T(1,128)S(1)} async-done(((s32[16,1,2]{2,1,0:T(1,128)}), s32[16,1,2]{2,1,0:T(1,128)S(1)}, u32[]{:S(2)}, u32[]{:S(2)}) %all-to-all-start.4) | async-done | bytes 160 | tf_op jit(solution)/shard_map/all_to_all | solution.py:68
  112.0 3.3 %all-to-all-start.2 = ((s32[8,1,2]{2,1,0:T(1,128)}), s32[8,1,2]{2,1,0:T(1,128)S(1)}, u32[]{:S(2)}, u32[]{:S(2)}) async-start(s32[8,1,2]{2,1,0:T(1,128)} %bitcast.15), calls=%async_computation.2 | async-start | bytes 8192 | tf_op jit(solution)/shard_map/all_to_all | solution.py:61
  115.4 7.4 %all-to-all-done.2 = s32[8,1,2]{2,1,0:T(1,128)S(1)} async-done(((s32[8,1,2]{2,1,0:T(1,128)}), s32[8,1,2]{2,1,0:T(1,128)S(1)}, u32[]{:S(2)}, u32[]{:S(2)}) %all-to-all-start.2) | async-done | bytes 96 | tf_op jit(solution)/shard_map/all_to_all | solution.py:61
  123.5 6.2 %all-to-all-start.5 = ((s32[4,16,1,2]{1,3,2,0:T(2,128)}), s32[4,16,1,2]{1,3,2,0:T(2,128)S(1)}, u32[]{:S(2)}, u32[]{:S(2)}) async-start(s32[4,16,1,2]{1,3,2,0:T(2,128)} %broadcast_in_dim.131), calls=%async_computation.5 | async-start | bytes 8192 | tf_op jit(solution)/shard_map/all_to_all | solution.py:34
  129.9 7.6 %all-to-all-done.5 = s32[4,16,1,2]{1,3,2,0:T(2,128)S(1)} async-done(((s32[4,16,1,2]{1,3,2,0:T(2,128)}), s32[4,16,1,2]{1,3,2,0:T(2,128)S(1)}, u32[]{:S(2)}, u32[]{:S(2)}) %all-to-all-start.5) | async-done | bytes 544 | tf_op jit(solution)/shard_map/all_to_all | solution.py:34
  138.1 5.9 %all-to-all-start.3 = ((s32[16,8,1,2]{1,3,2,0:T(2,128)}), s32[16,8,1,2]{1,3,2,0:T(2,128)S(1)}, u32[]{:S(2)}, u32[]{:S(2)}) async-start(s32[16,8,1,2]{1,3,2,0:T(2,128)} %broadcast_in_dim.127), calls=%async_computation.3 | async-start | bytes 32768 | tf_op jit(solution)/shard_map/all_to_all | solution.py:34
  144.5 4.7 %all-to-all-done.3 = s32[16,8,1,2]{1,3,2,0:T(2,128)S(1)} async-done(((s32[16,8,1,2]{1,3,2,0:T(2,128)}), s32[16,8,1,2]{1,3,2,0:T(2,128)S(1)}, u32[]{:S(2)}, u32[]{:S(2)}) %all-to-all-start.3) | async-done | bytes 1056 | tf_op jit(solution)/shard_map/all_to_all | solution.py:34
  149.5 0.8 gather_fusion.1
  152.5 4.4 %gather_fusion = bf16[64,128,128]{2,1,0:T(8,128)(2,1)S(1)} fusion(bf16[256,128,128]{2,1,0:T(8,128)(2,1)} %bitcast.105, s32[1024]{0:T(1024)S(1)} %pad_clamp_fusion.3), kind=kCustom, calls=%fused_computation | custom fusion | bytes 4194560 | tf_op jit(solution)/shard_map/jit(_take)/gather | solution.py:97
  156.9 30.5 %all-gather.7.cloned.1.call-done = bf16[64,1,2,128,128]{4,3,2,1,0:T(8,128)(2,1)} async-done(((bf16[16,1,2,128,128]{4,3,2,1,0:T(8,128)(2,1)}), bf16[64,1,2,128,128]{4,3,2,1,0:T(8,128)(2,1)}) %all-gather.7.cloned.1.call-update) | async-done | bytes 4194320 | tf_op jit(solution)/shard_map/all_gather | solution.py:85
  187.4 4.4 %gather_fusion.3 = bf16[64,128,128]{2,1,0:T(8,128)(2,1)} fusion(bf16[128,128,128]{2,1,0:T(8,128)(2,1)} %bitcast.104, s32[1024]{0:T(1024)S(1)} %pad_clamp_fusion), kind=kCustom, calls=%fused_computation.3 | custom fusion | bytes 4194560 | tf_op jit(solution)/shard_map/jit(_take)/gather | solution.py:109
  191.7 3.7 %fusion.7 = f32[1,1,32,128,128]{4,3,2,1,0:T(8,128)} fusion(bf16[32,2,128,128]{3,2,1,0:T(8,128)(2,1)} %bitcast.101, pred[32,2]{1,0:T(8,128)(4,1)S(1)} %copy.52, pred[32,2]{1,0:T(8,128)(4,1)S(1)} %get-tuple-element.9, bf16[32,2,128,128]{3,2,1,0:T(8,128)(2,1)S(1)} %bitcast.100, pred[32,2]{1,0:T(8,128)(4,1)S(1)} %copy.38), kind=kOutput, calls=%fused_computation.15 | convolution fusion | flops 271581184 | bytes 6291648 | tf_op jit(solution)/shard_map/pqab,pqbc->pac/dot_general | solution.py:116
  195.4 44.0 %reduce-scatter.2.cloned.1.call-done = f32[1,1,4,128,128]{4,3,2,1,0:T(8,128)} async-done(((f32[1,1,32,128,128]{4,3,2,1,0:T(8,128)}), f32[1,1,4,128,128]{4,3,2,1,0:T(8,128)}) %reduce-scatter.2.cloned.1.call-update) | async-done | bytes 262160 | tf_op jit(solution)/shard_map/reduce_scatter | solution.py:119
  239.4 1.7 log-plus-one_convert_fusion
  (60 shorter events, 6.9 us)
Async XLA Ops:
  6.5 94.5 %all-gather.5.cloned.1.call-start = ((), (), s32[]{:S(2)}) async-start(), calls=%async_computation.8 | async-start | bytes 8912896 | tf_op jit(solution)/shard_map/all_gather | solution.py:71
  9.3 30.1 %copy-start = (bf16[1,1,16,128,128]{4,3,2,1,0:T(8,128)(2,1)S(1)}, bf16[1,1,16,128,128]{4,3,2,1,0:T(8,128)(2,1)}, u32[]{:S(2)}) copy-start(bf16[1,1,16,128,128]{4,3,2,1,0:T(8,128)(2,1)} %param.4) | copy-start | bytes 1572868
  39.1 148.3 %all-gather.7.cloned.1.call-start = ((), (), s32[]{:S(2)}) async-start(), calls=%async_computation.9 | async-start | bytes 5242880 | tf_op jit(solution)/shard_map/all_gather | solution.py:85
  39.4 68.6 %copy-start.1 = (s32[1,1,32,2]{2,3,1,0:T(2,128)S(1)}, s32[1,1,32,2]{2,3,1,0:T(2,128)}, u32[]{:S(2)}) copy-start(s32[1,1,32,2]{2,3,1,0:T(2,128)} %param.7) | copy-start | bytes 772
  102.5 9.5 %all-to-all-start.4 = ((s32[16,1,2]{2,1,0:T(1,128)}), s32[16,1,2]{2,1,0:T(1,128)S(1)}, u32[]{:S(2)}, u32[]{:S(2)}) async-start(s32[16,1,2]{2,1,0:T(1,128)} %bitcast.17), calls=%async_computation.4 | async-start | bytes 16384 | tf_op jit(solution)/shard_map/all_to_all | solution.py:68
  112.0 10.8 %all-to-all-start.2 = ((s32[8,1,2]{2,1,0:T(1,128)}), s32[8,1,2]{2,1,0:T(1,128)S(1)}, u32[]{:S(2)}, u32[]{:S(2)}) async-start(s32[8,1,2]{2,1,0:T(1,128)} %bitcast.15), calls=%async_computation.2 | async-start | bytes 8192 | tf_op jit(solution)/shard_map/all_to_all | solution.py:61
  123.5 14.0 %all-to-all-start.5 = ((s32[4,16,1,2]{1,3,2,0:T(2,128)}), s32[4,16,1,2]{1,3,2,0:T(2,128)S(1)}, u32[]{:S(2)}, u32[]{:S(2)}) async-start(s32[4,16,1,2]{1,3,2,0:T(2,128)} %broadcast_in_dim.131), calls=%async_computation.5 | async-start | bytes 8192 | tf_op jit(solution)/shard_map/all_to_all | solution.py:34
  138.1 11.1 %all-to-all-start.3 = ((s32[16,8,1,2]{1,3,2,0:T(2,128)}), s32[16,8,1,2]{1,3,2,0:T(2,128)S(1)}, u32[]{:S(2)}, u32[]{:S(2)}) async-start(s32[16,8,1,2]{1,3,2,0:T(2,128)} %broadcast_in_dim.127), calls=%async_computation.3 | async-start | bytes 32768 | tf_op jit(solution)/shard_map/all_to_all | solution.py:34
  143.9 95.5 %reduce-scatter.2.cloned.1.call-start = ((), (), s32[]{:S(2)}) async-start(), calls=%async_computation.7 | async-start | bytes 2359296 | tf_op jit(solution)/shard_map/reduce_scatter | solution.py:119
Sparse Core Ops, SparseCore 0:
  39.2 61.7 all-gather.4
  103.1 84.2 all-gather.6
  195.5 43.7 reduce-scatter.1

commit v12 on v6

--- a/solution.py
+++ b/solution.py
@@ -34,16 +34,6 @@
     return codes[..., 0, :] * ID_BASE + codes[..., 1, :]
 
 
-def unpack_blocks(payload, capacity, block_size):
-    blocks = payload[..., : capacity * block_size, :]
-    return blocks.reshape(-1, block_size, block_size)
-
-
-def gather_by_exchange(x, axis, size):
-    copies = jnp.broadcast_to(x[None], (size,) + x.shape)
-    return lax.all_to_all(copies, axis, split_axis=0, concat_axis=0, tiled=True)
-
-
 def body(block_values, block_cols, live_count, out_pattern):
     depths = lax.axis_size("depth")
     columns = lax.axis_size("col")
@@ -62,37 +52,41 @@
 
     left = pack_slots(values, col_ids, col_ids // group_rows % depths, is_live, depths, cap_left)
     left = lax.all_to_all(left, "depth", split_axis=0, concat_axis=0, tiled=True)
-    left = lax.all_gather(left[None], "col", axis=0, tiled=True)
     right = pack_slots(values, col_ids, col_ids // col_block, is_live, columns, cap_right)
     right = lax.all_to_all(right, "col", split_axis=0, concat_axis=0, tiled=True)
-    right = gather_by_exchange(right, "row", row_groups)
+    left = lax.all_gather(left[None], "col", axis=0, tiled=True)
+    right, left = lax.optimization_barrier((right, left))
+    right = lax.all_gather(right[None], "row", axis=0, tiled=True)
 
-    left_ids = unpack_ids(left, cap_left, block_size).reshape(-1)
-    right_ids = unpack_ids(right, cap_right, block_size).reshape(-1, cap_right)
-    left_flat = unpack_blocks(left, cap_left, block_size)
-    right_flat = unpack_blocks(right, cap_right, block_size)
+    payload_rows = left.shape[-2]
+    left_rows = left.reshape(-1, payload_rows, block_size)
+    right_rows = right.reshape(-1, payload_rows, block_size)
 
     pattern_rows = out_pattern[0, 0, :, 0]
     pattern_cols = out_pattern[0, 0, :, 1]
     pattern_len = pattern_rows.shape[0]
     local_row = pattern_rows - row_index * plane_rows
     left_pos = (local_row % group_rows) * depths + local_row // group_rows
-    left_sel = left_pos[:, None] * cap_left + jnp.arange(cap_left, dtype=jnp.int32)[None, :]
-    left_pick = jnp.take(left_flat, left_sel.reshape(-1), axis=0)
-    inner = jnp.take(left_ids, left_sel, axis=0)
+    left_picked = jnp.take(left_rows, left_pos, axis=0)
+    inner = unpack_ids(left_picked, cap_left, block_size)
+    left_pick = left_picked[:, : cap_left * block_size, :].reshape(
+        pattern_len, cap_left, block_size, block_size
+    )
+
+    right_ids = unpack_ids(right_rows, cap_right, block_size)
     safe_inner = jnp.maximum(inner, 0)
     right_row = safe_inner // plane_rows * columns + safe_inner % group_rows
     right_here = jnp.take(right_ids, right_row, axis=0)
     matched = (right_here == pattern_cols[:, None, None]) & (inner >= 0)[:, :, None]
-    slot = jnp.sum(
-        jnp.where(matched, jnp.arange(cap_right, dtype=jnp.int32)[None, None, :], 0), axis=2
-    )
     found = jnp.any(matched, axis=2)
-    right_pick = jnp.take(right_flat, (right_row * cap_right + slot).reshape(-1), axis=0)
+    second = matched[:, :, 1]
+    right_picked = jnp.take(right_rows, right_row.reshape(-1), axis=0)
+    first_block = right_picked[:, :block_size, :]
+    second_block = right_picked[:, block_size : 2 * block_size, :]
+    right_pick = jnp.where(second.reshape(-1)[:, None, None], second_block, first_block)
     right_pick = jnp.where(
         found.reshape(-1)[:, None, None], right_pick, jnp.zeros_like(right_pick)
     )
-    left_pick = left_pick.reshape(pattern_len, cap_left, block_size, block_size)
     right_pick = right_pick.reshape(pattern_len, cap_left, block_size, block_size)
     partial_sum = jnp.einsum(
         "pqab,pqbc->pac", left_pick, right_pick, preferred_element_type=jnp.float32

time: 281 us -> 275 us (0.979)
  waiting for transfers between devices: 158 us -> 128 us
  local copies, waits for them, and re-layouts: 33.6 us -> 53.5 us
  other arithmetic: 5.46 us -> 17.6 us
  starting transfers between devices: 6.79 us -> 0.08 us
    all_to_all x1 -> x0, waiting for transfers between devices: 108 us -> none  [gather_by_exchange(): return lax.all_to_all(copies, axis, split_axis=0, concat_axis=0, tiled=True)]
    all_gather x0 -> x1, waiting for transfers between devices: none -> 49.1 us  [body(): right = lax.all_gather(right[None], 'row', axis=0, tiled=True)]
    all_gather x1, waiting for transfers between devices: 0.01 us -> 33.3 us  [body(): left = lax.all_gather(left[None], 'col', axis=0, tiled=True)]
    select_n x2 -> x5, other arithmetic: 0.09 us -> 12.9 us  [the longest x2 8.54 us: body(): left_picked = jnp.take(left_rows, left_pos, axis=0)]
    gather x6 -> x3, local copies, waits for them, and re-layouts: 9.76 us -> 18.6 us  [the longest x2 11.7 us: body(): left_picked = jnp.take(left_rows, left_pos, axis=0)]
    all_gather x0 -> x1, local copies, waits for them, and re-layouts: none -> 7.91 us  [body(): right = lax.all_gather(right[None], 'row', axis=0, tiled=True)]
    reshape x0 -> x1, local copies, waits for them, and re-layouts: none -> 7.59 us  [body(): left_picked[:, :cap_left * block_size, :]]
    all_to_all x1 -> x0, starting transfers between devices: 6.79 us -> none  [gather_by_exchange(): return lax.all_to_all(copies, axis, split_axis=0, concat_axis=0, tiled=True)]
  transfers between devices with their start and end apart: 3 -> 3, of which waited for: 2 -> 3; matrix products, arithmetic and copies ran while one was open for 4% -> 16% of each run, Pallas kernels for 0% -> 0%
where the time goes in v12:
time: 275 us; the launch traced here: 274 us
  waiting for transfers between devices  128 us (47%)
  blocking collectives  58.8 us (21%)
  local copies, waits for them, and re-layouts  53.5 us (19%)
  other arithmetic  17.6 us (6%)
  between operations  14.1 us (5%)
    all_gather x1, waiting for transfers between devices, body(): right = lax.all_gather(right[None], 'row', axis=0, tiled=True)  49.1 us
    reduce_scatter x1, waiting for transfers between devices, body(): lax.psum_scatter(partial_sum[None, None], 'depth', scatter_dimension=2, t...  45.1 us
    all_gather x1, waiting for transfers between devices, body(): left = lax.all_gather(left[None], 'col', axis=0, tiled=True)  33.3 us
    all_to_all x1, blocking collectives, body(): lax.all_to_all(right, 'col', split_axis=0, concat_axis=0, tiled=True)  30.3 us
    all_to_all x1, blocking collectives, body(): lax.all_to_all(left, 'depth', split_axis=0, concat_axis=0, tiled=True)  28.5 us
    gather x2, local copies, waits for them, and re-layouts, body(): left_picked = jnp.take(left_rows, left_pos, axis=0)  11.7 us
    slice x1, local copies, waits for them, and re-layouts, body(): left_picked[:, :cap_left * block_size, :]  10.4 us
    select_n x2, other arithmetic, body(): left_picked = jnp.take(left_rows, left_pos, axis=0)  8.54 us
  transfers between devices with their start and end apart: 3, of which 3 were waited for; matrix products, arithmetic and copies ran while one was open for 16% of the time, Pallas kernels for 0%

profile of v12, /device:TPU:6, one launch (start us, length us, event | category | flops | bytes accessed | tf_op | source)
XLA Modules:
  0.0 273.7 jit_solution(17484699621517388225)
XLA Ops:
  7.2 0.7 and_select_fusion.7
  8.5 0.7 fusion.28
  9.2 0.8 scatter_custom_fusion.3
  10.2 2.1 scatter_fusion.1
  12.4 28.5 %all_to_all.10 = bf16[8,272,128]{2,1,0:T(8,128)(2,1)} all-to-all(bf16[8,272,128]{2,1,0:T(8,128)(2,1)S(1)} %fusion.4), channel_id=1, replica_groups=mesh['row'=4,'col'=16,'depth'=8] {'depth'}, dimensions={0} | all-to-all | bytes 1114112 | tf_op jit(solution)/shard_map/all_to_all | solution.py:54
  41.0 0.8 scatter_custom_fusion.1
  42.2 1.1 scatter_fusion
  43.5 30.3 %all_to_all.11 = bf16[16,272,128]{2,1,0:T(8,128)(2,1)} all-to-all(bf16[16,272,128]{2,1,0:T(8,128)(2,1)S(1)} %fusion.2), channel_id=1, replica_groups=mesh['row'=4,'col'=16,'depth'=8] {'col'}, dimensions={0} | all-to-all | bytes 2228224 | tf_op jit(solution)/shard_map/all_to_all | solution.py:56
  73.8 33.3 %all-gather.5.cloned.1.call-done = bf16[128,272,128]{2,1,0:T(8,128)(2,1)} async-done(((bf16[8,272,128]{2,1,0:T(8,128)(2,1)}), bf16[128,272,128]{2,1,0:T(8,128)(2,1)}) %all-gather.5.cloned.1.call-update) | async-done | bytes 8912912 | tf_op jit(solution)/shard_map/all_gather | solution.py:57
  107.3 4.5 %gather_fusion = bf16[32,272,128]{2,1,0:T(8,128)(2,1)S(1)} fusion(bf16[128,272,128]{2,1,0:T(8,128)(2,1)} %all-gather.5.cloned.1.call-done, s32[1024]{0:T(1024)S(1)} %pad_clamp_fusion.2), kind=kCustom, calls=%fused_computation | custom fusion | bytes 4456576 | tf_op jit(solution)/shard_map/jit(_take)/gather | solution.py:70
  111.8 7.2 %copy.81 = bf16[32,272,128]{0,2,1:T(8,128)(2,1)} copy(bf16[32,272,128]{2,1,0:T(8,128)(2,1)S(1)} %gather_fusion) | data formatting | bytes 4456448 | tf_op jit(solution)/shard_map/jit(_take)/gather | solution.py:70
  119.0 8.5 %broadcast_select_fusion = bf16[32,272,128]{0,2,1:T(8,128)(2,1)} fusion(bf16[32,272,128]{0,2,1:T(8,128)(2,1)} %copy.81, pred[32]{0:T(512)(128)(4,1)S(1)} %compare_and_fusion.3), kind=kLoop, calls=%fused_computation.7 | loop fusion | flops 1114112 | bytes 4456480 | tf_op jit(solution)/shard_map/jit(_take)/select_n | solution.py:70
  127.5 0.7 slice_convert_fusion
  129.2 10.4 %slice.104 = bf16[32,256,128]{0,2,1:T(8,128)(2,1)} slice(bf16[32,272,128]{0,2,1:T(8,128)(2,1)} %broadcast_select_fusion), slice={[0:32], [0:256], [0:128]} | slice | bytes 4194304 | tf_op jit(solution)/shard_map/slice | solution.py:72
  140.0 7.6 %copy.96 = bf16[32,2,128,128]{3,2,1,0:T(8,128)(2,1)S(1)} copy(bf16[32,2,128,128]{0,3,2,1:T(8,128)(2,1)} %bitcast.145) | data formatting | bytes 4194304 | tf_op jit(solution)/shard_map/reshape | solution.py:72
  147.7 49.1 %all-gather.7.cloned.1.call-done = bf16[64,272,128]{2,1,0:T(8,128)(2,1)} async-done(((bf16[16,272,128]{2,1,0:T(8,128)(2,1)}), bf16[64,272,128]{2,1,0:T(8,128)(2,1)}) %all-gather.7.cloned.1.call-update) | async-done | bytes 4456464 | tf_op jit(solution)/shard_map/all_gather | solution.py:59
  196.8 0.9 slice.108
  199.2 7.9 %copy.94 = bf16[64,272,128]{1,2,0:T(8,128)(2,1)} copy(bf16[64,272,128]{2,1,0:T(8,128)(2,1)} %all-gather.7.cloned.1.call-done) | data formatting | bytes 8912896 | tf_op jit(solution)/shard_map/all_gather | solution.py:59
  207.1 6.9 %gather_fusion.2 = bf16[64,272,128]{1,2,0:T(8,128)(2,1)} fusion(bf16[64,272,128]{1,2,0:T(8,128)(2,1)} %copy.94, s32[1024]{0:T(1024)S(1)} %pad_clamp_fusion), kind=kCustom, calls=%fused_computation.2 | custom fusion | bytes 8913152 | tf_op jit(solution)/shard_map/jit(_take)/gather | solution.py:83
  214.0 3.6 %broadcast_select_fusion.1 = bf16[64,272,128]{1,2,0:T(8,128)(2,1)S(1)} fusion(bf16[64,272,128]{1,2,0:T(8,128)(2,1)} %gather_fusion.2, pred[64]{0:T(512)(128)(4,1)S(1)} %compare_and_fusion.1), kind=kLoop, calls=%fused_computation.8 | loop fusion | flops 2228224 | bytes 8912960 | tf_op jit(solution)/shard_map/jit(_take)/select_n | solution.py:83
  217.5 0.8 fusion.1
  218.3 2.1 convolution_bitcast_fusion
  220.4 45.1 %reduce-scatter.2.cloned.1.call-done = f32[1,1,4,128,128]{4,3,2,1,0:T(8,128)} async-done(((f32[1,1,32,128,128]{4,3,2,1,0:T(8,128)}), f32[1,1,4,128,128]{4,3,2,1,0:T(8,128)}) %reduce-scatter.2.cloned.1.call-update) | async-done | bytes 262160 | tf_op jit(solution)/shard_map/reduce_scatter | solution.py:94
  265.4 1.7 log-plus-one_convert_fusion
  (67 shorter events, 4.5 us)
Async XLA Ops:
  6.5 100.6 %all-gather.5.cloned.1.call-start = ((), (), s32[]{:S(2)}) async-start(), calls=%async_computation.4 | async-start | bytes 9469952 | tf_op jit(solution)/shard_map/all_gather | solution.py:57
  12.3 29.9 %copy-start = (bf16[1,1,16,128,128]{4,3,2,1,0:T(8,128)(2,1)S(1)}, bf16[1,1,16,128,128]{4,3,2,1,0:T(8,128)(2,1)}, u32[]{:S(2)}) copy-start(bf16[1,1,16,128,128]{4,3,2,1,0:T(8,128)(2,1)} %param.8) | copy-start | bytes 1572868
  41.0 155.9 %all-gather.7.cloned.1.call-start = ((), (), s32[]{:S(2)}) async-start(), calls=%async_computation.5 | async-start | bytes 5570560 | tf_op jit(solution)/shard_map/all_gather | solution.py:59
  43.4 63.8 %copy-start.1 = (s32[1,1,32,2]{2,3,1,0:T(2,128)S(1)}, s32[1,1,32,2]{2,3,1,0:T(2,128)}, u32[]{:S(2)}) copy-start(s32[1,1,32,2]{2,3,1,0:T(2,128)} %param.11) | copy-start | bytes 772
  107.2 158.3 %reduce-scatter.2.cloned.1.call-start = ((), (), s32[]{:S(2)}) async-start(), calls=%async_computation.3 | async-start | bytes 2359296 | tf_op jit(solution)/shard_map/reduce_scatter | solution.py:94
Sparse Core Ops, SparseCore 0:
  41.1 66.0 all-gather.4
  109.3 87.4 all-gather.6
  220.5 44.8 reduce-scatter.1

commit v13 on v8

--- a/solution.py
+++ b/solution.py
@@ -3,6 +3,8 @@
 import jax
 import jax.numpy as jnp
 from jax import lax
+from jax.experimental import pallas as pl
+from jax.experimental.pallas import tpu as pltpu
 from jax.sharding import PartitionSpec as P
 
 
@@ -32,6 +34,48 @@
 def gather_by_exchange(x, axis, size):
     copies = jnp.broadcast_to(x[None], (size,) + x.shape)
     return lax.all_to_all(copies, axis, split_axis=0, concat_axis=0, tiled=True)
+
+
+def pair_kernel(right_index, found, left_ref, right_hbm, out_ref, right_buf, sems):
+    count = right_buf.shape[0]
+    copies = [
+        pltpu.make_async_copy(right_hbm.at[right_index[t]], right_buf.at[t], sems.at[t])
+        for t in range(count)
+    ]
+    for copy in copies:
+        copy.start()
+    for copy in copies:
+        copy.wait()
+    for p in range(count // 2):
+        total = jnp.zeros(out_ref.shape[1:], jnp.float32)
+        for t in (2 * p, 2 * p + 1):
+            term = jnp.dot(left_ref[t], right_buf[t], preferred_element_type=jnp.float32)
+            total = total + jnp.where(found[t] != 0, term, 0.0)
+        out_ref[p] = total
+
+
+def pair_products(right_index, found, left_pick, right_flat):
+    count, block_size, _ = left_pick.shape
+    return pl.pallas_call(
+        pair_kernel,
+        out_shape=jax.ShapeDtypeStruct((count // 2, block_size, block_size), jnp.float32),
+        in_specs=[
+            pl.BlockSpec(memory_space=pltpu.SMEM),
+            pl.BlockSpec(memory_space=pltpu.SMEM),
+            pl.BlockSpec(memory_space=pltpu.VMEM),
+            pl.BlockSpec(memory_space=pl.ANY),
+        ],
+        out_specs=pl.BlockSpec(memory_space=pltpu.VMEM),
+        scratch_shapes=[
+            pltpu.VMEM((count, block_size, block_size), right_flat.dtype),
+            pltpu.SemaphoreType.DMA((count,)),
+        ],
+        cost_estimate=pl.CostEstimate(
+            flops=2 * count * block_size**3,
+            bytes_accessed=count * block_size * block_size * 2 * 2 + count * block_size * block_size * 2,
+            transcendentals=0,
+        ),
+    )(right_index, found, left_pick, right_flat)
 
 
 def body(block_values, block_cols, live_count, out_pattern):
@@ -105,16 +149,13 @@
         jnp.where(matched, jnp.arange(cap_right, dtype=jnp.int32)[None, None, :], 0), axis=2
     )
     found = jnp.any(matched, axis=2)
-    right_pick = jnp.take(right_flat, (right_row * cap_right + slot).reshape(-1), axis=0)
-    right_pick = jnp.where(
-        found.reshape(-1)[:, None, None], right_pick, jnp.zeros_like(right_pick)
-    )
     pattern_len = pattern_rows.shape[0]
-    left_pick = left_pick.reshape(pattern_len, cap_left, block_size, block_size)
-    right_pick = right_pick.reshape(pattern_len, cap_left, block_size, block_size)
-    partial_sum = jnp.einsum(
-        "pqab,pqbc->pac", left_pick, right_pick, preferred_element_type=jnp.float32
-    )
+    partial_sum = pair_products(
+        (right_row * cap_right + slot).reshape(-1),
+        found.reshape(-1).astype(jnp.int32),
+        left_pick,
+        right_flat,
+    ).reshape(pattern_len, block_size, block_size)
     share = lax.psum_scatter(partial_sum[None, None], "depth", scatter_dimension=2, tiled=True)
     return jnp.log1p(share).astype(jnp.bfloat16)
 

time: 248 us -> 247 us (level)
  waiting for transfers between devices: 136 us -> 126 us
  blocking collectives: 48.3 us -> 54.5 us
  Pallas kernels: 0 us -> 5.86 us
  local copies, waits for them, and re-layouts: 20.1 us -> 16.3 us
  matrix products: 3.74 us -> 0 us
    all_gather x1, waiting for transfers between devices: 55.7 us -> 0.01 us  [body(): lax.all_gather(left_vals[None], 'col', axis=0, tiled=True)]
    all_gather x1, waiting for transfers between devices: 11.8 us -> 60 us  [body(): lax.all_gather(right_vals[None], 'row', axis=0, tiled=True)]
    pallas_call x0 -> x1, Pallas kernels: none -> 5.86 us  [pair_products(): pl.pallas_call(pair_kernel, out_shape=jax.ShapeDtypeStruct((count // 2, b...]
    dot_general x1 -> x0, matrix products: 3.74 us -> none  [body(): jnp.einsum('pqab,pqbc->pac', left_pick, right_pick, preferred_element_typ...]
    all_to_all x1, blocking collectives: 23.5 us -> 26.8 us  [body(): lax.all_to_all(right_vals, 'col', split_axis=0, concat_axis=0, tiled=True)]
    gather x1 -> x0, local copies, waits for them, and re-layouts: 3.14 us -> none  [body(): jnp.take(right_flat, (right_row * cap_right + slot).reshape(-1), axis=0)]
    all_to_all x1, blocking collectives: 24.9 us -> 27.7 us  [body(): lax.all_to_all(left_vals, 'depth', split_axis=0, concat_axis=0, tiled=True)]
    all_to_all x1, starting transfers between devices: 4.77 us -> 7.39 us  [body(): lax.all_to_all(right_cols, 'col', split_axis=0, concat_axis=0, tiled=True)]
  transfers between devices with their start and end apart: 7 -> 7, of which waited for: 7 -> 6; matrix products, arithmetic and copies ran while one was open for 5% -> 7% of each run, Pallas kernels for 0% -> 0%
where the time goes in v13:
time: 247 us; the launch traced here: 246 us
  waiting for transfers between devices  126 us (51%)
  blocking collectives  54.5 us (22%)
  starting transfers between devices  22.7 us (9%)
  local copies, waits for them, and re-layouts  16.3 us (7%)
  between operations  14 us (6%)
  other arithmetic  6.13 us (2%)
  Pallas kernels  5.86 us (2%)
    all_gather x1, waiting for transfers between devices, body(): lax.all_gather(right_vals[None], 'row', axis=0, tiled=True)  60 us
    reduce_scatter x1, waiting for transfers between devices, body(): lax.psum_scatter(partial_sum[None, None], 'depth', scatter_dimension=2, t...  45.3 us
    all_to_all x1, blocking collectives, body(): lax.all_to_all(left_vals, 'depth', split_axis=0, concat_axis=0, tiled=True)  27.7 us
    all_to_all x1, blocking collectives, body(): lax.all_to_all(right_vals, 'col', split_axis=0, concat_axis=0, tiled=True)  26.8 us
    all_to_all x2, starting transfers between devices, gather_by_exchange(): return lax.all_to_all(copies, axis, split_axis=0, concat_axis=0, tiled=True)  12 us
    all_to_all x2, waiting for transfers between devices, gather_by_exchange(): return lax.all_to_all(copies, axis, split_axis=0, concat_axis=0, tiled=True)  11.4 us
    all_to_all x1, waiting for transfers between devices, body(): lax.all_to_all(left_cols, 'depth', split_axis=0, concat_axis=0, tiled=True)  7.5 us
    all_to_all x1, starting transfers between devices, body(): lax.all_to_all(right_cols, 'col', split_axis=0, concat_axis=0, tiled=True)  7.39 us
  transfers between devices with their start and end apart: 7, of which 6 were waited for; matrix products, arithmetic and copies ran while one was open for 7% of the time, Pallas kernels for 0%

profile of v13, /device:TPU:6, one launch (start us, length us, event | category | flops | bytes accessed | tf_op | source)
XLA Modules:
  0.0 245.7 jit_solution(18006394432052217039)
XLA Ops:
  8.5 0.7 fusion.17
  9.3 2.1 scatter_fusion
  11.4 27.7 %all_to_all.30 = bf16[8,1,2,128,128]{4,3,2,1,0:T(8,128)(2,1)} all-to-all(bf16[8,1,2,128,128]{4,3,2,1,0:T(8,128)(2,1)S(1)} %bitcast.86), channel_id=1, replica_groups=mesh['row'=4,'col'=16,'depth'=8] {'depth'}, dimensions={0} | all-to-all | bytes 1048576 | tf_op jit(solution)/shard_map/all_to_all | solution.py:104
  39.4 1.2 scatter_fusion.1
  40.6 26.8 %all_to_all.31 = bf16[16,1,2,128,128]{4,3,2,1,0:T(8,128)(2,1)} all-to-all(bf16[16,1,2,128,128]{4,3,2,1,0:T(8,128)(2,1)S(1)} %bitcast.85), channel_id=1, replica_groups=mesh['row'=4,'col'=16,'depth'=8] {'col'}, dimensions={0} | all-to-all | bytes 2097152 | tf_op jit(solution)/shard_map/all_to_all | solution.py:124
  67.4 0.8 scatter_custom_fusion.1
  68.2 0.7 reshape.937
  68.8 7.4 %all-to-all-start.2 = ((s32[16,1,2]{2,1,0:T(1,128)}), s32[16,1,2]{2,1,0:T(1,128)S(1)}, u32[]{:S(2)}, u32[]{:S(2)}) async-start(s32[16,1,2]{2,1,0:T(1,128)} %bitcast.10), calls=%async_computation.2 | async-start | bytes 16384 | tf_op jit(solution)/shard_map/all_to_all | solution.py:125
  76.7 0.8 scatter_custom_fusion
  77.4 0.7 reshape.935
  78.3 2.0 all-to-all-done.2
  80.3 3.3 %all-to-all-start = ((s32[8,1,2]{2,1,0:T(1,128)}), s32[8,1,2]{2,1,0:T(1,128)S(1)}, u32[]{:S(2)}, u32[]{:S(2)}) async-start(s32[8,1,2]{2,1,0:T(1,128)} %bitcast.6), calls=%async_computation | async-start | bytes 8192 | tf_op jit(solution)/shard_map/all_to_all | solution.py:105
  83.7 7.5 %all-to-all-done = s32[8,1,2]{2,1,0:T(1,128)S(1)} async-done(((s32[8,1,2]{2,1,0:T(1,128)}), s32[8,1,2]{2,1,0:T(1,128)S(1)}, u32[]{:S(2)}, u32[]{:S(2)}) %all-to-all-start) | async-done | bytes 96 | tf_op jit(solution)/shard_map/all_to_all | solution.py:105
  91.7 6.6 %all-to-all-start.3 = ((s32[4,16,1,2]{1,3,2,0:T(2,128)}), s32[4,16,1,2]{1,3,2,0:T(2,128)S(1)}, u32[]{:S(2)}, u32[]{:S(2)}) async-start(s32[4,16,1,2]{1,3,2,0:T(2,128)} %broadcast_in_dim.108), calls=%async_computation.3 | async-start | bytes 8192 | tf_op jit(solution)/shard_map/all_to_all | solution.py:36
  98.5 7.5 %all-to-all-done.3 = s32[4,16,1,2]{1,3,2,0:T(2,128)S(1)} async-done(((s32[4,16,1,2]{1,3,2,0:T(2,128)}), s32[4,16,1,2]{1,3,2,0:T(2,128)S(1)}, u32[]{:S(2)}, u32[]{:S(2)}) %all-to-all-start.3) | async-done | bytes 544 | tf_op jit(solution)/shard_map/all_to_all | solution.py:36
  106.7 5.4 %all-to-all-start.1 = ((s32[16,8,1,2]{1,3,2,0:T(2,128)}), s32[16,8,1,2]{1,3,2,0:T(2,128)S(1)}, u32[]{:S(2)}, u32[]{:S(2)}) async-start(s32[16,8,1,2]{1,3,2,0:T(2,128)} %broadcast_in_dim.102), calls=%async_computation.1 | async-start | bytes 32768 | tf_op jit(solution)/shard_map/all_to_all | solution.py:36
  112.3 3.9 %all-to-all-done.1 = s32[16,8,1,2]{1,3,2,0:T(2,128)S(1)} async-done(((s32[16,8,1,2]{1,3,2,0:T(2,128)}), s32[16,8,1,2]{1,3,2,0:T(2,128)S(1)}, u32[]{:S(2)}, u32[]{:S(2)}) %all-to-all-start.1) | async-done | bytes 1056 | tf_op jit(solution)/shard_map/all_to_all | solution.py:36
  116.5 0.8 gather_fusion
  120.4 4.3 %gather_fusion.2 = bf16[64,128,128]{2,1,0:T(8,128)(2,1)S(1)} fusion(bf16[256,128,128]{2,1,0:T(8,128)(2,1)} %bitcast.91, s32[1024]{0:T(1024)S(1)} %pad_clamp_fusion), kind=kCustom, calls=%fused_computation.2 | custom fusion | bytes 4194560 | tf_op jit(solution)/shard_map/jit(_take)/gather | solution.py:140
  124.7 1.6 broadcast_select_fusion.left_ref
  126.3 60.0 %all-gather.7.cloned.1.call-done = bf16[64,1,2,128,128]{4,3,2,1,0:T(8,128)(2,1)} async-done(((bf16[16,1,2,128,128]{4,3,2,1,0:T(8,128)(2,1)}), bf16[64,1,2,128,128]{4,3,2,1,0:T(8,128)(2,1)}) %all-gather.7.cloned.1.call-update) | async-done | bytes 4194320 | tf_op jit(solution)/shard_map/all_gather | solution.py:128
  186.3 5.9 %shard_map.46 = f32[32,128,128]{2,1,0:T(8,128)} custom-call(s32[64]{0:T(128)} %multiply_add_fusion.right_index, s32[64]{0:T(128)} %reshape.943.found, bf16[64,128,128]{2,1,0:T(8,128)(2,1)} %broadcast_select_fusion.left_ref, bf16[128,128,128]{2,1,0:T(8,128)(2,1)} %bitcast.87), custom_call_target="tpu_custom_call" | custom-call | flops 268435456 | bytes 6291456 | tf_op jit(solution)/shard_map/pallas_call | solution.py:59
  192.2 45.3 %reduce-scatter.2.cloned.1.call-done = f32[1,1,4,128,128]{4,3,2,1,0:T(8,128)} async-done(((f32[1,1,32,128,128]{4,3,2,1,0:T(8,128)}), f32[1,1,4,128,128]{4,3,2,1,0:T(8,128)}) %reduce-scatter.2.cloned.1.call-update) | async-done | bytes 262160 | tf_op jit(solution)/shard_map/reduce_scatter | solution.py:159
  237.5 1.7 log-plus-one_convert_fusion
  (63 shorter events, 7.3 us)
Async XLA Ops:
  6.5 113.8 %all-gather.5.cloned.1.call-start = ((), (), s32[]{:S(2)}) async-start(), calls=%async_computation.8 | async-start | bytes 8912896 | tf_op jit(solution)/shard_map/all_gather | solution.py:108
  9.3 30.1 %copy-start = (bf16[1,1,16,128,128]{4,3,2,1,0:T(8,128)(2,1)S(1)}, bf16[1,1,16,128,128]{4,3,2,1,0:T(8,128)(2,1)}, u32[]{:S(2)}) copy-start(bf16[1,1,16,128,128]{4,3,2,1,0:T(8,128)(2,1)} %param.4) | copy-start | bytes 1572868
  39.1 147.2 %all-gather.7.cloned.1.call-start = ((), (), s32[]{:S(2)}) async-start(), calls=%async_computation.9 | async-start | bytes 5242880 | tf_op jit(solution)/shard_map/all_gather | solution.py:128
  39.4 36.8 %copy-start.1 = (s32[1,1,32,2]{2,3,1,0:T(2,128)S(1)}, s32[1,1,32,2]{2,3,1,0:T(2,128)}, u32[]{:S(2)}) copy-start(s32[1,1,32,2]{2,3,1,0:T(2,128)} %param.7) | copy-start | bytes 772
  68.8 11.4 %all-to-all-start.2 = ((s32[16,1,2]{2,1,0:T(1,128)}), s32[16,1,2]{2,1,0:T(1,128)S(1)}, u32[]{:S(2)}, u32[]{:S(2)}) async-start(s32[16,1,2]{2,1,0:T(1,128)} %bitcast.10), calls=%async_computation.2 | async-start | bytes 16384 | tf_op jit(solution)/shard_map/all_to_all | solution.py:125
  80.3 10.9 %all-to-all-start = ((s32[8,1,2]{2,1,0:T(1,128)}), s32[8,1,2]{2,1,0:T(1,128)S(1)}, u32[]{:S(2)}, u32[]{:S(2)}) async-start(s32[8,1,2]{2,1,0:T(1,128)} %bitcast.6), calls=%async_computation | async-start | bytes 8192 | tf_op jit(solution)/shard_map/all_to_all | solution.py:105
  91.7 14.3 %all-to-all-start.3 = ((s32[4,16,1,2]{1,3,2,0:T(2,128)}), s32[4,16,1,2]{1,3,2,0:T(2,128)S(1)}, u32[]{:S(2)}, u32[]{:S(2)}) async-start(s32[4,16,1,2]{1,3,2,0:T(2,128)} %broadcast_in_dim.108), calls=%async_computation.3 | async-start | bytes 8192 | tf_op jit(solution)/shard_map/all_to_all | solution.py:36
  106.7 9.6 %all-to-all-start.1 = ((s32[16,8,1,2]{1,3,2,0:T(2,128)}), s32[16,8,1,2]{1,3,2,0:T(2,128)S(1)}, u32[]{:S(2)}, u32[]{:S(2)}) async-start(s32[16,8,1,2]{1,3,2,0:T(2,128)} %broadcast_in_dim.102), calls=%async_computation.1 | async-start | bytes 32768 | tf_op jit(solution)/shard_map/all_to_all | solution.py:36
  112.0 125.5 %reduce-scatter.2.cloned.1.call-start = ((), (), s32[]{:S(2)}) async-start(), calls=%async_computation.7 | async-start | bytes 2359296 | tf_op jit(solution)/shard_map/reduce_scatter | solution.py:159
Sparse Core Ops, SparseCore 0:
  39.2 61.8 all-gather.4
  103.2 83.0 all-gather.6
  192.3 45.1 reduce-scatter.1

commit v14 on v13

--- a/solution.py
+++ b/solution.py
@@ -104,10 +104,7 @@
         lax.all_to_all(left_vals, "depth", split_axis=0, concat_axis=0, tiled=True),
         lax.all_to_all(left_cols, "depth", split_axis=0, concat_axis=0, tiled=True),
     )
-    left_vals, left_cols = (
-        lax.all_gather(left_vals[None], "col", axis=0, tiled=True),
-        gather_by_exchange(left_cols, "col", columns),
-    )
+    left_vals = lax.all_gather(left_vals[None], "col", axis=0, tiled=True)
     left_shape = left_cols.shape
     source_col = lax.broadcasted_iota(jnp.int32, left_shape, 0)
     source_depth = lax.broadcasted_iota(jnp.int32, left_shape, 1)
@@ -120,10 +117,18 @@
     right_vals, right_cols = pack_slots(
         values, col_ids, col_ids // col_block, is_live, columns, cap_right
     )
-    right_vals, right_cols = (
-        lax.all_to_all(right_vals, "col", split_axis=0, concat_axis=0, tiled=True),
-        lax.all_to_all(right_cols, "col", split_axis=0, concat_axis=0, tiled=True),
+    right_vals = lax.all_to_all(right_vals, "col", split_axis=0, concat_axis=0, tiled=True)
+    left_width = left_cols.size
+    id_pack = jnp.concatenate(
+        [
+            jnp.broadcast_to(left_cols.reshape(1, -1), (columns, left_width)),
+            right_cols.reshape(columns, -1),
+        ],
+        axis=1,
     )
+    id_pack = lax.all_to_all(id_pack, "col", split_axis=0, concat_axis=0, tiled=True)
+    left_cols = id_pack[:, :left_width].reshape((columns,) + left_cols.shape)
+    right_cols = id_pack[:, left_width:].reshape(right_cols.shape)
     right_vals, right_cols = (
         lax.all_gather(right_vals[None], "row", axis=0, tiled=True),
         gather_by_exchange(right_cols, "row", row_groups),

time: 247 us -> 247 us (level)
  starting transfers between devices: 22.7 us -> 17.3 us
  waiting for transfers between devices: 126 us -> 131 us
    all_gather x1, waiting for transfers between devices: 60 us -> 68.2 us  [body(): lax.all_gather(right_vals[None], 'row', axis=0, tiled=True)]
    all_to_all x2 -> x1, starting transfers between devices: 12 us -> 6.58 us  [gather_by_exchange(): return lax.all_to_all(copies, axis, split_axis=0, concat_axis=0, tiled=True)]
    all_to_all x2 -> x1, waiting for transfers between devices: 11.4 us -> 7.16 us  [gather_by_exchange(): return lax.all_to_all(copies, axis, split_axis=0, concat_axis=0, tiled=True)]
  transfers between devices with their start and end apart: 7 -> 6, of which waited for: 6 -> 5; matrix products, arithmetic and copies ran while one was open for 7% -> 7% of each run, Pallas kernels for 0% -> 0%
where the time goes in v14:
time: 247 us; the launch traced here: 246 us
  waiting for transfers between devices  131 us (53%)
  blocking collectives  54.5 us (22%)
  starting transfers between devices  17.3 us (7%)
  local copies, waits for them, and re-layouts  16.1 us (7%)
  between operations  14 us (6%)
  other arithmetic  7.47 us (3%)
  Pallas kernels  5.89 us (2%)
    all_gather x1, waiting for transfers between devices, body(): lax.all_gather(right_vals[None], 'row', axis=0, tiled=True)  68.2 us
    reduce_scatter x1, waiting for transfers between devices, body(): lax.psum_scatter(partial_sum[None, None], 'depth', scatter_dimension=2, t...  45.4 us
    all_to_all x1, blocking collectives, body(): lax.all_to_all(left_vals, 'depth', split_axis=0, concat_axis=0, tiled=True)  27.7 us
    all_to_all x1, blocking collectives, body(): lax.all_to_all(right_vals, 'col', split_axis=0, concat_axis=0, tiled=True)  26.8 us
    all_to_all x1, starting transfers between devices, body(): lax.all_to_all(id_pack, 'col', split_axis=0, concat_axis=0, tiled=True)  7.38 us
    all_to_all x1, waiting for transfers between devices, gather_by_exchange(): return lax.all_to_all(copies, axis, split_axis=0, concat_axis=0, tiled=True)  7.16 us
    all_to_all x1, starting transfers between devices, gather_by_exchange(): return lax.all_to_all(copies, axis, split_axis=0, concat_axis=0, tiled=True)  6.58 us
    all_to_all x1, waiting for transfers between devices, body(): lax.all_to_all(left_cols, 'depth', split_axis=0, concat_axis=0, tiled=True)  5.9 us
  transfers between devices with their start and end apart: 6, of which 5 were waited for; matrix products, arithmetic and copies ran while one was open for 7% of the time, Pallas kernels for 0%

profile of v14, /device:TPU:6, one launch (start us, length us, event | category | flops | bytes accessed | tf_op | source)
XLA Modules:
  0.0 245.9 jit_solution(17331902891880709114)
XLA Ops:
  7.2 0.7 and_select_fusion.7
  8.5 0.7 fusion.16
  9.3 2.1 scatter_fusion
  11.3 27.7 %all_to_all.32 = bf16[8,1,2,128,128]{4,3,2,1,0:T(8,128)(2,1)} all-to-all(bf16[8,1,2,128,128]{4,3,2,1,0:T(8,128)(2,1)S(1)} %bitcast.82), channel_id=1, replica_groups=mesh['row'=4,'col'=16,'depth'=8] {'depth'}, dimensions={0} | all-to-all | bytes 1048576 | tf_op jit(solution)/shard_map/all_to_all | solution.py:104
  39.4 1.1 scatter_fusion.1
  40.6 26.8 %all_to_all.33 = bf16[16,1,2,128,128]{4,3,2,1,0:T(8,128)(2,1)} all-to-all(bf16[16,1,2,128,128]{4,3,2,1,0:T(8,128)(2,1)S(1)} %bitcast.81), channel_id=1, replica_groups=mesh['row'=4,'col'=16,'depth'=8] {'col'}, dimensions={0} | all-to-all | bytes 2097152 | tf_op jit(solution)/shard_map/all_to_all | solution.py:120
  67.4 0.8 scatter_custom_fusion
  68.2 0.7 reshape.930
  68.8 3.3 %all-to-all-start = ((s32[8,1,2]{2,1,0:T(1,128)}), s32[8,1,2]{2,1,0:T(1,128)S(1)}, u32[]{:S(2)}, u32[]{:S(2)}) async-start(s32[8,1,2]{2,1,0:T(1,128)} %bitcast.6), calls=%async_computation | async-start | bytes 8192 | tf_op jit(solution)/shard_map/all_to_all | solution.py:105
  72.1 0.8 scatter_custom_fusion.1
  73.8 5.9 %all-to-all-done = s32[8,1,2]{2,1,0:T(1,128)S(1)} async-done(((s32[8,1,2]{2,1,0:T(1,128)}), s32[8,1,2]{2,1,0:T(1,128)S(1)}, u32[]{:S(2)}, u32[]{:S(2)}) %all-to-all-start) | async-done | bytes 96 | tf_op jit(solution)/shard_map/all_to_all | solution.py:105
  80.2 0.7 reduce.5
  80.9 0.7 pad_add_fusion
  81.6 7.4 %all-to-all-start.1 = ((s32[16,1,18]{2,1,0:T(1,128)}), s32[16,1,18]{2,1,0:T(1,128)S(1)}, u32[]{:S(2)}, u32[]{:S(2)}) async-start(s32[16,1,18]{2,1,0:T(1,128)} %bitcast.9), calls=%async_computation.1 | async-start | bytes 16384 | tf_op jit(solution)/shard_map/all_to_all | solution.py:129
  89.1 3.9 %all-to-all-done.1 = s32[16,1,18]{2,1,0:T(1,128)S(1)} async-done(((s32[16,1,18]{2,1,0:T(1,128)}), s32[16,1,18]{2,1,0:T(1,128)S(1)}, u32[]{:S(2)}, u32[]{:S(2)}) %all-to-all-start.1) | async-done | bytes 1184 | tf_op jit(solution)/shard_map/all_to_all | solution.py:129
  93.2 0.8 gather_fusion
  94.9 6.6 %all-to-all-start.2 = ((s32[4,16,1,2]{1,3,2,0:T(2,128)}), s32[4,16,1,2]{1,3,2,0:T(2,128)S(1)}, u32[]{:S(2)}, u32[]{:S(2)}) async-start(s32[4,16,1,2]{1,3,2,0:T(2,128)} %broadcast_in_dim.103), calls=%async_computation.2 | async-start | bytes 8192 | tf_op jit(solution)/shard_map/all_to_all | solution.py:36
  102.0 7.2 %all-to-all-done.2 = s32[4,16,1,2]{1,3,2,0:T(2,128)S(1)} async-done(((s32[4,16,1,2]{1,3,2,0:T(2,128)}), s32[4,16,1,2]{1,3,2,0:T(2,128)S(1)}, u32[]{:S(2)}, u32[]{:S(2)}) %all-to-all-start.2) | async-done | bytes 544 | tf_op jit(solution)/shard_map/all_to_all | solution.py:36
  111.6 5.0 %gather_fusion.2 = bf16[64,128,128]{2,1,0:T(8,128)(2,1)S(1)} fusion(bf16[256,128,128]{2,1,0:T(8,128)(2,1)} %bitcast.87, s32[1024]{0:T(1024)S(1)} %pad_clamp_fusion), kind=kCustom, calls=%fused_computation.2 | custom fusion | bytes 4194560 | tf_op jit(solution)/shard_map/jit(_take)/gather | solution.py:145
  116.6 1.6 broadcast_select_fusion.left_ref
  118.2 68.2 %all-gather.7.cloned.1.call-done = bf16[64,1,2,128,128]{4,3,2,1,0:T(8,128)(2,1)} async-done(((bf16[16,1,2,128,128]{4,3,2,1,0:T(8,128)(2,1)}), bf16[64,1,2,128,128]{4,3,2,1,0:T(8,128)(2,1)}) %all-gather.7.cloned.1.call-update) | async-done | bytes 4194320 | tf_op jit(solution)/shard_map/all_gather | solution.py:133
  186.4 5.9 %shard_map.46 = f32[32,128,128]{2,1,0:T(8,128)} custom-call(s32[64]{0:T(128)} %multiply_add_fusion.right_index, s32[64]{0:T(128)} %reshape.936.found, bf16[64,128,128]{2,1,0:T(8,128)(2,1)} %broadcast_select_fusion.left_ref, bf16[128,128,128]{2,1,0:T(8,128)(2,1)} %bitcast.83), custom_call_target="tpu_custom_call" | custom-call | flops 268435456 | bytes 6291456 | tf_op jit(solution)/shard_map/pallas_call | solution.py:59
  192.3 45.4 %reduce-scatter.2.cloned.1.call-done = f32[1,1,4,128,128]{4,3,2,1,0:T(8,128)} async-done(((f32[1,1,32,128,128]{4,3,2,1,0:T(8,128)}), f32[1,1,4,128,128]{4,3,2,1,0:T(8,128)}) %reduce-scatter.2.cloned.1.call-update) | async-done | bytes 262160 | tf_op jit(solution)/shard_map/reduce_scatter | solution.py:164
  237.7 1.7 log-plus-one_convert_fusion
  (64 shorter events, 6.4 us)
Async XLA Ops:
  6.5 105.0 %all-gather.5.cloned.1.call-start = ((), (), s32[]{:S(2)}) async-start(), calls=%async_computation.7 | async-start | bytes 8912896 | tf_op jit(solution)/shard_map/all_gather | solution.py:107
  9.3 30.1 %copy-start = (bf16[1,1,16,128,128]{4,3,2,1,0:T(8,128)(2,1)S(1)}, bf16[1,1,16,128,128]{4,3,2,1,0:T(8,128)(2,1)}, u32[]{:S(2)}) copy-start(bf16[1,1,16,128,128]{4,3,2,1,0:T(8,128)(2,1)} %param.4) | copy-start | bytes 1572868
  39.1 147.3 %all-gather.7.cloned.1.call-start = ((), (), s32[]{:S(2)}) async-start(), calls=%async_computation.8 | async-start | bytes 5242880 | tf_op jit(solution)/shard_map/all_gather | solution.py:133
  39.4 33.5 %copy-start.1 = (s32[1,1,32,2]{2,3,1,0:T(2,128)S(1)}, s32[1,1,32,2]{2,3,1,0:T(2,128)}, u32[]{:S(2)}) copy-start(s32[1,1,32,2]{2,3,1,0:T(2,128)} %param.7) | copy-start | bytes 772
  68.8 10.8 %all-to-all-start = ((s32[8,1,2]{2,1,0:T(1,128)}), s32[8,1,2]{2,1,0:T(1,128)S(1)}, u32[]{:S(2)}, u32[]{:S(2)}) async-start(s32[8,1,2]{2,1,0:T(1,128)} %bitcast.6), calls=%async_computation | async-start | bytes 8192 | tf_op jit(solution)/shard_map/all_to_all | solution.py:105
  81.6 11.4 %all-to-all-start.1 = ((s32[16,1,18]{2,1,0:T(1,128)}), s32[16,1,18]{2,1,0:T(1,128)S(1)}, u32[]{:S(2)}, u32[]{:S(2)}) async-start(s32[16,1,18]{2,1,0:T(1,128)} %bitcast.9), calls=%async_computation.1 | async-start | bytes 16384 | tf_op jit(solution)/shard_map/all_to_all | solution.py:129
  94.9 14.3 %all-to-all-start.2 = ((s32[4,16,1,2]{1,3,2,0:T(2,128)}), s32[4,16,1,2]{1,3,2,0:T(2,128)S(1)}, u32[]{:S(2)}, u32[]{:S(2)}) async-start(s32[4,16,1,2]{1,3,2,0:T(2,128)} %broadcast_in_dim.103), calls=%async_computation.2 | async-start | bytes 8192 | tf_op jit(solution)/shard_map/all_to_all | solution.py:36
  101.5 136.2 %reduce-scatter.2.cloned.1.call-start = ((), (), s32[]{:S(2)}) async-start(), calls=%async_computation.6 | async-start | bytes 2359296 | tf_op jit(solution)/shard_map/reduce_scatter | solution.py:164
Sparse Core Ops, SparseCore 0:
  39.2 61.8 all-gather.4
  103.2 83.1 all-gather.6
  192.4 45.1 reduce-scatter.1

commit v15 on v14

--- a/solution.py
+++ b/solution.py
@@ -44,11 +44,10 @@
     ]
     for copy in copies:
         copy.start()
-    for copy in copies:
-        copy.wait()
     for p in range(count // 2):
         total = jnp.zeros(out_ref.shape[1:], jnp.float32)
         for t in (2 * p, 2 * p + 1):
+            copies[t].wait()
             term = jnp.dot(left_ref[t], right_buf[t], preferred_element_type=jnp.float32)
             total = total + jnp.where(found[t] != 0, term, 0.0)
         out_ref[p] = total

time: 247 us -> 254 us (1.028)
  Pallas kernels: 5.89 us -> 13.6 us
    pallas_call x1, Pallas kernels: 5.89 us -> 13.6 us  [pair_products(): pl.pallas_call(pair_kernel, out_shape=jax.ShapeDtypeStruct((count // 2, b...]
where the time goes in v15:
time: 254 us
  waiting for transfers between devices  131 us (52%)
  blocking collectives  54.5 us (21%)
  starting transfers between devices  17.3 us (7%)
  local copies, waits for them, and re-layouts  16.1 us (6%)
  between operations  14 us (6%)
  Pallas kernels  13.6 us (5%)
  other arithmetic  7.47 us (3%)
    all_gather x1, waiting for transfers between devices, body(): lax.all_gather(right_vals[None], 'row', axis=0, tiled=True)  68.2 us
    reduce_scatter x1, waiting for transfers between devices, body(): lax.psum_scatter(partial_sum[None, None], 'depth', scatter_dimension=2, t...  45.6 us
    all_to_all x1, blocking collectives, body(): lax.all_to_all(left_vals, 'depth', split_axis=0, concat_axis=0, tiled=True)  27.7 us
    all_to_all x1, blocking collectives, body(): lax.all_to_all(right_vals, 'col', split_axis=0, concat_axis=0, tiled=True)  26.8 us
    pallas_call x1, Pallas kernels, pair_products(): pl.pallas_call(pair_kernel, out_shape=jax.ShapeDtypeStruct((count // 2, b...  13.6 us
    all_to_all x1, starting transfers between devices, body(): lax.all_to_all(id_pack, 'col', split_axis=0, concat_axis=0, tiled=True)  7.38 us
    all_to_all x1, waiting for transfers between devices, gather_by_exchange(): return lax.all_to_all(copies, axis, split_axis=0, concat_axis=0, tiled=True)  7.16 us
    all_to_all x1, starting transfers between devices, gather_by_exchange(): return lax.all_to_all(copies, axis, split_axis=0, concat_axis=0, tiled=True)  6.57 us
  transfers between devices with their start and end apart: 6, of which 5 were waited for; matrix products, arithmetic and copies ran while one was open for 7% of the time, Pallas kernels for 0%

profile of v15, /device:TPU:6, one launch (start us, length us, event | category | flops | bytes accessed | tf_op | source)
XLA Modules:
  0.0 253.8 jit_solution(4776543440174066868)
XLA Ops:
  7.2 0.7 and_select_fusion.7
  8.5 0.7 fusion.16
  9.3 2.1 scatter_fusion
  11.3 27.7 %all_to_all.32 = bf16[8,1,2,128,128]{4,3,2,1,0:T(8,128)(2,1)} all-to-all(bf16[8,1,2,128,128]{4,3,2,1,0:T(8,128)(2,1)S(1)} %bitcast.82), channel_id=1, replica_groups=mesh['row'=4,'col'=16,'depth'=8] {'depth'}, dimensions={0} | all-to-all | bytes 1048576 | tf_op jit(solution)/shard_map/all_to_all | solution.py:103
  39.4 1.1 scatter_fusion.1
  40.6 26.8 %all_to_all.33 = bf16[16,1,2,128,128]{4,3,2,1,0:T(8,128)(2,1)} all-to-all(bf16[16,1,2,128,128]{4,3,2,1,0:T(8,128)(2,1)S(1)} %bitcast.81), channel_id=1, replica_groups=mesh['row'=4,'col'=16,'depth'=8] {'col'}, dimensions={0} | all-to-all | bytes 2097152 | tf_op jit(solution)/shard_map/all_to_all | solution.py:119
  67.4 0.8 scatter_custom_fusion
  68.2 0.7 reshape.930
  68.8 3.3 %all-to-all-start = ((s32[8,1,2]{2,1,0:T(1,128)}), s32[8,1,2]{2,1,0:T(1,128)S(1)}, u32[]{:S(2)}, u32[]{:S(2)}) async-start(s32[8,1,2]{2,1,0:T(1,128)} %bitcast.6), calls=%async_computation | async-start | bytes 8192 | tf_op jit(solution)/shard_map/all_to_all | solution.py:104
  72.1 0.8 scatter_custom_fusion.1
  73.8 5.9 %all-to-all-done = s32[8,1,2]{2,1,0:T(1,128)S(1)} async-done(((s32[8,1,2]{2,1,0:T(1,128)}), s32[8,1,2]{2,1,0:T(1,128)S(1)}, u32[]{:S(2)}, u32[]{:S(2)}) %all-to-all-start) | async-done | bytes 96 | tf_op jit(solution)/shard_map/all_to_all | solution.py:104
  80.2 0.7 reduce.5
  80.9 0.7 pad_add_fusion
  81.6 7.4 %all-to-all-start.1 = ((s32[16,1,18]{2,1,0:T(1,128)}), s32[16,1,18]{2,1,0:T(1,128)S(1)}, u32[]{:S(2)}, u32[]{:S(2)}) async-start(s32[16,1,18]{2,1,0:T(1,128)} %bitcast.9), calls=%async_computation.1 | async-start | bytes 16384 | tf_op jit(solution)/shard_map/all_to_all | solution.py:128
  89.1 3.9 %all-to-all-done.1 = s32[16,1,18]{2,1,0:T(1,128)S(1)} async-done(((s32[16,1,18]{2,1,0:T(1,128)}), s32[16,1,18]{2,1,0:T(1,128)S(1)}, u32[]{:S(2)}, u32[]{:S(2)}) %all-to-all-start.1) | async-done | bytes 1184 | tf_op jit(solution)/shard_map/all_to_all | solution.py:128
  93.2 0.8 gather_fusion
  94.9 6.6 %all-to-all-start.2 = ((s32[4,16,1,2]{1,3,2,0:T(2,128)}), s32[4,16,1,2]{1,3,2,0:T(2,128)S(1)}, u32[]{:S(2)}, u32[]{:S(2)}) async-start(s32[4,16,1,2]{1,3,2,0:T(2,128)} %broadcast_in_dim.103), calls=%async_computation.2 | async-start | bytes 8192 | tf_op jit(solution)/shard_map/all_to_all | solution.py:36
  102.0 7.2 %all-to-all-done.2 = s32[4,16,1,2]{1,3,2,0:T(2,128)S(1)} async-done(((s32[4,16,1,2]{1,3,2,0:T(2,128)}), s32[4,16,1,2]{1,3,2,0:T(2,128)S(1)}, u32[]{:S(2)}, u32[]{:S(2)}) %all-to-all-start.2) | async-done | bytes 544 | tf_op jit(solution)/shard_map/all_to_all | solution.py:36
  111.6 5.0 %gather_fusion.2 = bf16[64,128,128]{2,1,0:T(8,128)(2,1)S(1)} fusion(bf16[256,128,128]{2,1,0:T(8,128)(2,1)} %bitcast.87, s32[1024]{0:T(1024)S(1)} %pad_clamp_fusion), kind=kCustom, calls=%fused_computation.2 | custom fusion | bytes 4194560 | tf_op jit(solution)/shard_map/jit(_take)/gather | solution.py:144
  116.6 1.6 broadcast_select_fusion.left_ref
  118.2 68.2 %all-gather.7.cloned.1.call-done = bf16[64,1,2,128,128]{4,3,2,1,0:T(8,128)(2,1)} async-done(((bf16[16,1,2,128,128]{4,3,2,1,0:T(8,128)(2,1)}), bf16[64,1,2,128,128]{4,3,2,1,0:T(8,128)(2,1)}) %all-gather.7.cloned.1.call-update) | async-done | bytes 4194320 | tf_op jit(solution)/shard_map/all_gather | solution.py:132
  186.4 13.6 %shard_map.46 = f32[32,128,128]{2,1,0:T(8,128)} custom-call(s32[64]{0:T(128)} %multiply_add_fusion.right_index, s32[64]{0:T(128)} %reshape.936.found, bf16[64,128,128]{2,1,0:T(8,128)(2,1)} %broadcast_select_fusion.left_ref, bf16[128,128,128]{2,1,0:T(8,128)(2,1)} %bitcast.83), custom_call_target="tpu_custom_call" | custom-call | flops 268435456 | bytes 6291456 | tf_op jit(solution)/shard_map/pallas_call | solution.py:58
  200.1 45.6 %reduce-scatter.2.cloned.1.call-done = f32[1,1,4,128,128]{4,3,2,1,0:T(8,128)} async-done(((f32[1,1,32,128,128]{4,3,2,1,0:T(8,128)}), f32[1,1,4,128,128]{4,3,2,1,0:T(8,128)}) %reduce-scatter.2.cloned.1.call-update) | async-done | bytes 262160 | tf_op jit(solution)/shard_map/reduce_scatter | solution.py:163
  245.6 1.7 log-plus-one_convert_fusion
  (64 shorter events, 6.4 us)
Async XLA Ops:
  6.5 105.0 %all-gather.5.cloned.1.call-start = ((), (), s32[]{:S(2)}) async-start(), calls=%async_computation.7 | async-start | bytes 8912896 | tf_op jit(solution)/shard_map/all_gather | solution.py:106
  9.3 30.1 %copy-start = (bf16[1,1,16,128,128]{4,3,2,1,0:T(8,128)(2,1)S(1)}, bf16[1,1,16,128,128]{4,3,2,1,0:T(8,128)(2,1)}, u32[]{:S(2)}) copy-start(bf16[1,1,16,128,128]{4,3,2,1,0:T(8,128)(2,1)} %param.4) | copy-start | bytes 1572868
  39.1 147.3 %all-gather.7.cloned.1.call-start = ((), (), s32[]{:S(2)}) async-start(), calls=%async_computation.8 | async-start | bytes 5242880 | tf_op jit(solution)/shard_map/all_gather | solution.py:132
  39.4 33.5 %copy-start.1 = (s32[1,1,32,2]{2,3,1,0:T(2,128)S(1)}, s32[1,1,32,2]{2,3,1,0:T(2,128)}, u32[]{:S(2)}) copy-start(s32[1,1,32,2]{2,3,1,0:T(2,128)} %param.7) | copy-start | bytes 772
  68.8 10.8 %all-to-all-start = ((s32[8,1,2]{2,1,0:T(1,128)}), s32[8,1,2]{2,1,0:T(1,128)S(1)}, u32[]{:S(2)}, u32[]{:S(2)}) async-start(s32[8,1,2]{2,1,0:T(1,128)} %bitcast.6), calls=%async_computation | async-start | bytes 8192 | tf_op jit(solution)/shard_map/all_to_all | solution.py:104
  81.6 11.4 %all-to-all-start.1 = ((s32[16,1,18]{2,1,0:T(1,128)}), s32[16,1,18]{2,1,0:T(1,128)S(1)}, u32[]{:S(2)}, u32[]{:S(2)}) async-start(s32[16,1,18]{2,1,0:T(1,128)} %bitcast.9), calls=%async_computation.1 | async-start | bytes 16384 | tf_op jit(solution)/shard_map/all_to_all | solution.py:128
  94.9 14.3 %all-to-all-start.2 = ((s32[4,16,1,2]{1,3,2,0:T(2,128)}), s32[4,16,1,2]{1,3,2,0:T(2,128)S(1)}, u32[]{:S(2)}, u32[]{:S(2)}) async-start(s32[4,16,1,2]{1,3,2,0:T(2,128)} %broadcast_in_dim.103), calls=%async_computation.2 | async-start | bytes 8192 | tf_op jit(solution)/shard_map/all_to_all | solution.py:36
  101.5 144.2 %reduce-scatter.2.cloned.1.call-start = ((), (), s32[]{:S(2)}) async-start(), calls=%async_computation.6 | async-start | bytes 2359296 | tf_op jit(solution)/shard_map/reduce_scatter | solution.py:163
Sparse Core Ops, SparseCore 0:
  39.2 61.8 all-gather.4
  103.2 83.1 all-gather.6
  200.2 45.3 reduce-scatter.1

commit v16 on v14

--- a/solution.py
+++ b/solution.py
@@ -36,46 +36,46 @@
     return lax.all_to_all(copies, axis, split_axis=0, concat_axis=0, tiled=True)
 
 
-def pair_kernel(right_index, found, left_ref, right_hbm, out_ref, right_buf, sems):
-    count = right_buf.shape[0]
+def pair_kernel(right_index, left_ref, right_hbm, out_ref, right_buf, sems):
+    pairs, width, block_size = right_buf.shape
+    per_pair = width // block_size
     copies = [
-        pltpu.make_async_copy(right_hbm.at[right_index[t]], right_buf.at[t], sems.at[t])
-        for t in range(count)
+        pltpu.make_async_copy(
+            right_hbm.at[right_index[t]],
+            right_buf.at[t // per_pair, pl.ds((t % per_pair) * block_size, block_size)],
+            sems.at[t],
+        )
+        for t in range(pairs * per_pair)
     ]
     for copy in copies:
         copy.start()
     for copy in copies:
         copy.wait()
-    for p in range(count // 2):
-        total = jnp.zeros(out_ref.shape[1:], jnp.float32)
-        for t in (2 * p, 2 * p + 1):
-            term = jnp.dot(left_ref[t], right_buf[t], preferred_element_type=jnp.float32)
-            total = total + jnp.where(found[t] != 0, term, 0.0)
-        out_ref[p] = total
+    for p in range(pairs):
+        out_ref[p] = jnp.dot(left_ref[p], right_buf[p], preferred_element_type=jnp.float32)
 
 
-def pair_products(right_index, found, left_pick, right_flat):
-    count, block_size, _ = left_pick.shape
+def pair_products(right_index, left_wide, right_flat):
+    pairs, block_size, width = left_wide.shape
     return pl.pallas_call(
         pair_kernel,
-        out_shape=jax.ShapeDtypeStruct((count // 2, block_size, block_size), jnp.float32),
+        out_shape=jax.ShapeDtypeStruct((pairs, block_size, block_size), jnp.float32),
         in_specs=[
-            pl.BlockSpec(memory_space=pltpu.SMEM),
             pl.BlockSpec(memory_space=pltpu.SMEM),
             pl.BlockSpec(memory_space=pltpu.VMEM),
             pl.BlockSpec(memory_space=pl.ANY),
         ],
         out_specs=pl.BlockSpec(memory_space=pltpu.VMEM),
         scratch_shapes=[
-            pltpu.VMEM((count, block_size, block_size), right_flat.dtype),
-            pltpu.SemaphoreType.DMA((count,)),
+            pltpu.VMEM((pairs, width, block_size), right_flat.dtype),
+            pltpu.SemaphoreType.DMA((pairs * (width // block_size),)),
         ],
         cost_estimate=pl.CostEstimate(
-            flops=2 * count * block_size**3,
-            bytes_accessed=count * block_size * block_size * 2 * 2 + count * block_size * block_size * 2,
+            flops=2 * pairs * block_size * width * block_size,
+            bytes_accessed=pairs * block_size * width * 2 * 2 + pairs * block_size * block_size * 4,
             transcendentals=0,
         ),
-    )(right_index, found, left_pick, right_flat)
+    )(right_index, left_wide, right_flat)
 
 
 def body(block_values, block_cols, live_count, out_pattern):
@@ -155,12 +155,13 @@
     )
     found = jnp.any(matched, axis=2)
     pattern_len = pattern_rows.shape[0]
+    left_wide = jnp.where(
+        found.reshape(-1)[:, None, None], left_pick, jnp.zeros_like(left_pick)
+    ).reshape(pattern_len, cap_left, block_size, block_size)
+    left_wide = left_wide.transpose(0, 2, 1, 3).reshape(pattern_len, block_size, cap_left * block_size)
     partial_sum = pair_products(
-        (right_row * cap_right + slot).reshape(-1),
-        found.reshape(-1).astype(jnp.int32),
-        left_pick,
-        right_flat,
-    ).reshape(pattern_len, block_size, block_size)
+        (right_row * cap_right + slot).reshape(-1), left_wide, right_flat
+    )
     share = lax.psum_scatter(partial_sum[None, None], "depth", scatter_dimension=2, tiled=True)
     return jnp.log1p(share).astype(jnp.bfloat16)
 

time: 247 us -> 247 us (level)
  no operation moved by 1% of the time
where the time goes in v16:
time: 247 us; the launch traced here: 246 us
  waiting for transfers between devices  131 us (53%)
  blocking collectives  54.5 us (22%)
  starting transfers between devices  17.3 us (7%)
  local copies, waits for them, and re-layouts  15.4 us (6%)
  between operations  14 us (6%)
  other arithmetic  7.81 us (3%)
  Pallas kernels  5.93 us (2%)
    all_gather x1, waiting for transfers between devices, body(): lax.all_gather(right_vals[None], 'row', axis=0, tiled=True)  68.4 us
    reduce_scatter x1, waiting for transfers between devices, body(): lax.psum_scatter(partial_sum[None, None], 'depth', scatter_dimension=2, t...  45.4 us
    all_to_all x1, blocking collectives, body(): lax.all_to_all(left_vals, 'depth', split_axis=0, concat_axis=0, tiled=True)  27.7 us
    all_to_all x1, blocking collectives, body(): lax.all_to_all(right_vals, 'col', split_axis=0, concat_axis=0, tiled=True)  26.8 us
    all_to_all x1, starting transfers between devices, body(): lax.all_to_all(id_pack, 'col', split_axis=0, concat_axis=0, tiled=True)  7.38 us
    all_to_all x1, waiting for transfers between devices, gather_by_exchange(): return lax.all_to_all(copies, axis, split_axis=0, concat_axis=0, tiled=True)  7.15 us
    all_to_all x1, starting transfers between devices, gather_by_exchange(): return lax.all_to_all(copies, axis, split_axis=0, concat_axis=0, tiled=True)  6.58 us
    all_to_all x1, waiting for transfers between devices, body(): lax.all_to_all(left_cols, 'depth', split_axis=0, concat_axis=0, tiled=True)  6.22 us
  transfers between devices with their start and end apart: 6, of which 5 were waited for; matrix products, arithmetic and copies ran while one was open for 7% of the time, Pallas kernels for 0%

profile of v16, /device:TPU:6, one launch (start us, length us, event | category | flops | bytes accessed | tf_op | source)
XLA Modules:
  0.0 246.0 jit_solution(4179822633200088277)
XLA Ops:
  6.5 0.7 and_select_fusion.6
  8.5 0.7 fusion.16
  9.3 2.1 scatter_fusion
  11.3 27.7 %all_to_all.32 = bf16[8,1,2,128,128]{4,3,2,1,0:T(8,128)(2,1)} all-to-all(bf16[8,1,2,128,128]{4,3,2,1,0:T(8,128)(2,1)S(1)} %bitcast.86), channel_id=1, replica_groups=mesh['row'=4,'col'=16,'depth'=8] {'depth'}, dimensions={0} | all-to-all | bytes 1048576 | tf_op jit(solution)/shard_map/all_to_all | solution.py:104
  39.4 1.1 scatter_fusion.1
  40.5 26.8 %all_to_all.33 = bf16[16,1,2,128,128]{4,3,2,1,0:T(8,128)(2,1)} all-to-all(bf16[16,1,2,128,128]{4,3,2,1,0:T(8,128)(2,1)S(1)} %bitcast.85), channel_id=1, replica_groups=mesh['row'=4,'col'=16,'depth'=8] {'col'}, dimensions={0} | all-to-all | bytes 2097152 | tf_op jit(solution)/shard_map/all_to_all | solution.py:120
  67.4 0.8 scatter_custom_fusion
  68.1 0.7 reshape.936
  68.8 3.3 %all-to-all-start = ((s32[8,1,2]{2,1,0:T(1,128)}), s32[8,1,2]{2,1,0:T(1,128)S(1)}, u32[]{:S(2)}, u32[]{:S(2)}) async-start(s32[8,1,2]{2,1,0:T(1,128)} %bitcast.6), calls=%async_computation | async-start | bytes 8192 | tf_op jit(solution)/shard_map/all_to_all | solution.py:105
  72.6 0.8 scatter_custom_fusion.1
  73.4 6.2 %all-to-all-done = s32[8,1,2]{2,1,0:T(1,128)S(1)} async-done(((s32[8,1,2]{2,1,0:T(1,128)}), s32[8,1,2]{2,1,0:T(1,128)S(1)}, u32[]{:S(2)}, u32[]{:S(2)}) %all-to-all-start) | async-done | bytes 96 | tf_op jit(solution)/shard_map/all_to_all | solution.py:105
  80.2 0.7 reduce.5
  80.9 0.7 pad_add_fusion
  81.6 7.4 %all-to-all-start.1 = ((s32[16,1,18]{2,1,0:T(1,128)}), s32[16,1,18]{2,1,0:T(1,128)S(1)}, u32[]{:S(2)}, u32[]{:S(2)}) async-start(s32[16,1,18]{2,1,0:T(1,128)} %bitcast.9), calls=%async_computation.1 | async-start | bytes 16384 | tf_op jit(solution)/shard_map/all_to_all | solution.py:129
  89.3 3.7 %all-to-all-done.1 = s32[16,1,18]{2,1,0:T(1,128)S(1)} async-done(((s32[16,1,18]{2,1,0:T(1,128)}), s32[16,1,18]{2,1,0:T(1,128)S(1)}, u32[]{:S(2)}, u32[]{:S(2)}) %all-to-all-start.1) | async-done | bytes 1184 | tf_op jit(solution)/shard_map/all_to_all | solution.py:129
  93.2 0.8 gather_fusion
  95.0 6.6 %all-to-all-start.2 = ((s32[4,16,1,2]{1,3,2,0:T(2,128)}), s32[4,16,1,2]{1,3,2,0:T(2,128)S(1)}, u32[]{:S(2)}, u32[]{:S(2)}) async-start(s32[4,16,1,2]{1,3,2,0:T(2,128)} %broadcast_in_dim.114), calls=%async_computation.2 | async-start | bytes 8192 | tf_op jit(solution)/shard_map/all_to_all | solution.py:36
  102.1 7.2 %all-to-all-done.2 = s32[4,16,1,2]{1,3,2,0:T(2,128)S(1)} async-done(((s32[4,16,1,2]{1,3,2,0:T(2,128)}), s32[4,16,1,2]{1,3,2,0:T(2,128)S(1)}, u32[]{:S(2)}, u32[]{:S(2)}) %all-to-all-start.2) | async-done | bytes 544 | tf_op jit(solution)/shard_map/all_to_all | solution.py:36
  111.0 5.0 %gather_fusion.2 = bf16[64,128,128]{2,1,0:T(8,128)(2,1)S(1)} fusion(bf16[256,128,128]{2,1,0:T(8,128)(2,1)} %bitcast.91, s32[1024]{0:T(1024)S(1)} %pad_clamp_fusion), kind=kCustom, calls=%fused_computation.2 | custom fusion | bytes 4194560 | tf_op jit(solution)/shard_map/jit(_take)/gather | solution.py:145
  116.0 2.0 copy_bitcast_fusion.left_ref
  118.0 68.4 %all-gather.7.cloned.1.call-done = bf16[64,1,2,128,128]{4,3,2,1,0:T(8,128)(2,1)} async-done(((bf16[16,1,2,128,128]{4,3,2,1,0:T(8,128)(2,1)}), bf16[64,1,2,128,128]{4,3,2,1,0:T(8,128)(2,1)}) %all-gather.7.cloned.1.call-update) | async-done | bytes 4194320 | tf_op jit(solution)/shard_map/all_gather | solution.py:133
  186.4 5.9 %shard_map.46 = f32[32,128,128]{2,1,0:T(8,128)} custom-call(s32[64]{0:T(128)} %multiply_add_fusion.right_index, bf16[32,128,256]{2,1,0:T(8,128)(2,1)} %copy_bitcast_fusion.left_ref, bf16[128,128,128]{2,1,0:T(8,128)(2,1)} %bitcast.87), custom_call_target="tpu_custom_call" | custom-call | flops 268435456 | bytes 6291456 | tf_op jit(solution)/shard_map/pallas_call | solution.py:60
  192.3 45.4 %reduce-scatter.2.cloned.1.call-done = f32[1,1,4,128,128]{4,3,2,1,0:T(8,128)} async-done(((f32[1,1,32,128,128]{4,3,2,1,0:T(8,128)}), f32[1,1,4,128,128]{4,3,2,1,0:T(8,128)}) %reduce-scatter.2.cloned.1.call-update) | async-done | bytes 262160 | tf_op jit(solution)/shard_map/reduce_scatter | solution.py:165
  237.7 1.7 log-plus-one_convert_fusion
  (59 shorter events, 5.8 us)
Async XLA Ops:
  6.5 104.5 %all-gather.5.cloned.1.call-start = ((), (), s32[]{:S(2)}) async-start(), calls=%async_computation.7 | async-start | bytes 8912896 | tf_op jit(solution)/shard_map/all_gather | solution.py:107
  9.3 30.1 %copy-start = (bf16[1,1,16,128,128]{4,3,2,1,0:T(8,128)(2,1)S(1)}, bf16[1,1,16,128,128]{4,3,2,1,0:T(8,128)(2,1)}, u32[]{:S(2)}) copy-start(bf16[1,1,16,128,128]{4,3,2,1,0:T(8,128)(2,1)} %param.4) | copy-start | bytes 1572868
  39.1 147.3 %all-gather.7.cloned.1.call-start = ((), (), s32[]{:S(2)}) async-start(), calls=%async_computation.8 | async-start | bytes 5242880 | tf_op jit(solution)/shard_map/all_gather | solution.py:133
  39.4 32.8 %copy-start.1 = (s32[1,1,32,2]{2,3,1,0:T(2,128)S(1)}, s32[1,1,32,2]{2,3,1,0:T(2,128)}, u32[]{:S(2)}) copy-start(s32[1,1,32,2]{2,3,1,0:T(2,128)} %param.7) | copy-start | bytes 772
  68.8 10.8 %all-to-all-start = ((s32[8,1,2]{2,1,0:T(1,128)}), s32[8,1,2]{2,1,0:T(1,128)S(1)}, u32[]{:S(2)}, u32[]{:S(2)}) async-start(s32[8,1,2]{2,1,0:T(1,128)} %bitcast.6), calls=%async_computation | async-start | bytes 8192 | tf_op jit(solution)/shard_map/all_to_all | solution.py:105
  81.6 11.4 %all-to-all-start.1 = ((s32[16,1,18]{2,1,0:T(1,128)}), s32[16,1,18]{2,1,0:T(1,128)S(1)}, u32[]{:S(2)}, u32[]{:S(2)}) async-start(s32[16,1,18]{2,1,0:T(1,128)} %bitcast.9), calls=%async_computation.1 | async-start | bytes 16384 | tf_op jit(solution)/shard_map/all_to_all | solution.py:129
  95.0 14.3 %all-to-all-start.2 = ((s32[4,16,1,2]{1,3,2,0:T(2,128)}), s32[4,16,1,2]{1,3,2,0:T(2,128)S(1)}, u32[]{:S(2)}, u32[]{:S(2)}) async-start(s32[4,16,1,2]{1,3,2,0:T(2,128)} %broadcast_in_dim.114), calls=%async_computation.2 | async-start | bytes 8192 | tf_op jit(solution)/shard_map/all_to_all | solution.py:36
  101.5 136.2 %reduce-scatter.2.cloned.1.call-start = ((), (), s32[]{:S(2)}) async-start(), calls=%async_computation.6 | async-start | bytes 2359296 | tf_op jit(solution)/shard_map/reduce_scatter | solution.py:165
Sparse Core Ops, SparseCore 0:
  39.2 61.8 all-gather.4
  103.2 83.1 all-gather.6
  192.5 45.2 reduce-scatter.1

commit v17 on v14

--- a/solution.py
+++ b/solution.py
@@ -161,7 +161,9 @@
         left_pick,
         right_flat,
     ).reshape(pattern_len, block_size, block_size)
-    share = lax.psum_scatter(partial_sum[None, None], "depth", scatter_dimension=2, tiled=True)
+    share = lax.psum_scatter(
+        partial_sum.reshape(-1, block_size), "depth", scatter_dimension=0, tiled=True
+    ).reshape(1, 1, -1, block_size, block_size)
     return jnp.log1p(share).astype(jnp.bfloat16)
 
 

time: 247 us -> 247 us (level)
  no operation moved by 1% of the time
where the time goes in v17:
time: 247 us; the launch traced here: 245 us
  waiting for transfers between devices  130 us (53%)
  blocking collectives  54.5 us (22%)
  starting transfers between devices  17.3 us (7%)
  local copies, waits for them, and re-layouts  16.1 us (7%)
  between operations  14 us (6%)
  other arithmetic  7.47 us (3%)
  Pallas kernels  5.78 us (2%)
    all_gather x1, waiting for transfers between devices, body(): lax.all_gather(right_vals[None], 'row', axis=0, tiled=True)  68.2 us
    reduce_scatter x1, waiting for transfers between devices, body(): lax.psum_scatter(partial_sum.reshape(-1, block_size), 'depth', scatter_di...  45 us
    all_to_all x1, blocking collectives, body(): lax.all_to_all(left_vals, 'depth', split_axis=0, concat_axis=0, tiled=True)  27.7 us
    all_to_all x1, blocking collectives, body(): lax.all_to_all(right_vals, 'col', split_axis=0, concat_axis=0, tiled=True)  26.8 us
    all_to_all x1, starting transfers between devices, body(): lax.all_to_all(id_pack, 'col', split_axis=0, concat_axis=0, tiled=True)  7.38 us
    all_to_all x1, waiting for transfers between devices, gather_by_exchange(): return lax.all_to_all(copies, axis, split_axis=0, concat_axis=0, tiled=True)  7.16 us
    all_to_all x1, starting transfers between devices, gather_by_exchange(): return lax.all_to_all(copies, axis, split_axis=0, concat_axis=0, tiled=True)  6.6 us
    all_to_all x1, waiting for transfers between devices, body(): lax.all_to_all(left_cols, 'depth', split_axis=0, concat_axis=0, tiled=True)  5.9 us
  transfers between devices with their start and end apart: 6, of which 5 were waited for; matrix products, arithmetic and copies ran while one was open for 7% of the time, Pallas kernels for 0%

profile of v17, /device:TPU:6, one launch (start us, length us, event | category | flops | bytes accessed | tf_op | source)
XLA Modules:
  0.0 245.4 jit_solution(12636871411932722198)
XLA Ops:
  7.2 0.7 and_select_fusion.7
  8.5 0.7 fusion.16
  9.3 2.1 scatter_fusion
  11.3 27.7 %all_to_all.32 = bf16[8,1,2,128,128]{4,3,2,1,0:T(8,128)(2,1)} all-to-all(bf16[8,1,2,128,128]{4,3,2,1,0:T(8,128)(2,1)S(1)} %bitcast.83), channel_id=1, replica_groups=mesh['row'=4,'col'=16,'depth'=8] {'depth'}, dimensions={0} | all-to-all | bytes 1048576 | tf_op jit(solution)/shard_map/all_to_all | solution.py:104
  39.4 1.1 scatter_fusion.1
  40.6 26.8 %all_to_all.33 = bf16[16,1,2,128,128]{4,3,2,1,0:T(8,128)(2,1)} all-to-all(bf16[16,1,2,128,128]{4,3,2,1,0:T(8,128)(2,1)S(1)} %bitcast.82), channel_id=1, replica_groups=mesh['row'=4,'col'=16,'depth'=8] {'col'}, dimensions={0} | all-to-all | bytes 2097152 | tf_op jit(solution)/shard_map/all_to_all | solution.py:120
  67.4 0.8 scatter_custom_fusion
  68.2 0.7 reshape.952
  68.8 3.3 %all-to-all-start = ((s32[8,1,2]{2,1,0:T(1,128)}), s32[8,1,2]{2,1,0:T(1,128)S(1)}, u32[]{:S(2)}, u32[]{:S(2)}) async-start(s32[8,1,2]{2,1,0:T(1,128)} %bitcast.6), calls=%async_computation | async-start | bytes 8192 | tf_op jit(solution)/shard_map/all_to_all | solution.py:105
  72.1 0.8 scatter_custom_fusion.1
  73.8 5.9 %all-to-all-done = s32[8,1,2]{2,1,0:T(1,128)S(1)} async-done(((s32[8,1,2]{2,1,0:T(1,128)}), s32[8,1,2]{2,1,0:T(1,128)S(1)}, u32[]{:S(2)}, u32[]{:S(2)}) %all-to-all-start) | async-done | bytes 96 | tf_op jit(solution)/shard_map/all_to_all | solution.py:105
  80.2 0.7 reduce.5
  80.9 0.7 pad_add_fusion
  81.6 7.4 %all-to-all-start.1 = ((s32[16,1,18]{2,1,0:T(1,128)}), s32[16,1,18]{2,1,0:T(1,128)S(1)}, u32[]{:S(2)}, u32[]{:S(2)}) async-start(s32[16,1,18]{2,1,0:T(1,128)} %bitcast.9), calls=%async_computation.1 | async-start | bytes 16384 | tf_op jit(solution)/shard_map/all_to_all | solution.py:129
  89.1 3.9 %all-to-all-done.1 = s32[16,1,18]{2,1,0:T(1,128)S(1)} async-done(((s32[16,1,18]{2,1,0:T(1,128)}), s32[16,1,18]{2,1,0:T(1,128)S(1)}, u32[]{:S(2)}, u32[]{:S(2)}) %all-to-all-start.1) | async-done | bytes 1184 | tf_op jit(solution)/shard_map/all_to_all | solution.py:129
  93.2 0.8 gather_fusion
  94.9 6.6 %all-to-all-start.2 = ((s32[4,16,1,2]{1,3,2,0:T(2,128)}), s32[4,16,1,2]{1,3,2,0:T(2,128)S(1)}, u32[]{:S(2)}, u32[]{:S(2)}) async-start(s32[4,16,1,2]{1,3,2,0:T(2,128)} %broadcast_in_dim.100), calls=%async_computation.2 | async-start | bytes 8192 | tf_op jit(solution)/shard_map/all_to_all | solution.py:36
  102.0 7.2 %all-to-all-done.2 = s32[4,16,1,2]{1,3,2,0:T(2,128)S(1)} async-done(((s32[4,16,1,2]{1,3,2,0:T(2,128)}), s32[4,16,1,2]{1,3,2,0:T(2,128)S(1)}, u32[]{:S(2)}, u32[]{:S(2)}) %all-to-all-start.2) | async-done | bytes 544 | tf_op jit(solution)/shard_map/all_to_all | solution.py:36
  111.6 5.0 %gather_fusion.2 = bf16[64,128,128]{2,1,0:T(8,128)(2,1)S(1)} fusion(bf16[256,128,128]{2,1,0:T(8,128)(2,1)} %bitcast.88, s32[1024]{0:T(1024)S(1)} %pad_clamp_fusion), kind=kCustom, calls=%fused_computation.2 | custom fusion | bytes 4194560 | tf_op jit(solution)/shard_map/jit(_take)/gather | solution.py:145
  116.6 1.6 broadcast_select_fusion.left_ref
  118.2 68.2 %all-gather.7.cloned.1.call-done = bf16[64,1,2,128,128]{4,3,2,1,0:T(8,128)(2,1)} async-done(((bf16[16,1,2,128,128]{4,3,2,1,0:T(8,128)(2,1)}), bf16[64,1,2,128,128]{4,3,2,1,0:T(8,128)(2,1)}) %all-gather.7.cloned.1.call-update) | async-done | bytes 4194320 | tf_op jit(solution)/shard_map/all_gather | solution.py:133
  186.4 5.8 %shard_map.46 = f32[32,128,128]{2,1,0:T(8,128)} custom-call(s32[64]{0:T(128)} %multiply_add_fusion.right_index, s32[64]{0:T(128)} %reshape.959.found, bf16[64,128,128]{2,1,0:T(8,128)(2,1)} %broadcast_select_fusion.left_ref, bf16[128,128,128]{2,1,0:T(8,128)(2,1)} %bitcast.84), custom_call_target="tpu_custom_call" | custom-call | flops 268435456 | bytes 6291456 | tf_op jit(solution)/shard_map/pallas_call | solution.py:59
  192.2 45.0 %reduce-scatter.2.cloned.1.call-done = f32[512,128]{1,0:T(8,128)} async-done(((f32[4096,128]{1,0:T(8,128)}), f32[512,128]{1,0:T(8,128)}) %reduce-scatter.2.cloned.1.call-update) | async-done | bytes 262160 | tf_op jit(solution)/shard_map/reduce_scatter | solution.py:164
  237.2 1.7 log-plus-one_convert_fusion
  (64 shorter events, 6.4 us)
Async XLA Ops:
  6.5 105.1 %all-gather.5.cloned.1.call-start = ((), (), s32[]{:S(2)}) async-start(), calls=%async_computation.7 | async-start | bytes 8912896 | tf_op jit(solution)/shard_map/all_gather | solution.py:107
  9.3 30.1 %copy-start = (bf16[1,1,16,128,128]{4,3,2,1,0:T(8,128)(2,1)S(1)}, bf16[1,1,16,128,128]{4,3,2,1,0:T(8,128)(2,1)}, u32[]{:S(2)}) copy-start(bf16[1,1,16,128,128]{4,3,2,1,0:T(8,128)(2,1)} %param.4) | copy-start | bytes 1572868
  39.1 147.3 %all-gather.7.cloned.1.call-start = ((), (), s32[]{:S(2)}) async-start(), calls=%async_computation.8 | async-start | bytes 5242880 | tf_op jit(solution)/shard_map/all_gather | solution.py:133
  39.4 33.5 %copy-start.1 = (s32[1,1,32,2]{2,3,1,0:T(2,128)S(1)}, s32[1,1,32,2]{2,3,1,0:T(2,128)}, u32[]{:S(2)}) copy-start(s32[1,1,32,2]{2,3,1,0:T(2,128)} %param.7) | copy-start | bytes 772
  68.8 10.8 %all-to-all-start = ((s32[8,1,2]{2,1,0:T(1,128)}), s32[8,1,2]{2,1,0:T(1,128)S(1)}, u32[]{:S(2)}, u32[]{:S(2)}) async-start(s32[8,1,2]{2,1,0:T(1,128)} %bitcast.6), calls=%async_computation | async-start | bytes 8192 | tf_op jit(solution)/shard_map/all_to_all | solution.py:105
  81.6 11.4 %all-to-all-start.1 = ((s32[16,1,18]{2,1,0:T(1,128)}), s32[16,1,18]{2,1,0:T(1,128)S(1)}, u32[]{:S(2)}, u32[]{:S(2)}) async-start(s32[16,1,18]{2,1,0:T(1,128)} %bitcast.9), calls=%async_computation.1 | async-start | bytes 16384 | tf_op jit(solution)/shard_map/all_to_all | solution.py:129
  94.9 14.3 %all-to-all-start.2 = ((s32[4,16,1,2]{1,3,2,0:T(2,128)}), s32[4,16,1,2]{1,3,2,0:T(2,128)S(1)}, u32[]{:S(2)}, u32[]{:S(2)}) async-start(s32[4,16,1,2]{1,3,2,0:T(2,128)} %broadcast_in_dim.100), calls=%async_computation.2 | async-start | bytes 8192 | tf_op jit(solution)/shard_map/all_to_all | solution.py:36
  101.5 135.7 %reduce-scatter.2.cloned.1.call-start = ((), (), s32[]{:S(2)}) async-start(), calls=%async_computation.6 | async-start | bytes 2359296 | tf_op jit(solution)/shard_map/reduce_scatter | solution.py:164
Sparse Core Ops, SparseCore 0:
  39.2 61.8 all-gather.4
  103.2 83.1 all-gather.6
  192.3 44.8 reduce-scatter.1

commit v18 on v14

--- a/solution.py
+++ b/solution.py
@@ -10,24 +10,29 @@
 
 def pack_slots(values, col_ids, targets, is_live, part_count, capacity):
     row_count = col_ids.shape[0]
+    slot_count = col_ids.shape[1]
     block_size = values.shape[-1]
     chosen = (
         targets[:, :, None] == jnp.arange(part_count, dtype=jnp.int32)[None, None, :]
     ) & is_live[:, :, None]
     running = jnp.cumsum(chosen.astype(jnp.int32), axis=1) - 1
-    order_in = jnp.sum(jnp.where(chosen, running, 0), axis=2)
-    row_ids = jnp.arange(row_count, dtype=jnp.int32)[:, None]
-    total = part_count * row_count * capacity
-    position = (targets * row_count + row_ids) * capacity + order_in
-    position = jnp.where(is_live, position, total).reshape(-1)
-    packed = jnp.zeros((total, block_size, block_size), values.dtype)
-    packed = packed.at[position].set(values.reshape(-1, block_size, block_size), mode="drop")
-    packed_cols = (
-        jnp.full((total,), -1, jnp.int32).at[position].set(col_ids.reshape(-1), mode="drop")
+    picks = jnp.arange(capacity, dtype=jnp.int32)
+    hit = jnp.transpose(chosen, (0, 2, 1))[:, :, None, :] & (
+        jnp.transpose(running, (0, 2, 1))[:, :, None, :] == picks[None, None, :, None]
     )
+    slot_ids = jnp.arange(slot_count, dtype=jnp.int32)
+    source = jnp.sum(jnp.where(hit, slot_ids, 0), axis=3)
+    filled = jnp.any(hit, axis=3)
+    row_ids = jnp.arange(row_count, dtype=jnp.int32)[:, None, None]
+    flat_source = (row_ids * slot_count + source).reshape(-1)
+    blocks = jnp.take(values.reshape(-1, block_size, block_size), flat_source, axis=0)
+    blocks = jnp.where(filled.reshape(-1)[:, None, None], blocks, jnp.zeros_like(blocks))
+    cols = jnp.where(filled.reshape(-1), jnp.take(col_ids.reshape(-1), flat_source), -1)
+    packed = blocks.reshape(row_count, part_count, capacity, block_size, block_size)
+    packed_cols = cols.reshape(row_count, part_count, capacity)
     return (
-        packed.reshape(part_count, row_count, capacity, block_size, block_size),
-        packed_cols.reshape(part_count, row_count, capacity),
+        jnp.transpose(packed, (1, 0, 2, 3, 4)),
+        jnp.transpose(packed_cols, (1, 0, 2)),
     )
 
 

time: 247 us -> 247 us (level)
    scatter x4 -> x0, local copies, waits for them, and re-layouts: 4.72 us -> none  [the longest x2 3.22 us: pack_slots(): packed.at[position]]
    gather x0 -> x8, local copies, waits for them, and re-layouts: none -> 3.09 us  [the longest x6 1.69 us: pack_slots(): jnp.take(col_ids.reshape(-1), flat_source)]
where the time goes in v18:
time: 247 us; the launch traced here: 246 us
  waiting for transfers between devices  130 us (53%)
  blocking collectives  56.1 us (23%)
  starting transfers between devices  17.4 us (7%)
  local copies, waits for them, and re-layouts  15.1 us (6%)
  between operations  14.1 us (6%)
  other arithmetic  7.34 us (3%)
  Pallas kernels  5.94 us (2%)
    all_gather x1, waiting for transfers between devices, body(): lax.all_gather(right_vals[None], 'row', axis=0, tiled=True)  66.4 us
    reduce_scatter x1, waiting for transfers between devices, body(): lax.psum_scatter(partial_sum[None, None], 'depth', scatter_dimension=2, t...  45.5 us
    all_to_all x1, blocking collectives, body(): lax.all_to_all(right_vals, 'col', split_axis=0, concat_axis=0, tiled=True)  28.4 us
    all_to_all x1, blocking collectives, body(): lax.all_to_all(left_vals, 'depth', split_axis=0, concat_axis=0, tiled=True)  27.7 us
    all_to_all x1, starting transfers between devices, body(): lax.all_to_all(id_pack, 'col', split_axis=0, concat_axis=0, tiled=True)  7.39 us
    all_to_all x1, waiting for transfers between devices, gather_by_exchange(): return lax.all_to_all(copies, axis, split_axis=0, concat_axis=0, tiled=True)  7.25 us
    all_to_all x1, waiting for transfers between devices, body(): lax.all_to_all(left_cols, 'depth', split_axis=0, concat_axis=0, tiled=True)  6.67 us
    all_to_all x1, starting transfers between devices, gather_by_exchange(): return lax.all_to_all(copies, axis, split_axis=0, concat_axis=0, tiled=True)  6.65 us
  transfers between devices with their start and end apart: 6, of which 5 were waited for; matrix products, arithmetic and copies ran while one was open for 7% of the time, Pallas kernels for 0%

profile of v18, /device:TPU:6, one launch (start us, length us, event | category | flops | bytes accessed | tf_op | source)
XLA Modules:
  0.0 245.8 jit_solution(5313909969325964064)
XLA Ops:
  6.5 0.7 and_select_fusion.7
  8.8 0.6 gather_fusion.4
  9.7 27.7 %all_to_all.32 = bf16[8,1,2,128,128]{4,3,2,1,0:T(8,128)(2,1)} all-to-all(bf16[8,1,2,128,128]{4,3,2,1,0:T(8,128)(2,1)S(1)} %select_select_fusion.1), channel_id=1, replica_groups=mesh['row'=4,'col'=16,'depth'=8] {'depth'}, dimensions={0} | all-to-all | bytes 1048576 | tf_op jit(solution)/shard_map/all_to_all | solution.py:109
  38.0 0.7 gather_fusion.6
  38.8 0.7 gather_fusion.1
  40.2 28.4 %all_to_all.33 = bf16[16,1,2,128,128]{4,3,2,1,0:T(8,128)(2,1)} all-to-all(bf16[16,1,2,128,128]{4,3,2,1,0:T(8,128)(2,1)S(1)} %select_select_fusion), channel_id=1, replica_groups=mesh['row'=4,'col'=16,'depth'=8] {'col'}, dimensions={0} | all-to-all | bytes 2097152 | tf_op jit(solution)/shard_map/all_to_all | solution.py:125
  68.6 0.7 gather_fusion
  69.5 0.7 copy.62
  70.1 3.3 %all-to-all-start = ((s32[8,1,2]{2,1,0:T(1,128)}), s32[8,1,2]{2,1,0:T(1,128)S(1)}, u32[]{:S(2)}, u32[]{:S(2)}) async-start(s32[8,1,2]{2,1,0:T(1,128)} %copy.62), calls=%async_computation | async-start | bytes 8192 | tf_op jit(solution)/shard_map/all_to_all | solution.py:110
  74.3 6.7 %all-to-all-done = s32[8,1,2]{2,1,0:T(1,128)S(1)} async-done(((s32[8,1,2]{2,1,0:T(1,128)}), s32[8,1,2]{2,1,0:T(1,128)S(1)}, u32[]{:S(2)}, u32[]{:S(2)}) %all-to-all-start) | async-done | bytes 96 | tf_op jit(solution)/shard_map/all_to_all | solution.py:110
  81.5 0.7 reduce.7
  82.3 0.7 pad_add_fusion
  82.9 7.4 %all-to-all-start.1 = ((s32[16,1,18]{2,1,0:T(1,128)}), s32[16,1,18]{2,1,0:T(1,128)S(1)}, u32[]{:S(2)}, u32[]{:S(2)}) async-start(s32[16,1,18]{2,1,0:T(1,128)} %bitcast.15), calls=%async_computation.1 | async-start | bytes 16384 | tf_op jit(solution)/shard_map/all_to_all | solution.py:134
  90.5 3.9 %all-to-all-done.1 = s32[16,1,18]{2,1,0:T(1,128)S(1)} async-done(((s32[16,1,18]{2,1,0:T(1,128)}), s32[16,1,18]{2,1,0:T(1,128)S(1)}, u32[]{:S(2)}, u32[]{:S(2)}) %all-to-all-start.1) | async-done | bytes 1184 | tf_op jit(solution)/shard_map/all_to_all | solution.py:134
  94.5 0.8 gather_fusion.2
  96.3 6.7 %all-to-all-start.2 = ((s32[4,16,1,2]{1,3,2,0:T(2,128)}), s32[4,16,1,2]{1,3,2,0:T(2,128)S(1)}, u32[]{:S(2)}, u32[]{:S(2)}) async-start(s32[4,16,1,2]{1,3,2,0:T(2,128)} %broadcast_in_dim.166), calls=%async_computation.2 | async-start | bytes 8192 | tf_op jit(solution)/shard_map/all_to_all | solution.py:41
  103.4 7.2 %all-to-all-done.2 = s32[4,16,1,2]{1,3,2,0:T(2,128)S(1)} async-done(((s32[4,16,1,2]{1,3,2,0:T(2,128)}), s32[4,16,1,2]{1,3,2,0:T(2,128)S(1)}, u32[]{:S(2)}, u32[]{:S(2)}) %all-to-all-start.2) | async-done | bytes 544 | tf_op jit(solution)/shard_map/all_to_all | solution.py:41
  111.9 0.6 reshape.881.found
  113.1 4.9 %gather_fusion.5 = bf16[64,128,128]{2,1,0:T(8,128)(2,1)S(1)} fusion(bf16[256,128,128]{2,1,0:T(8,128)(2,1)} %bitcast.75, s32[1024]{0:T(1024)S(1)} %pad_clamp_fusion), kind=kCustom, calls=%fused_computation.5 | custom fusion | bytes 4194560 | tf_op jit(solution)/shard_map/jit(_take)/gather | solution.py:150
  118.0 1.6 broadcast_select_fusion.left_ref
  119.6 66.4 %all-gather.7.cloned.1.call-done = bf16[64,1,2,128,128]{4,3,2,1,0:T(8,128)(2,1)} async-done(((bf16[16,1,2,128,128]{4,3,2,1,0:T(8,128)(2,1)}), bf16[64,1,2,128,128]{4,3,2,1,0:T(8,128)(2,1)}) %all-gather.7.cloned.1.call-update) | async-done | bytes 4194320 | tf_op jit(solution)/shard_map/all_gather | solution.py:138
  186.0 5.9 %shard_map.46 = f32[32,128,128]{2,1,0:T(8,128)} custom-call(s32[64]{0:T(128)} %multiply_add_fusion.right_index, s32[64]{0:T(128)} %reshape.881.found, bf16[64,128,128]{2,1,0:T(8,128)(2,1)} %broadcast_select_fusion.left_ref, bf16[128,128,128]{2,1,0:T(8,128)(2,1)} %bitcast.72), custom_call_target="tpu_custom_call" | custom-call | flops 268435456 | bytes 6291456 | tf_op jit(solution)/shard_map/pallas_call | solution.py:64
  192.0 45.5 %reduce-scatter.2.cloned.1.call-done = f32[1,1,4,128,128]{4,3,2,1,0:T(8,128)} async-done(((f32[1,1,32,128,128]{4,3,2,1,0:T(8,128)}), f32[1,1,4,128,128]{4,3,2,1,0:T(8,128)}) %reduce-scatter.2.cloned.1.call-update) | async-done | bytes 262160 | tf_op jit(solution)/shard_map/reduce_scatter | solution.py:169
  237.5 1.7 log-plus-one_convert_fusion
  (92 shorter events, 7.4 us)
Async XLA Ops:
  6.5 2.3 copy-start
  6.5 106.5 %all-gather.5.cloned.1.call-start = ((), (), s32[]{:S(2)}) async-start(), calls=%async_computation.7 | async-start | bytes 8912896 | tf_op jit(solution)/shard_map/all_gather | solution.py:112
  9.6 29.2 %copy-start.1 = (s32[1,1,16]{2,1,0:T(1,128)S(1)}, s32[1,1,16]{2,1,0:T(1,128)}, u32[]{:S(2)}) copy-start(s32[1,1,16]{2,1,0:T(1,128)} %param.5) | copy-start | bytes 196
  37.4 148.6 %all-gather.7.cloned.1.call-start = ((), (), s32[]{:S(2)}) async-start(), calls=%async_computation.8 | async-start | bytes 5242880 | tf_op jit(solution)/shard_map/all_gather | solution.py:138
  40.2 33.2 %copy-start.2 = (s32[1,1,32,2]{2,3,1,0:T(2,128)S(1)}, s32[1,1,32,2]{2,3,1,0:T(2,128)}, u32[]{:S(2)}) copy-start(s32[1,1,32,2]{2,3,1,0:T(2,128)} %param.7) | copy-start | bytes 772
  70.1 10.8 %all-to-all-start = ((s32[8,1,2]{2,1,0:T(1,128)}), s32[8,1,2]{2,1,0:T(1,128)S(1)}, u32[]{:S(2)}, u32[]{:S(2)}) async-start(s32[8,1,2]{2,1,0:T(1,128)} %copy.62), calls=%async_computation | async-start | bytes 8192 | tf_op jit(solution)/shard_map/all_to_all | solution.py:110
  82.9 11.4 %all-to-all-start.1 = ((s32[16,1,18]{2,1,0:T(1,128)}), s32[16,1,18]{2,1,0:T(1,128)S(1)}, u32[]{:S(2)}, u32[]{:S(2)}) async-start(s32[16,1,18]{2,1,0:T(1,128)} %bitcast.15), calls=%async_computation.1 | async-start | bytes 16384 | tf_op jit(solution)/shard_map/all_to_all | solution.py:134
  96.3 14.4 %all-to-all-start.2 = ((s32[4,16,1,2]{1,3,2,0:T(2,128)}), s32[4,16,1,2]{1,3,2,0:T(2,128)S(1)}, u32[]{:S(2)}, u32[]{:S(2)}) async-start(s32[4,16,1,2]{1,3,2,0:T(2,128)} %broadcast_in_dim.166), calls=%async_computation.2 | async-start | bytes 8192 | tf_op jit(solution)/shard_map/all_to_all | solution.py:41
  103.0 134.6 %reduce-scatter.2.cloned.1.call-start = ((), (), s32[]{:S(2)}) async-start(), calls=%async_computation.6 | async-start | bytes 2359296 | tf_op jit(solution)/shard_map/reduce_scatter | solution.py:169
Sparse Core Ops, SparseCore 0:
  37.5 63.2 all-gather.4
  102.9 83.0 all-gather.6
  192.1 45.3 reduce-scatter.1

commit v19 on v16

--- a/solution.py
+++ b/solution.py
@@ -10,24 +10,29 @@
 
 def pack_slots(values, col_ids, targets, is_live, part_count, capacity):
     row_count = col_ids.shape[0]
+    slot_count = col_ids.shape[1]
     block_size = values.shape[-1]
     chosen = (
         targets[:, :, None] == jnp.arange(part_count, dtype=jnp.int32)[None, None, :]
     ) & is_live[:, :, None]
     running = jnp.cumsum(chosen.astype(jnp.int32), axis=1) - 1
-    order_in = jnp.sum(jnp.where(chosen, running, 0), axis=2)
-    row_ids = jnp.arange(row_count, dtype=jnp.int32)[:, None]
-    total = part_count * row_count * capacity
-    position = (targets * row_count + row_ids) * capacity + order_in
-    position = jnp.where(is_live, position, total).reshape(-1)
-    packed = jnp.zeros((total, block_size, block_size), values.dtype)
-    packed = packed.at[position].set(values.reshape(-1, block_size, block_size), mode="drop")
-    packed_cols = (
-        jnp.full((total,), -1, jnp.int32).at[position].set(col_ids.reshape(-1), mode="drop")
+    picks = jnp.arange(capacity, dtype=jnp.int32)
+    hit = jnp.transpose(chosen, (0, 2, 1))[:, :, None, :] & (
+        jnp.transpose(running, (0, 2, 1))[:, :, None, :] == picks[None, None, :, None]
     )
+    slot_ids = jnp.arange(slot_count, dtype=jnp.int32)
+    source = jnp.sum(jnp.where(hit, slot_ids, 0), axis=3)
+    filled = jnp.any(hit, axis=3)
+    row_ids = jnp.arange(row_count, dtype=jnp.int32)[:, None, None]
+    flat_source = (row_ids * slot_count + source).reshape(-1)
+    blocks = jnp.take(values.reshape(-1, block_size, block_size), flat_source, axis=0)
+    blocks = jnp.where(filled.reshape(-1)[:, None, None], blocks, jnp.zeros_like(blocks))
+    cols = jnp.where(filled.reshape(-1), jnp.take(col_ids.reshape(-1), flat_source), -1)
+    packed = blocks.reshape(row_count, part_count, capacity, block_size, block_size)
+    packed_cols = cols.reshape(row_count, part_count, capacity)
     return (
-        packed.reshape(part_count, row_count, capacity, block_size, block_size),
-        packed_cols.reshape(part_count, row_count, capacity),
+        jnp.transpose(packed, (1, 0, 2, 3, 4)),
+        jnp.transpose(packed_cols, (1, 0, 2)),
     )
 
 

time: 247 us -> 246 us (level)
    scatter x4 -> x0, local copies, waits for them, and re-layouts: 4.72 us -> none  [the longest x2 3.22 us: pack_slots(): packed.at[position]]
    gather x0 -> x8, local copies, waits for them, and re-layouts: none -> 3.09 us  [the longest x6 1.69 us: pack_slots(): jnp.take(col_ids.reshape(-1), flat_source)]
where the time goes in v19:
time: 246 us
  waiting for transfers between devices  130 us (53%)
  blocking collectives  56.1 us (23%)
  starting transfers between devices  17.4 us (7%)
  local copies, waits for them, and re-layouts  14.5 us (6%)
  between operations  14 us (6%)
  other arithmetic  7.69 us (3%)
  Pallas kernels  6 us (2%)
    all_gather x1, waiting for transfers between devices, body(): lax.all_gather(right_vals[None], 'row', axis=0, tiled=True)  66.8 us
    reduce_scatter x1, waiting for transfers between devices, body(): lax.psum_scatter(partial_sum[None, None], 'depth', scatter_dimension=2, t...  45.4 us
    all_to_all x1, blocking collectives, body(): lax.all_to_all(right_vals, 'col', split_axis=0, concat_axis=0, tiled=True)  28.4 us
    all_to_all x1, blocking collectives, body(): lax.all_to_all(left_vals, 'depth', split_axis=0, concat_axis=0, tiled=True)  27.7 us
    all_to_all x1, starting transfers between devices, body(): lax.all_to_all(id_pack, 'col', split_axis=0, concat_axis=0, tiled=True)  7.39 us
    all_to_all x1, waiting for transfers between devices, gather_by_exchange(): return lax.all_to_all(copies, axis, split_axis=0, concat_axis=0, tiled=True)  7.15 us
    all_to_all x1, waiting for transfers between devices, body(): lax.all_to_all(left_cols, 'depth', split_axis=0, concat_axis=0, tiled=True)  6.98 us
    all_to_all x1, starting transfers between devices, gather_by_exchange(): return lax.all_to_all(copies, axis, split_axis=0, concat_axis=0, tiled=True)  6.65 us
  transfers between devices with their start and end apart: 6, of which 5 were waited for; matrix products, arithmetic and copies ran while one was open for 7% of the time, Pallas kernels for 0%

profile of v19, /device:TPU:6, one launch (start us, length us, event | category | flops | bytes accessed | tf_op | source)
XLA Modules:
  0.0 245.8 jit_solution(13095419854746061358)
XLA Ops:
  6.5 0.7 and_select_fusion.6
  8.8 0.6 gather_fusion.4
  9.7 27.7 %all_to_all.32 = bf16[8,1,2,128,128]{4,3,2,1,0:T(8,128)(2,1)} all-to-all(bf16[8,1,2,128,128]{4,3,2,1,0:T(8,128)(2,1)S(1)} %select_select_fusion.1), channel_id=1, replica_groups=mesh['row'=4,'col'=16,'depth'=8] {'depth'}, dimensions={0} | all-to-all | bytes 1048576 | tf_op jit(solution)/shard_map/all_to_all | solution.py:109
  38.0 0.7 gather_fusion.6
  38.8 0.7 gather_fusion.1
  40.2 28.4 %all_to_all.33 = bf16[16,1,2,128,128]{4,3,2,1,0:T(8,128)(2,1)} all-to-all(bf16[16,1,2,128,128]{4,3,2,1,0:T(8,128)(2,1)S(1)} %select_select_fusion), channel_id=1, replica_groups=mesh['row'=4,'col'=16,'depth'=8] {'col'}, dimensions={0} | all-to-all | bytes 2097152 | tf_op jit(solution)/shard_map/all_to_all | solution.py:125
  68.6 0.7 gather_fusion
  69.5 0.7 copy.65
  70.1 3.3 %all-to-all-start = ((s32[8,1,2]{2,1,0:T(1,128)}), s32[8,1,2]{2,1,0:T(1,128)S(1)}, u32[]{:S(2)}, u32[]{:S(2)}) async-start(s32[8,1,2]{2,1,0:T(1,128)} %copy.65), calls=%async_computation | async-start | bytes 8192 | tf_op jit(solution)/shard_map/all_to_all | solution.py:110
  74.0 7.0 %all-to-all-done = s32[8,1,2]{2,1,0:T(1,128)S(1)} async-done(((s32[8,1,2]{2,1,0:T(1,128)}), s32[8,1,2]{2,1,0:T(1,128)S(1)}, u32[]{:S(2)}, u32[]{:S(2)}) %all-to-all-start) | async-done | bytes 96 | tf_op jit(solution)/shard_map/all_to_all | solution.py:110
  81.5 0.7 reduce.7
  82.3 0.7 pad_add_fusion
  82.9 7.4 %all-to-all-start.1 = ((s32[16,1,18]{2,1,0:T(1,128)}), s32[16,1,18]{2,1,0:T(1,128)S(1)}, u32[]{:S(2)}, u32[]{:S(2)}) async-start(s32[16,1,18]{2,1,0:T(1,128)} %bitcast.15), calls=%async_computation.1 | async-start | bytes 16384 | tf_op jit(solution)/shard_map/all_to_all | solution.py:134
  90.6 3.8 %all-to-all-done.1 = s32[16,1,18]{2,1,0:T(1,128)S(1)} async-done(((s32[16,1,18]{2,1,0:T(1,128)}), s32[16,1,18]{2,1,0:T(1,128)S(1)}, u32[]{:S(2)}, u32[]{:S(2)}) %all-to-all-start.1) | async-done | bytes 1184 | tf_op jit(solution)/shard_map/all_to_all | solution.py:134
  94.5 0.8 gather_fusion.2
  95.7 0.6 broadcast_in_dim.177
  96.3 6.7 %all-to-all-start.2 = ((s32[4,16,1,2]{1,3,2,0:T(2,128)}), s32[4,16,1,2]{1,3,2,0:T(2,128)S(1)}, u32[]{:S(2)}, u32[]{:S(2)}) async-start(s32[4,16,1,2]{1,3,2,0:T(2,128)} %broadcast_in_dim.177), calls=%async_computation.2 | async-start | bytes 8192 | tf_op jit(solution)/shard_map/all_to_all | solution.py:41
  103.5 7.2 %all-to-all-done.2 = s32[4,16,1,2]{1,3,2,0:T(2,128)S(1)} async-done(((s32[4,16,1,2]{1,3,2,0:T(2,128)}), s32[4,16,1,2]{1,3,2,0:T(2,128)S(1)}, u32[]{:S(2)}, u32[]{:S(2)}) %all-to-all-start.2) | async-done | bytes 544 | tf_op jit(solution)/shard_map/all_to_all | solution.py:41
  112.4 5.0 %gather_fusion.5 = bf16[64,128,128]{2,1,0:T(8,128)(2,1)S(1)} fusion(bf16[256,128,128]{2,1,0:T(8,128)(2,1)} %bitcast.83, s32[1024]{0:T(1024)S(1)} %pad_clamp_fusion), kind=kCustom, calls=%fused_computation.5 | custom fusion | bytes 4194560 | tf_op jit(solution)/shard_map/jit(_take)/gather | solution.py:150
  117.4 2.0 copy_bitcast_fusion.left_ref
  119.4 66.8 %all-gather.7.cloned.1.call-done = bf16[64,1,2,128,128]{4,3,2,1,0:T(8,128)(2,1)} async-done(((bf16[16,1,2,128,128]{4,3,2,1,0:T(8,128)(2,1)}), bf16[64,1,2,128,128]{4,3,2,1,0:T(8,128)(2,1)}) %all-gather.7.cloned.1.call-update) | async-done | bytes 4194320 | tf_op jit(solution)/shard_map/all_gather | solution.py:138
  186.2 6.0 %shard_map.46 = f32[32,128,128]{2,1,0:T(8,128)} custom-call(s32[64]{0:T(128)} %multiply_add_fusion.right_index, bf16[32,128,256]{2,1,0:T(8,128)(2,1)} %copy_bitcast_fusion.left_ref, bf16[128,128,128]{2,1,0:T(8,128)(2,1)} %bitcast.80), custom_call_target="tpu_custom_call" | custom-call | flops 268435456 | bytes 6291456 | tf_op jit(solution)/shard_map/pallas_call | solution.py:65
  192.2 45.4 %reduce-scatter.2.cloned.1.call-done = f32[1,1,4,128,128]{4,3,2,1,0:T(8,128)} async-done(((f32[1,1,32,128,128]{4,3,2,1,0:T(8,128)}), f32[1,1,4,128,128]{4,3,2,1,0:T(8,128)}) %reduce-scatter.2.cloned.1.call-update) | async-done | bytes 262160 | tf_op jit(solution)/shard_map/reduce_scatter | solution.py:170
  237.6 1.7 log-plus-one_convert_fusion
  (87 shorter events, 6.7 us)
Async XLA Ops:
  6.5 2.3 copy-start
  6.5 105.9 %all-gather.5.cloned.1.call-start = ((), (), s32[]{:S(2)}) async-start(), calls=%async_computation.7 | async-start | bytes 8912896 | tf_op jit(solution)/shard_map/all_gather | solution.py:112
  9.6 29.2 %copy-start.1 = (s32[1,1,16]{2,1,0:T(1,128)S(1)}, s32[1,1,16]{2,1,0:T(1,128)}, u32[]{:S(2)}) copy-start(s32[1,1,16]{2,1,0:T(1,128)} %param.5) | copy-start | bytes 196
  37.4 148.8 %all-gather.7.cloned.1.call-start = ((), (), s32[]{:S(2)}) async-start(), calls=%async_computation.8 | async-start | bytes 5242880 | tf_op jit(solution)/shard_map/all_gather | solution.py:138
  40.2 33.2 %copy-start.2 = (s32[1,1,32,2]{2,3,1,0:T(2,128)S(1)}, s32[1,1,32,2]{2,3,1,0:T(2,128)}, u32[]{:S(2)}) copy-start(s32[1,1,32,2]{2,3,1,0:T(2,128)} %param.7) | copy-start | bytes 772
  70.1 10.8 %all-to-all-start = ((s32[8,1,2]{2,1,0:T(1,128)}), s32[8,1,2]{2,1,0:T(1,128)S(1)}, u32[]{:S(2)}, u32[]{:S(2)}) async-start(s32[8,1,2]{2,1,0:T(1,128)} %copy.65), calls=%async_computation | async-start | bytes 8192 | tf_op jit(solution)/shard_map/all_to_all | solution.py:110
  82.9 11.4 %all-to-all-start.1 = ((s32[16,1,18]{2,1,0:T(1,128)}), s32[16,1,18]{2,1,0:T(1,128)S(1)}, u32[]{:S(2)}, u32[]{:S(2)}) async-start(s32[16,1,18]{2,1,0:T(1,128)} %bitcast.15), calls=%async_computation.1 | async-start | bytes 16384 | tf_op jit(solution)/shard_map/all_to_all | solution.py:134
  96.3 14.4 %all-to-all-start.2 = ((s32[4,16,1,2]{1,3,2,0:T(2,128)}), s32[4,16,1,2]{1,3,2,0:T(2,128)S(1)}, u32[]{:S(2)}, u32[]{:S(2)}) async-start(s32[4,16,1,2]{1,3,2,0:T(2,128)} %broadcast_in_dim.177), calls=%async_computation.2 | async-start | bytes 8192 | tf_op jit(solution)/shard_map/all_to_all | solution.py:41
  103.0 134.6 %reduce-scatter.2.cloned.1.call-start = ((), (), s32[]{:S(2)}) async-start(), calls=%async_computation.6 | async-start | bytes 2359296 | tf_op jit(solution)/shard_map/reduce_scatter | solution.py:170
Sparse Core Ops, SparseCore 0:
  37.5 63.2 all-gather.4
  102.9 83.2 all-gather.6
  192.4 45.1 reduce-scatter.1

commit v20 on v14

--- a/solution.py
+++ b/solution.py
@@ -114,6 +114,7 @@
     ).reshape(-1)
     left_flat = left_vals.reshape(-1, block_size, block_size)
     left_ids = left_cols.reshape(-1)
+    values, left_vals = lax.optimization_barrier((values, left_vals))
     right_vals, right_cols = pack_slots(
         values, col_ids, col_ids // col_block, is_live, columns, cap_right
     )

time: 247 us -> 263 us (1.065)
  waiting for transfers between devices: 131 us -> 152 us
  blocking collectives: 54.5 us -> 47.4 us
    all_gather x1, waiting for transfers between devices: 0.01 us -> 53.6 us  [body(): left_vals = lax.all_gather(left_vals[None], 'col', axis=0, tiled=True)]
    all_gather x1, waiting for transfers between devices: 68.2 us -> 36.8 us  [body(): lax.all_gather(right_vals[None], 'row', axis=0, tiled=True)]
    all_to_all x1, blocking collectives: 26.8 us -> 19.7 us  [body(): lax.all_to_all(right_vals, 'col', split_axis=0, concat_axis=0, tiled=True)]
    all_to_all x1, starting transfers between devices: 3.31 us -> 7.38 us  [body(): lax.all_to_all(left_cols, 'depth', split_axis=0, concat_axis=0, tiled=True)]
  transfers between devices with their start and end apart: 6 -> 6, of which waited for: 5 -> 6; matrix products, arithmetic and copies ran while one was open for 7% -> 6% of each run, Pallas kernels for 0% -> 0%
where the time goes in v20:
time: 263 us; the launch traced here: 262 us
  waiting for transfers between devices  152 us (58%)
  blocking collectives  47.4 us (18%)
  starting transfers between devices  19.4 us (7%)
  local copies, waits for them, and re-layouts  15.5 us (6%)
  between operations  14 us (5%)
  other arithmetic  7.47 us (3%)
  Pallas kernels  5.88 us (2%)
    all_gather x1, waiting for transfers between devices, body(): left_vals = lax.all_gather(left_vals[None], 'col', axis=0, tiled=True)  53.6 us
    reduce_scatter x1, waiting for transfers between devices, body(): lax.psum_scatter(partial_sum[None, None], 'depth', scatter_dimension=2, t...  44.9 us
    all_gather x1, waiting for transfers between devices, body(): lax.all_gather(right_vals[None], 'row', axis=0, tiled=True)  36.8 us
    all_to_all x1, blocking collectives, body(): lax.all_to_all(left_vals, 'depth', split_axis=0, concat_axis=0, tiled=True)  27.7 us
    all_to_all x1, blocking collectives, body(): lax.all_to_all(right_vals, 'col', split_axis=0, concat_axis=0, tiled=True)  19.7 us
    all_to_all x1, starting transfers between devices, body(): lax.all_to_all(left_cols, 'depth', split_axis=0, concat_axis=0, tiled=True)  7.38 us
    all_to_all x1, waiting for transfers between devices, gather_by_exchange(): return lax.all_to_all(copies, axis, split_axis=0, concat_axis=0, tiled=True)  7.28 us
    all_to_all x1, starting transfers between devices, gather_by_exchange(): return lax.all_to_all(copies, axis, split_axis=0, concat_axis=0, tiled=True)  6.44 us
  transfers between devices with their start and end apart: 6, of which 6 were waited for; matrix products, arithmetic and copies ran while one was open for 6% of the time, Pallas kernels for 0%

profile of v20, /device:TPU:6, one launch (start us, length us, event | category | flops | bytes accessed | tf_op | source)
XLA Modules:
  0.0 262.2 jit_solution(15934734367937779747)
XLA Ops:
  7.2 0.7 and_select_fusion.7
  8.5 0.7 fusion.16
  9.3 2.1 scatter_fusion
  11.4 27.7 %all_to_all.32 = bf16[8,1,2,128,128]{4,3,2,1,0:T(8,128)(2,1)} all-to-all(bf16[8,1,2,128,128]{4,3,2,1,0:T(8,128)(2,1)S(1)} %bitcast.85), channel_id=1, replica_groups=mesh['row'=4,'col'=16,'depth'=8] {'depth'}, dimensions={0} | all-to-all | bytes 1048576 | tf_op jit(solution)/shard_map/all_to_all | solution.py:104
  39.1 53.6 %all-gather.5.cloned.1.call-done = bf16[128,1,2,128,128]{4,3,2,1,0:T(8,128)(2,1)} async-done(((bf16[8,1,2,128,128]{4,3,2,1,0:T(8,128)(2,1)}), bf16[128,1,2,128,128]{4,3,2,1,0:T(8,128)(2,1)}) %all-gather.5.cloned.1.call-update) | async-done | bytes 8388624 | tf_op jit(solution)/shard_map/all_gather | solution.py:107
  93.0 1.2 scatter_fusion.1
  94.2 19.7 %all_to_all.33 = bf16[16,1,2,128,128]{4,3,2,1,0:T(8,128)(2,1)} all-to-all(bf16[16,1,2,128,128]{4,3,2,1,0:T(8,128)(2,1)S(1)} %bitcast.84), channel_id=1, replica_groups=mesh['row'=4,'col'=16,'depth'=8] {'col'}, dimensions={0} | all-to-all | bytes 2097152 | tf_op jit(solution)/shard_map/all_to_all | solution.py:121
  113.9 0.8 scatter_custom_fusion
  114.7 0.7 reshape.936
  115.3 7.4 %all-to-all-start = ((s32[8,1,2]{2,1,0:T(1,128)}), s32[8,1,2]{2,1,0:T(1,128)S(1)}, u32[]{:S(2)}, u32[]{:S(2)}) async-start(s32[8,1,2]{2,1,0:T(1,128)} %bitcast.6), calls=%async_computation | async-start | bytes 8192 | tf_op jit(solution)/shard_map/all_to_all | solution.py:105
  122.7 0.8 scatter_custom_fusion.1
  124.3 6.0 %all-to-all-done = s32[8,1,2]{2,1,0:T(1,128)S(1)} async-done(((s32[8,1,2]{2,1,0:T(1,128)}), s32[8,1,2]{2,1,0:T(1,128)S(1)}, u32[]{:S(2)}, u32[]{:S(2)}) %all-to-all-start) | async-done | bytes 96 | tf_op jit(solution)/shard_map/all_to_all | solution.py:105
  131.6 0.7 pad_add_fusion
  132.3 5.6 %all-to-all-start.1 = ((s32[16,1,18]{2,1,0:T(1,128)}), s32[16,1,18]{2,1,0:T(1,128)S(1)}, u32[]{:S(2)}, u32[]{:S(2)}) async-start(s32[16,1,18]{2,1,0:T(1,128)} %bitcast.9), calls=%async_computation.1 | async-start | bytes 16384 | tf_op jit(solution)/shard_map/all_to_all | solution.py:130
  137.9 3.9 %all-to-all-done.1 = s32[16,1,18]{2,1,0:T(1,128)S(1)} async-done(((s32[16,1,18]{2,1,0:T(1,128)}), s32[16,1,18]{2,1,0:T(1,128)S(1)}, u32[]{:S(2)}, u32[]{:S(2)}) %all-to-all-start.1) | async-done | bytes 1184 | tf_op jit(solution)/shard_map/all_to_all | solution.py:130
  142.0 0.8 gather_fusion
  143.7 6.4 %all-to-all-start.2 = ((s32[4,16,1,2]{1,3,2,0:T(2,128)}), s32[4,16,1,2]{1,3,2,0:T(2,128)S(1)}, u32[]{:S(2)}, u32[]{:S(2)}) async-start(s32[4,16,1,2]{1,3,2,0:T(2,128)} %broadcast_in_dim.103), calls=%async_computation.2 | async-start | bytes 8192 | tf_op jit(solution)/shard_map/all_to_all | solution.py:36
  150.7 7.3 %all-to-all-done.2 = s32[4,16,1,2]{1,3,2,0:T(2,128)S(1)} async-done(((s32[4,16,1,2]{1,3,2,0:T(2,128)}), s32[4,16,1,2]{1,3,2,0:T(2,128)S(1)}, u32[]{:S(2)}, u32[]{:S(2)}) %all-to-all-start.2) | async-done | bytes 544 | tf_op jit(solution)/shard_map/all_to_all | solution.py:36
  160.4 4.4 %gather_fusion.2 = bf16[64,128,128]{2,1,0:T(8,128)(2,1)S(1)} fusion(bf16[256,128,128]{2,1,0:T(8,128)(2,1)} %bitcast.90, s32[1024]{0:T(1024)S(1)} %pad_clamp_fusion), kind=kCustom, calls=%fused_computation.2 | custom fusion | bytes 4194560 | tf_op jit(solution)/shard_map/jit(_take)/gather | solution.py:146
  164.8 1.6 broadcast_select_fusion.left_ref
  166.4 36.8 %all-gather.7.cloned.1.call-done = bf16[64,1,2,128,128]{4,3,2,1,0:T(8,128)(2,1)} async-done(((bf16[16,1,2,128,128]{4,3,2,1,0:T(8,128)(2,1)}), bf16[64,1,2,128,128]{4,3,2,1,0:T(8,128)(2,1)}) %all-gather.7.cloned.1.call-update) | async-done | bytes 4194320 | tf_op jit(solution)/shard_map/all_gather | solution.py:134
  203.2 5.9 %shard_map.46 = f32[32,128,128]{2,1,0:T(8,128)} custom-call(s32[64]{0:T(128)} %multiply_add_fusion.right_index, s32[64]{0:T(128)} %reshape.944.found, bf16[64,128,128]{2,1,0:T(8,128)(2,1)} %broadcast_select_fusion.left_ref, bf16[128,128,128]{2,1,0:T(8,128)(2,1)} %bitcast.86), custom_call_target="tpu_custom_call" | custom-call | flops 268435456 | bytes 6291456 | tf_op jit(solution)/shard_map/pallas_call | solution.py:59
  209.1 44.9 %reduce-scatter.2.cloned.1.call-done = f32[1,1,4,128,128]{4,3,2,1,0:T(8,128)} async-done(((f32[1,1,32,128,128]{4,3,2,1,0:T(8,128)}), f32[1,1,4,128,128]{4,3,2,1,0:T(8,128)}) %reduce-scatter.2.cloned.1.call-update) | async-done | bytes 262160 | tf_op jit(solution)/shard_map/reduce_scatter | solution.py:165
  254.0 1.7 log-plus-one_convert_fusion
  (64 shorter events, 7.1 us)
Async XLA Ops:
  6.5 86.2 %all-gather.5.cloned.1.call-start = ((), (), s32[]{:S(2)}) async-start(), calls=%async_computation.7 | async-start | bytes 8912896 | tf_op jit(solution)/shard_map/all_gather | solution.py:107
  9.3 83.7 %copy-start = (bf16[1,1,16,128,128]{4,3,2,1,0:T(8,128)(2,1)S(1)}, bf16[1,1,16,128,128]{4,3,2,1,0:T(8,128)(2,1)}, u32[]{:S(2)}) copy-start(bf16[1,1,16,128,128]{4,3,2,1,0:T(8,128)(2,1)} %param.4) | copy-start | bytes 1572868
  39.1 164.1 %all-gather.7.cloned.1.call-start = ((), (), s32[]{:S(2)}) async-start(), calls=%async_computation.8 | async-start | bytes 5242880 | tf_op jit(solution)/shard_map/all_gather | solution.py:134
  93.0 30.5 %copy-start.1 = (s32[1,1,32,2]{2,3,1,0:T(2,128)S(1)}, s32[1,1,32,2]{2,3,1,0:T(2,128)}, u32[]{:S(2)}) copy-start(s32[1,1,32,2]{2,3,1,0:T(2,128)} %param.7) | copy-start | bytes 772
  115.3 15.0 %all-to-all-start = ((s32[8,1,2]{2,1,0:T(1,128)}), s32[8,1,2]{2,1,0:T(1,128)S(1)}, u32[]{:S(2)}, u32[]{:S(2)}) async-start(s32[8,1,2]{2,1,0:T(1,128)} %bitcast.6), calls=%async_computation | async-start | bytes 8192 | tf_op jit(solution)/shard_map/all_to_all | solution.py:105
  132.3 9.6 %all-to-all-start.1 = ((s32[16,1,18]{2,1,0:T(1,128)}), s32[16,1,18]{2,1,0:T(1,128)S(1)}, u32[]{:S(2)}, u32[]{:S(2)}) async-start(s32[16,1,18]{2,1,0:T(1,128)} %bitcast.9), calls=%async_computation.1 | async-start | bytes 16384 | tf_op jit(solution)/shard_map/all_to_all | solution.py:130
  143.7 14.3 %all-to-all-start.2 = ((s32[4,16,1,2]{1,3,2,0:T(2,128)}), s32[4,16,1,2]{1,3,2,0:T(2,128)S(1)}, u32[]{:S(2)}, u32[]{:S(2)}) async-start(s32[4,16,1,2]{1,3,2,0:T(2,128)} %broadcast_in_dim.103), calls=%async_computation.2 | async-start | bytes 8192 | tf_op jit(solution)/shard_map/all_to_all | solution.py:36
  150.2 103.8 %reduce-scatter.2.cloned.1.call-start = ((), (), s32[]{:S(2)}) async-start(), calls=%async_computation.6 | async-start | bytes 2359296 | tf_op jit(solution)/shard_map/reduce_scatter | solution.py:165
Sparse Core Ops, SparseCore 0:
  39.2 53.4 all-gather.4
  114.0 89.0 all-gather.6
  209.2 44.7 reduce-scatter.1
